TPU v7x, 256 devices: a whole 4x4x8 slice. The times are simulated.
256 devices in a mesh: sensor: 8 (over z_lo, core), tm: 32 (over x, y, z_hi).
Axes of the slice: x: 4, y: 4, z: 8 (z_hi: 2, z_lo: 4; z = z_hi * 4 + z_lo), core: 2. Of those that a mesh axis runs over, the one named last changes fastest.
Arguments:
- readings: float32 [4096, 128], P(('sensor', 'tm')), may hold values from -18 to 18
- noise_var: float32 [4096, 128], P(('sensor', 'tm')), may hold values from 0.1 to 1
- sensor_weights: float32 [4096, 64, 128], P(('sensor', 'tm')), may hold values from -0.1 to 1, as said below
- time_weights: float32 [4096, 128, 128], P(('sensor', 'tm')), may hold values from -0.1 to 1, as said below
- window_index: int32 [4096], P(('sensor', 'tm')), may hold values from 0 to 7
- sensor_kernel: float32 [4096, 4096], P('sensor'), may hold values from -1 to 1.5, as said below
- time_kernel: float32 [4096, 4096], P('tm'), may hold values from -1 to 1.5, as said below
Outputs:
- solution: float32 [4096, 128], P(('sensor', 'tm'))
- residual: float32 [4096, 128], P(('sensor', 'tm'))
Inputs may be any that keep to these rules, and one draw needn't show every extreme that they name: Block b's readings interpolate from sensor rows 64 * window_index[b] to 64 * window_index[b] + 63 of the sensor rows that its device holds. `sensor_weights`: each reading's column holds the four cubic convolution weights of one position, in rows p - 1 to p + 2 for some p with 1 <= p <= 61; the other entries are zero. `time_weights`: each reading's column holds the four cubic convolution weights of one position, in rows p - 1 to p + 2 for some p with 1 <= p <= 125; the other entries are zero. `sensor_kernel`: symmetric and positive definite. `time_kernel`: symmetric and positive definite.
All inputs are finite; a program needn't handle non-finite values.
Results may differ from a plain program's by a relative error of at most 0.0003.
Values sent between devices are 32-bit elements; how exact they have to be, the bound alone decides.
No kernel may reach another device: no remote copies, remote signals or barrier semaphores. Data moves between devices by JAX's collectives and lax.ppermute only.
A program may use at most 64 MiB of HBM per device.

v0:
```python
import jax
import jax.numpy as jnp
from jax import lax
from jax.sharding import PartitionSpec as P

ITERS = 2


PRECISE = lax.Precision.HIGHEST


def on_device(
    readings, noise_var, sensor_weights, time_weights, window_index, sensor_kernel, time_kernel
):
    sensor_dev = sensor_kernel.shape[0]
    time_dev = time_kernel.shape[0]
    win_rows = sensor_weights.shape[1]
    win_count = sensor_dev // win_rows
    window_ids = jnp.arange(win_count, dtype=jnp.int32)
    onehot = (window_index[:, None] == window_ids[None, :]).astype(jnp.float32)
    own_square = lax.dynamic_slice_in_dim(
        sensor_kernel, lax.axis_index("sensor") * sensor_dev, sensor_dev, 1
    )
    own_square = own_square.reshape(win_count, win_rows, win_count, win_rows)
    window_kernel = own_square[window_ids, :, window_ids, :]
    block_kernel = jnp.einsum("bw,wik->bik", onehot, window_kernel, precision=PRECISE)
    sensor_quad = jnp.sum(
        sensor_weights
        * jnp.einsum("bik,bkr->bir", block_kernel, sensor_weights, precision=PRECISE),
        axis=1,
    )
    time_square = lax.dynamic_slice_in_dim(
        time_kernel, lax.axis_index("tm") * time_dev, time_dev, 1
    )
    time_quad = jnp.sum(
        time_weights * jnp.einsum("jl,blr->bjr", time_square, time_weights, precision=PRECISE),
        axis=1,
    )
    inverse = 1.0 / (sensor_quad * time_quad + noise_var)

    def residual_inner(residual, precond):
        return lax.psum(jnp.sum(residual * precond), ("sensor", "tm"))

    residual = readings
    solution = jnp.zeros_like(readings)
    precond = inverse * residual
    direction = precond
    inner_now = residual_inner(residual, precond)
    for iteration in range(ITERS):
        scaled = direction[:, None, :] * time_weights
        contrib = jnp.einsum("bir,bjr->bij", sensor_weights, scaled, precision=PRECISE)
        grid_field = jnp.einsum("bw,bij->wij", onehot, contrib, precision=PRECISE).reshape(
            sensor_dev, time_dev
        )
        left_product = jnp.dot(
            sensor_kernel,
            lax.all_gather(grid_field, "sensor", axis=0, tiled=True),
            precision=PRECISE,
            preferred_element_type=jnp.float32,
        )
        smooth = lax.dot_general(
            lax.all_gather(left_product, "tm", axis=1, tiled=True),
            time_kernel,
            (((1,), (1,)), ((), ())),
            precision=PRECISE,
            preferred_element_type=jnp.float32,
        )
        gathered = jnp.einsum(
            "bw,wij->bij", onehot, smooth.reshape(win_count, win_rows, time_dev), precision=PRECISE
        )
        interp_cols = jnp.einsum("bij,bjr->bir", gathered, time_weights, precision=PRECISE)
        image_vec = jnp.sum(sensor_weights * interp_cols, axis=1) + noise_var * direction
        step_size = inner_now / lax.psum(jnp.sum(direction * image_vec), ("sensor", "tm"))
        solution = solution + step_size * direction
        residual = residual - step_size * image_vec
        if iteration + 1 < ITERS:
            precond = inverse * residual
            inner_next = residual_inner(residual, precond)
            direction = precond + inner_next / inner_now * direction
            inner_now = inner_next
    return (solution, residual)


def solution(mesh):
    in_specs = (
        P(("sensor", "tm"), None),
        P(("sensor", "tm"), None),
        P(("sensor", "tm"), None, None),
        P(("sensor", "tm"), None, None),
        P(("sensor", "tm")),
        P("sensor", None),
        P("tm", None),
    )
    out_specs = (P(("sensor", "tm"), None), P(("sensor", "tm"), None))
    return jax.shard_map(
        on_device, mesh=mesh, in_specs=in_specs, out_specs=out_specs, check_vma=False
    )
```

profile of v0, /device:TPU:1, one launch (start us, length us, event | category | flops | bytes accessed | tf_op | source)
XLA Modules:
  0.0 706.3 jit_solution(7459923984500713900)
XLA Ops:
  7.2 0.0 copy-start
  7.2 0.0 all-gather.5.cloned.1.call-start
  7.2 1.4 constant_dynamic-slice_fusion
  8.7 1.8 reshape.22
  10.5 0.0 copy-start.7
  10.5 3.3 copy.11
  13.7 0.0 copy-start.1
  13.7 0.0 copy-start.5
  13.7 0.0 copy-start.6
  13.7 2.2 gather_fusion
  16.0 0.0 copy-done.7
  16.0 0.0 copy-start.2
  16.0 0.5 fusion.20
  16.5 2.1 fusion.4
  18.6 0.0 copy-done
  18.6 0.0 copy-done.1
  18.6 1.0 fusion.1
  19.7 0.0 copy-done.5
  19.7 0.0 copy-done.6
  19.7 0.0 copy-done.2
  19.7 2.1 convolution_bitcast_fusion.2
  21.8 0.6 fusion.11
  22.4 0.8 copy.15
  23.2 0.0 all-gather.5.cloned.1.call-update
  23.2 0.3 all-gather.7.cloned.1.call-start
  23.5 40.7 %all-gather.5.cloned.1.call-done = f32[4096,128]{1,0:T(8,128)} async-done(((f32[512,128]{1,0:T(8,128)}), f32[4096,128]{1,0:T(8,128)}) %all-gather.5.cloned.1.call-update) | async-done | bytes 2097168 | tf_op jit(solution)/shard_map/all_gather | solution.py:57
  64.3 13.5 %convolution_bitcast_fusion.4 = f32[512,128]{0,1:T(8,128)} fusion(f32[4096,128]{1,0:T(8,128)} %all-gather.5.cloned.1.call-done, f32[512,4096]{1,0:T(8,128)} %param.12), kind=kOutput, calls=%fused_computation.13 | convolution fusion | flops 3221225472 | bytes 10747904 | tf_op jit(solution)/shard_map/dot_general | solution.py:55
  77.8 0.0 all-gather.7.cloned.1.call-update
  77.8 0.6 all-gather.9.cloned.1.call-start
  78.4 147.9 %all-gather.7.cloned.1.call-done = f32[512,4096]{0,1:T(8,128)} async-done(((f32[512,128]{0,1:T(8,128)}), f32[512,4096]{0,1:T(8,128)}) %all-gather.7.cloned.1.call-update) | async-done | bytes 8388624 | tf_op jit(solution)/shard_map/all_gather | solution.py:62
  226.3 0.0 copy-start.3
  226.3 15.6 %fusion.38 = f32[512,128]{1,0:T(8,128)S(1)} fusion(f32[512,4096]{0,1:T(8,128)} %all-gather.7.cloned.1.call-done, f32[128,4096]{1,0:T(8,128)S(1)} %copy-done), kind=kOutput, calls=%fused_computation.56 | convolution fusion | flops 3221225472 | bytes 10747904 | tf_op jit(solution)/shard_map/dot_general | solution.py:61
  241.9 0.5 fusion.18
  242.4 0.0 copy-done.3
  242.4 1.2 fusion.2
  243.6 0.6 multiply_reduce_fusion.2
  244.2 79.9 %all-reduce = (f32[]{:T(128)}, f32[]{:T(128)}) all-reduce(f32[]{:T(128)} %get-tuple-element.3, f32[]{:T(128)} %get-tuple-element.2), channel_id=1, replica_groups=mesh['sensor'=8,'tm'=32] {'sensor','tm'}, use_global_device_ids=true, to_apply=%region_3.0 | all-reduce | flops 2 | bytes 16 | tf_op jit(solution)/shard_map/psum | solution.py:42
  325.4 0.6 multiply_reduce_fusion.1
  326.0 72.6 %psum.30 = f32[]{:T(128)} all-reduce(f32[]{:T(128)} %multiply_reduce_fusion.1), channel_id=1, replica_groups=mesh['sensor'=8,'tm'=32] {'sensor','tm'}, use_global_device_ids=true, to_apply=%region_8.0 | all-reduce | flops 1 | bytes 8 | tf_op jit(solution)/shard_map/psum | solution.py:42
  400.0 3.1 convolution_bitcast_fusion.1
  403.1 0.6 fusion.8
  403.7 0.8 copy.19
  404.5 0.0 all-gather.9.cloned.1.call-update
  404.5 0.2 all-gather.11.cloned.1.call-start
  404.7 33.0 %all-gather.9.cloned.1.call-done = f32[4096,128]{1,0:T(8,128)} async-done(((f32[512,128]{1,0:T(8,128)}), f32[4096,128]{1,0:T(8,128)}) %all-gather.9.cloned.1.call-update) | async-done | bytes 2097168 | tf_op jit(solution)/shard_map/all_gather | solution.py:57
  437.7 13.5 %convolution_bitcast_fusion.3 = f32[512,128]{0,1:T(8,128)} fusion(f32[4096,128]{1,0:T(8,128)} %all-gather.9.cloned.1.call-done, f32[512,4096]{1,0:T(8,128)} %param.12), kind=kOutput, calls=%fused_computation.12 | convolution fusion | flops 3221225472 | bytes 10747904 | tf_op jit(solution)/shard_map/dot_general | solution.py:55
  451.3 0.0 all-gather.11.cloned.1.call-update
  451.3 148.5 %all-gather.11.cloned.1.call-done = f32[512,4096]{0,1:T(8,128)} async-done(((f32[512,128]{0,1:T(8,128)}), f32[512,4096]{0,1:T(8,128)}) %all-gather.11.cloned.1.call-update) | async-done | bytes 8388624 | tf_op jit(solution)/shard_map/all_gather | solution.py:62
  599.8 0.0 copy-start.4
  599.8 15.7 %fusion.39 = f32[512,128]{1,0:T(8,128)S(1)} fusion(f32[512,4096]{0,1:T(8,128)} %all-gather.11.cloned.1.call-done, f32[128,4096]{1,0:T(8,128)S(1)} %copy-done), kind=kOutput, calls=%fused_computation.57 | convolution fusion | flops 3221225472 | bytes 10747904 | tf_op jit(solution)/shard_map/dot_general | solution.py:61
  615.5 0.5 fusion.16
  616.0 0.0 copy-done.4
  616.0 1.2 fusion.3
  617.2 0.6 multiply_reduce_fusion
  617.8 79.8 %psum.31 = f32[]{:T(128)} all-reduce(f32[]{:T(128)} %multiply_reduce_fusion), channel_id=1, replica_groups=mesh['sensor'=8,'tm'=32] {'sensor','tm'}, use_global_device_ids=true, to_apply=%region_11.0 | all-reduce | flops 1 | bytes 8 | tf_op jit(solution)/shard_map/psum | solution.py:73
  698.9 0.6 multiply_subtract_fusion
  (3 shorter events, 0.0 us)
Async XLA Ops:
  7.2 11.4 %copy-start = (f32[128,4096]{1,0:T(8,128)S(1)}, f32[128,4096]{1,0:T(8,128)}, u32[]{:S(2)}) copy-start(f32[128,4096]{1,0:T(8,128)} %param.13) | copy-start | bytes 6291460
  7.2 57.1 %all-gather.5.cloned.1.call-start = ((), (), s32[]{:S(2)}) async-start(), calls=%async_computation | async-start | bytes 2359296 | tf_op jit(solution)/shard_map/all_gather | solution.py:57
  10.5 5.5 copy-start.7
  13.7 4.9 copy-start.1
  13.7 5.9 copy-start.5
  13.7 5.9 copy-start.6
  16.0 3.7 copy-start.2
  23.2 203.1 %all-gather.7.cloned.1.call-start = ((), (), s32[]{:S(2)}) async-start(), calls=%async_computation.1 | async-start | bytes 8650752 | tf_op jit(solution)/shard_map/all_gather | solution.py:62
  77.8 359.9 %all-gather.9.cloned.1.call-start = ((), (), s32[]{:S(2)}) async-start(), calls=%async_computation.2 | async-start | bytes 2359296 | tf_op jit(solution)/shard_map/all_gather | solution.py:57
  226.3 16.1 %copy-start.3 = (f32[16,64,128]{2,1,0:T(8,128)S(1)}, f32[16,64,128]{2,1,0:T(8,128)}, u32[]{:S(2)}) copy-start(f32[16,64,128]{2,1,0:T(8,128)} %param.9) | copy-start | bytes 1572868
  404.5 195.3 %all-gather.11.cloned.1.call-start = ((), (), s32[]{:S(2)}) async-start(), calls=%async_computation.3 | async-start | bytes 8650752 | tf_op jit(solution)/shard_map/all_gather | solution.py:62
  599.8 16.2 %copy-start.4 = (f32[16,64,128]{2,1,0:T(8,128)S(1)}, f32[16,64,128]{2,1,0:T(8,128)}, u32[]{:S(2)}) copy-start(f32[16,64,128]{2,1,0:T(8,128)} %param.9) | copy-start | bytes 1572868
Sparse Core Ops, SparseCore 0:
  23.3 40.9 all-gather.4
  77.9 148.3 all-gather.6
  404.6 33.0 all-gather.8
  451.4 148.3 all-gather.10
where the time goes:
time: 711 us; the launch traced here: 706 us
  waiting for transfers between devices  370 us (52%)
  blocking collectives  232 us (33%)
  matrix products  71.6 us (10%)
  between operations  18.2 us (3%)
  local copies, waits for them, and re-layouts  10.3 us (1%)
    all_gather x2, waiting for transfers between devices, on_device(): lax.all_gather(left_product, 'tm', axis=1, tiled=True)  296 us
    psum x2, blocking collectives, residual_inner(): return lax.psum(jnp.sum(residual * precond), ('sensor', 'tm'))  152 us
    psum x1, blocking collectives, on_device(): lax.psum(jnp.sum(direction * image_vec), ('sensor', 'tm'))  79.8 us
    all_gather x2, waiting for transfers between devices, on_device(): lax.all_gather(grid_field, 'sensor', axis=0, tiled=True)  73.7 us
    dot_general x2, matrix products, on_device(): lax.dot_general(lax.all_gather(left_product, 'tm', axis=1, tiled=True), t...  31.3 us
    dot_general x2, matrix products, on_device(): jnp.dot(sensor_kernel, lax.all_gather(grid_field, 'sensor', axis=0, tiled...  27 us
  transfers between devices with their start and end apart: 4, of which 4 were waited for; matrix products, arithmetic and copies ran while one was open for 0% of the time, Pallas kernels for 0%

commit v1 on v0

v1 whole, which is shorter than its diff:
```python
import jax
import jax.numpy as jnp
from jax import lax
from jax.sharding import PartitionSpec as P

PRECISE = lax.Precision.HIGHEST
PAY_ROWS = 8


def on_device(
    readings, noise_var, sensor_weights, time_weights, window_index, sensor_kernel, time_kernel
):
    sensor_dev = sensor_kernel.shape[0]
    time_dev = time_kernel.shape[0]
    win_rows = sensor_weights.shape[1]
    win_count = sensor_dev // win_rows
    n_tm = time_kernel.shape[1] // time_dev
    window_ids = jnp.arange(win_count, dtype=jnp.int32)
    onehot = (window_index[:, None] == window_ids[None, :]).astype(jnp.float32)
    own_square = lax.dynamic_slice_in_dim(
        sensor_kernel, lax.axis_index("sensor") * sensor_dev, sensor_dev, 1
    )
    own_square = own_square.reshape(win_count, win_rows, win_count, win_rows)
    window_kernel = own_square[window_ids, :, window_ids, :]
    block_kernel = jnp.einsum("bw,wik->bik", onehot, window_kernel, precision=PRECISE)
    sensor_quad = jnp.sum(
        sensor_weights
        * jnp.einsum("bik,bkr->bir", block_kernel, sensor_weights, precision=PRECISE),
        axis=1,
    )
    time_square = lax.dynamic_slice_in_dim(
        time_kernel, lax.axis_index("tm") * time_dev, time_dev, 1
    )
    time_quad = jnp.sum(
        time_weights * jnp.einsum("jl,blr->bjr", time_square, time_weights, precision=PRECISE),
        axis=1,
    )
    inverse = 1.0 / (sensor_quad * time_quad + noise_var)

    def operator_apply(vector, payload=None):
        scaled = vector[:, None, :] * time_weights
        contrib = jnp.einsum("bir,bjr->bij", sensor_weights, scaled, precision=PRECISE)
        grid_field = jnp.einsum("bw,bij->wij", onehot, contrib, precision=PRECISE).reshape(
            sensor_dev, time_dev
        )
        if payload is None:
            full_field = lax.all_gather(grid_field, "sensor", axis=0, tiled=True)
        else:
            pad = jnp.zeros((PAY_ROWS, time_dev), jnp.float32)
            pad = pad.at[0, : payload.shape[0]].set(payload)
            both = lax.all_gather(
                jnp.concatenate([grid_field, pad], axis=0), "sensor", axis=0, tiled=False
            )
            full_field = both[:, :sensor_dev, :].reshape(-1, time_dev)
            sensor_sum = jnp.sum(both[:, sensor_dev:, :], axis=0)
        left_product = jnp.dot(
            sensor_kernel, full_field, precision=PRECISE, preferred_element_type=jnp.float32
        )
        if payload is not None:
            left_product = jnp.concatenate([left_product, sensor_sum], axis=0)
        gathered = lax.all_gather(left_product, "tm", axis=1, tiled=True)
        smooth = lax.dot_general(
            gathered[:sensor_dev],
            time_kernel,
            (((1,), (1,)), ((), ())),
            precision=PRECISE,
            preferred_element_type=jnp.float32,
        )
        field_rows = jnp.einsum(
            "bw,wij->bij", onehot, smooth.reshape(win_count, win_rows, time_dev), precision=PRECISE
        )
        interp_cols = jnp.einsum("bij,bjr->bir", field_rows, time_weights, precision=PRECISE)
        image = jnp.sum(sensor_weights * interp_cols, axis=1) + noise_var * vector
        if payload is None:
            return image, None
        totals = jnp.sum(
            gathered[sensor_dev:].reshape(PAY_ROWS, n_tm, time_dev), axis=1
        )[0, : payload.shape[0]]
        return image, totals

    residual0 = readings
    precond0 = inverse * residual0
    direction0 = precond0
    image0, _ = operator_apply(direction0)
    scaled_image0 = inverse * image0
    first_partials = jnp.stack(
        [jnp.sum(residual0 * precond0), jnp.sum(direction0 * image0)]
    )
    image_scaled, first_totals = operator_apply(scaled_image0, first_partials)
    inner0 = first_totals[0]
    step0 = inner0 / first_totals[1]
    solution = step0 * direction0
    residual1 = residual0 - step0 * image0
    precond1 = inverse * residual1
    image_precond1 = image0 - step0 * image_scaled
    second = lax.psum(
        jnp.stack(
            [
                jnp.sum(residual1 * precond1),
                jnp.sum(precond1 * image_precond1),
                jnp.sum(precond1 * image0 + direction0 * image_precond1),
            ]
        ),
        ("sensor", "tm"),
    )
    inner1 = second[0]
    ratio = inner1 / inner0
    direction1 = precond1 + ratio * direction0
    image1 = image_precond1 + ratio * image0
    curvature1 = second[1] + ratio * second[2] + ratio * ratio * first_totals[1]
    step1 = inner1 / curvature1
    solution = solution + step1 * direction1
    residual = residual1 - step1 * image1
    return (solution, residual)


def solution(mesh):
    in_specs = (
        P(("sensor", "tm"), None),
        P(("sensor", "tm"), None),
        P(("sensor", "tm"), None, None),
        P(("sensor", "tm"), None, None),
        P(("sensor", "tm")),
        P("sensor", None),
        P("tm", None),
    )
    out_specs = (P(("sensor", "tm"), None), P(("sensor", "tm"), None))
    return jax.shard_map(
        on_device, mesh=mesh, in_specs=in_specs, out_specs=out_specs, check_vma=False
    )
```

time: 711 us -> 597 us (0.84)
  blocking collectives: 232 us -> 74.4 us
  waiting for transfers between devices: 370 us -> 405 us
    psum x3 -> x1, blocking collectives: 232 us -> 74.4 us  [on_device(): lax.psum(jnp.stack([jnp.sum(residual1 * precond1), jnp.sum(precond1 * ima...]
    all_gather x4, waiting for transfers between devices: 370 us -> 405 us  [the longest x2 325 us: operator_apply(): gathered = lax.all_gather(left_product, 'tm', axis=1, tiled=True)]
where the time goes in v1:
time: 597 us; the launch traced here: 592 us
  waiting for transfers between devices  405 us (68%)
  blocking collectives  74.4 us (12%)
  matrix products  67.7 us (11%)
  between operations  19.4 us (3%)
  local copies, waits for them, and re-layouts  15.6 us (3%)
  other arithmetic  9.29 us (2%)
    all_gather x2, waiting for transfers between devices, operator_apply(): gathered = lax.all_gather(left_product, 'tm', axis=1, tiled=True)  325 us
    psum x1, blocking collectives, on_device(): lax.psum(jnp.stack([jnp.sum(residual1 * precond1), jnp.sum(precond1 * ima...  74.4 us
    all_gather x1, waiting for transfers between devices, operator_apply(): full_field = lax.all_gather(grid_field, 'sensor', axis=0, tiled=True)  40.5 us
    all_gather x1, waiting for transfers between devices, operator_apply(): lax.all_gather(jnp.concatenate([grid_field, pad], axis=0), 'sensor', axis...  38.8 us
    dot_general x2, matrix products, operator_apply(): lax.dot_general(gathered[:sensor_dev], time_kernel, (((1,), (1,)), ((), (...  31.4 us
    dot_general x2, matrix products, operator_apply(): jnp.dot(sensor_kernel, full_field, precision=PRECISE, preferred_element_t...  23 us
  transfers between devices with their start and end apart: 4, of which 4 were waited for; matrix products, arithmetic and copies ran while one was open for 0% of the time, Pallas kernels for 0%

profile of v1, /device:TPU:1, one launch (start us, length us, event | category | flops | bytes accessed | tf_op | source)
XLA Modules:
  0.0 592.1 jit_solution(16767710434967427257)
XLA Ops:
  7.2 0.0 copy-start
  7.2 0.0 all-gather.6.cloned.1.call-start
  7.2 1.4 constant_dynamic-slice_fusion
  8.7 1.8 reshape.62
  10.5 0.0 copy-start.6
  10.5 3.3 copy.22
  13.7 0.0 copy-start.1
  13.7 0.0 copy-start.4
  13.7 0.0 copy-start.5
  13.7 2.2 gather_fusion
  16.0 0.0 copy-done.6
  16.0 0.5 fusion.22
  16.5 2.0 fusion.6
  18.5 0.0 copy-done
  18.5 0.0 copy-done.1
  18.5 1.0 fusion.3
  19.6 0.0 copy-done.4
  19.6 0.0 copy-done.5
  19.6 3.1 convolution_bitcast_fusion.2
  22.7 0.6 fusion.13
  23.3 0.8 copy.26
  24.1 0.0 all-gather.6.cloned.1.call-update
  24.1 0.6 all-gather.8.cloned.1.call-start
  24.7 40.5 %all-gather.6.cloned.1.call-done = f32[4096,128]{1,0:T(8,128)} async-done(((f32[512,128]{1,0:T(8,128)}), f32[4096,128]{1,0:T(8,128)}) %all-gather.6.cloned.1.call-update) | async-done | bytes 2097168 | tf_op jit(solution)/shard_map/all_gather | solution.py:47
  65.2 13.5 %convolution_bitcast_fusion.4 = f32[512,128]{0,1:T(8,128)} fusion(f32[4096,128]{1,0:T(8,128)} %all-gather.6.cloned.1.call-done, f32[512,4096]{1,0:T(8,128)} %param.14), kind=kOutput, calls=%fused_computation.15 | convolution fusion | flops 3221225472 | bytes 10747904 | tf_op jit(solution)/shard_map/dot_general | solution.py:56
  78.7 0.0 all-gather.8.cloned.1.call-update
  78.8 0.2 all-gather.12.cloned.1.call-start
  79.0 148.3 %all-gather.8.cloned.1.call-done = f32[512,4096]{0,1:T(8,128)} async-done(((f32[512,128]{0,1:T(8,128)}), f32[512,4096]{0,1:T(8,128)}) %all-gather.8.cloned.1.call-update) | async-done | bytes 8388624 | tf_op jit(solution)/shard_map/all_gather | solution.py:61
  227.3 0.0 copy-start.2
  227.3 15.6 %fusion.44 = f32[512,128]{1,0:T(8,128)S(1)} fusion(f32[512,4096]{0,1:T(8,128)} %all-gather.8.cloned.1.call-done, f32[128,4096]{1,0:T(8,128)S(1)} %copy-done), kind=kOutput, calls=%fused_computation.67 | convolution fusion | flops 3221225472 | bytes 10747904 | tf_op jit(solution)/shard_map/dot_general | solution.py:62
  242.9 0.5 fusion.20
  243.3 0.0 copy-done.2
  243.3 1.2 fusion.4
  244.6 0.6 multiply_reduce_fusion.3
  245.2 2.1 convolution_bitcast_fusion.1
  247.2 0.6 fusion.10
  247.8 0.1 copy.30
  247.9 1.4 maximum_bitcast_fusion
  249.3 0.8 select_maximum_fusion
  250.0 0.0 all-gather.12.cloned.1.call-update
  250.0 0.3 all-gather.10.cloned.1.call-start
  250.3 38.8 %all-gather.12.cloned.1.call-done = f32[4160,128]{1,0:T(8,128)} async-done(((f32[520,128]{1,0:T(8,128)}), f32[4160,128]{1,0:T(8,128)}) %all-gather.12.cloned.1.call-update) | async-done | bytes 2129936 | tf_op jit(solution)/shard_map/all_gather | solution.py:51
  289.1 1.7 slice.60
  290.8 0.8 slice_reduce_fusion
  291.6 9.5 %convolution_bitcast_fusion.3 = f32[512,128]{0,1:T(8,128)S(1)} fusion(f32[4096,128]{1,0:T(8,128)S(1)} %bitcast.59, f32[512,4096]{1,0:T(8,128)} %param.14), kind=kOutput, calls=%fused_computation.14 | convolution fusion | flops 3221225472 | bytes 10747904 | tf_op jit(solution)/shard_map/dot_general | solution.py:56
  301.1 0.1 copy.31
  301.2 0.8 pad_maximum_fusion
  302.0 0.0 all-gather.10.cloned.1.call-update
  302.0 177.0 %all-gather.10.cloned.1.call-done = f32[520,4096]{0,1:T(8,128)} async-done(((f32[520,128]{0,1:T(8,128)}), f32[520,4096]{0,1:T(8,128)}) %all-gather.10.cloned.1.call-update) | async-done | bytes 8519696 | tf_op jit(solution)/shard_map/all_gather | solution.py:61
  479.0 3.0 slice.62
  482.0 1.8 reduce_sum.105
  483.8 0.5 fusion.42
  484.3 0.0 copy-start.3
  484.3 15.8 %fusion = f32[512,128]{1,0:T(8,128)S(1)} fusion(f32[128,4096]{1,0:T(8,128)S(1)} %copy-done, f32[520,4096]{0,1:T(8,128)} %all-gather.10.cloned.1.call-done), kind=kOutput, calls=%fused_computation.1 | convolution fusion | flops 3221225472 | bytes 10747904 | tf_op jit(solution)/shard_map/dot_general | solution.py:62
  500.1 0.5 fusion.18
  500.6 0.0 copy-done.3
  500.6 1.2 fusion.5
  503.1 0.7 multiply_reduce_fusion.1
  503.8 2.0 pad_maximum_fusion.1
  505.8 74.4 %psum.7 = f32[3]{0:T(128)S(1)} all-reduce(f32[3]{0:T(128)S(1)} %pad_maximum_fusion.1), channel_id=1, replica_groups=mesh['sensor'=8,'tm'=32] {'sensor','tm'}, use_global_device_ids=true, to_apply=%region_11.0 | all-reduce | flops 3 | bytes 24 | tf_op jit(solution)/shard_map/psum | solution.py:96
  580.2 0.7 fusion.43
  584.7 0.6 multiply_subtract_fusion
  (3 shorter events, 0.0 us)
Async XLA Ops:
  7.2 11.3 %copy-start = (f32[128,4096]{1,0:T(8,128)S(1)}, f32[128,4096]{1,0:T(8,128)}, u32[]{:S(2)}) copy-start(f32[128,4096]{1,0:T(8,128)} %param.15) | copy-start | bytes 6291460
  7.2 58.0 %all-gather.6.cloned.1.call-start = ((), (), s32[]{:S(2)}) async-start(), calls=%async_computation | async-start | bytes 2359296 | tf_op jit(solution)/shard_map/all_gather | solution.py:47
  10.5 5.5 copy-start.6
  13.7 4.8 copy-start.1
  13.7 5.8 copy-start.4
  13.7 5.8 copy-start.5
  24.1 203.1 %all-gather.8.cloned.1.call-start = ((), (), s32[]{:S(2)}) async-start(), calls=%async_computation.1 | async-start | bytes 8650752 | tf_op jit(solution)/shard_map/all_gather | solution.py:61
  78.8 210.3 %all-gather.12.cloned.1.call-start = ((), (), s32[]{:S(2)}) async-start(), calls=%async_computation.3 | async-start | bytes 2396160 | tf_op jit(solution)/shard_map/all_gather | solution.py:51
  227.3 16.1 %copy-start.2 = (f32[16,64,128]{2,1,0:T(8,128)S(1)}, f32[16,64,128]{2,1,0:T(8,128)}, u32[]{:S(2)}) copy-start(f32[16,64,128]{2,1,0:T(8,128)} %param.11) | copy-start | bytes 1572868
  250.0 228.9 %all-gather.10.cloned.1.call-start = ((), (), s32[]{:S(2)}) async-start(), calls=%async_computation.2 | async-start | bytes 10813440 | tf_op jit(solution)/shard_map/all_gather | solution.py:61
  484.3 16.3 %copy-start.3 = (f32[16,64,128]{2,1,0:T(8,128)S(1)}, f32[16,64,128]{2,1,0:T(8,128)}, u32[]{:S(2)}) copy-start(f32[16,64,128]{2,1,0:T(8,128)} %param.11) | copy-start | bytes 1572868
Sparse Core Ops, SparseCore 0:
  24.2 40.9 all-gather.5
  78.9 148.3 all-gather.7
  250.2 38.8 all-gather.11
  302.1 176.8 all-gather.9

commit v2 on v1

--- a/solution.py
+++ b/solution.py
@@ -1,10 +1,21 @@
 import jax
 import jax.numpy as jnp
 from jax import lax
-from jax.sharding import PartitionSpec as P
+import numpy as np
+from jax.sharding import Mesh, PartitionSpec as P
 
 PRECISE = lax.Precision.HIGHEST
 PAY_ROWS = 8
+TM = ("tx", "ty", "tz")
+ALL = ("sensor",) + TM
+
+
+def tm_index():
+    return (
+        lax.axis_index("tx") * (lax.axis_size("ty") * lax.axis_size("tz"))
+        + lax.axis_index("ty") * lax.axis_size("tz")
+        + lax.axis_index("tz")
+    )
 
 
 def on_device(
@@ -29,7 +40,7 @@
         axis=1,
     )
     time_square = lax.dynamic_slice_in_dim(
-        time_kernel, lax.axis_index("tm") * time_dev, time_dev, 1
+        time_kernel, tm_index() * time_dev, time_dev, 1
     )
     time_quad = jnp.sum(
         time_weights * jnp.einsum("jl,blr->bjr", time_square, time_weights, precision=PRECISE),
@@ -58,7 +69,8 @@
         )
         if payload is not None:
             left_product = jnp.concatenate([left_product, sensor_sum], axis=0)
-        gathered = lax.all_gather(left_product, "tm", axis=1, tiled=True)
+        gathered = lax.all_gather(left_product, "tz", axis=1, tiled=True)
+        gathered = lax.all_gather(gathered, ("tx", "ty"), axis=1, tiled=True)
         smooth = lax.dot_general(
             gathered[:sensor_dev],
             time_kernel,
@@ -101,7 +113,7 @@
                 jnp.sum(precond1 * image0 + direction0 * image_precond1),
             ]
         ),
-        ("sensor", "tm"),
+        ALL,
     )
     inner1 = second[0]
     ratio = inner1 / inner0
@@ -115,16 +127,19 @@
 
 
 def solution(mesh):
+    n_sensor, n_tm = mesh.devices.shape
+    devices = np.asarray(mesh.devices).reshape(n_sensor, n_tm // 8, 4, 2)
+    mesh = Mesh(devices, ("sensor",) + TM)
     in_specs = (
-        P(("sensor", "tm"), None),
-        P(("sensor", "tm"), None),
-        P(("sensor", "tm"), None, None),
-        P(("sensor", "tm"), None, None),
-        P(("sensor", "tm")),
+        P(ALL, None),
+        P(ALL, None),
+        P(ALL, None, None),
+        P(ALL, None, None),
+        P(ALL),
         P("sensor", None),
-        P("tm", None),
+        P(TM, None),
     )
-    out_specs = (P(("sensor", "tm"), None), P(("sensor", "tm"), None))
+    out_specs = (P(ALL, None), P(ALL, None))
     return jax.shard_map(
         on_device, mesh=mesh, in_specs=in_specs, out_specs=out_specs, check_vma=False
     )

time: 597 us -> 459 us (0.77)
  waiting for transfers between devices: 405 us -> 239 us
  blocking collectives: 74.4 us -> 114 us
    all_gather x2, waiting for transfers between devices: 325 us -> 160 us  [operator_apply(): gathered = lax.all_gather(gathered, ('tx', 'ty'), axis=1, tiled=True)]
    all_gather x0 -> x2, blocking collectives: none -> 37.7 us  [operator_apply(): gathered = lax.all_gather(left_product, 'tz', axis=1, tiled=True)]
where the time goes in v2:
time: 459 us
  waiting for transfers between devices  239 us (52%)
  blocking collectives  114 us (25%)
  matrix products  62.7 us (14%)
  between operations  19.2 us (4%)
  local copies, waits for them, and re-layouts  15.6 us (3%)
  other arithmetic  8.55 us (2%)
    all_gather x2, waiting for transfers between devices, operator_apply(): gathered = lax.all_gather(gathered, ('tx', 'ty'), axis=1, tiled=True)  160 us
    psum x1, blocking collectives, on_device(): lax.psum(jnp.stack([jnp.sum(residual1 * precond1), jnp.sum(precond1 * ima...  75.9 us
    all_gather x1, waiting for transfers between devices, operator_apply(): full_field = lax.all_gather(grid_field, 'sensor', axis=0, tiled=True)  41 us
    all_gather x2, blocking collectives, operator_apply(): gathered = lax.all_gather(left_product, 'tz', axis=1, tiled=True)  37.7 us
    all_gather x1, waiting for transfers between devices, operator_apply(): lax.all_gather(jnp.concatenate([grid_field, pad], axis=0), 'sensor', axis...  37.1 us
    dot_general x2, matrix products, operator_apply(): lax.dot_general(gathered[:sensor_dev], time_kernel, (((1,), (1,)), ((), (...  31.2 us
    dot_general x2, matrix products, operator_apply(): jnp.dot(sensor_kernel, full_field, precision=PRECISE, preferred_element_t...  19.4 us
  transfers between devices with their start and end apart: 4, of which 4 were waited for; matrix products, arithmetic and copies ran while one was open for 0% of the time, Pallas kernels for 0%

profile of v2, /device:TPU:1, one launch (start us, length us, event | category | flops | bytes accessed | tf_op | source)
XLA Modules:
  0.0 458.9 jit_solution(8615900791557293216)
XLA Ops:
  7.2 0.0 copy-start
  7.2 0.0 all-gather.6.cloned.1.call-start
  7.2 1.4 constant_dynamic-slice_fusion
  8.7 1.8 reshape.62
  10.5 0.0 copy-start.7
  10.5 3.3 copy.22
  13.7 0.0 copy-start.1
  13.7 0.0 copy-start.5
  13.7 0.0 copy-start.6
  13.7 2.2 gather_fusion
  16.0 0.0 copy-done.7
  16.0 0.0 copy-start.2
  16.0 0.5 fusion.22
  16.5 2.0 fusion.6
  18.5 0.0 copy-done
  18.5 0.0 copy-done.1
  18.5 1.0 fusion.3
  19.6 0.0 copy-done.5
  19.6 0.0 copy-done.6
  19.6 0.0 copy-done.2
  19.6 2.1 convolution_bitcast_fusion.2
  21.7 0.6 fusion.13
  22.3 0.8 copy.26
  23.1 0.0 all-gather.6.cloned.1.call-update
  23.1 0.0 all-gather.8.cloned.1.call-start
  23.1 41.0 %all-gather.6.cloned.1.call-done = f32[4096,128]{1,0:T(8,128)} async-done(((f32[512,128]{1,0:T(8,128)}), f32[4096,128]{1,0:T(8,128)}) %all-gather.6.cloned.1.call-update) | async-done | bytes 2097168 | tf_op jit(solution)/shard_map/all_gather | solution.py:58
  64.2 9.9 %convolution_bitcast_fusion.4 = f32[512,128]{0,1:T(8,128)S(1)} fusion(f32[4096,128]{1,0:T(8,128)} %all-gather.6.cloned.1.call-done, f32[512,4096]{1,0:T(8,128)} %param.14), kind=kOutput, calls=%fused_computation.15 | convolution fusion | flops 3221225472 | bytes 10747904 | tf_op jit(solution)/shard_map/dot_general | solution.py:67
  74.1 17.2 %all_gather.22 = f32[512,256]{0,1:T(8,128)} all-gather(f32[512,128]{0,1:T(8,128)S(1)} %convolution_bitcast_fusion.4), channel_id=1, replica_groups=mesh['sensor'=8,'tx'=4,'ty'=4,'tz'=2] {'tz'}, dimensions={1}, use_global_device_ids=true | all-gather | bytes 786432 | tf_op jit(solution)/shard_map/all_gather | solution.py:72
  91.3 0.0 all-gather.8.cloned.1.call-update
  91.3 0.2 all-gather.12.cloned.1.call-start
  91.5 75.6 %all-gather.8.cloned.1.call-done = f32[512,4096]{0,1:T(8,128)} async-done(((f32[512,256]{0,1:T(8,128)}), f32[512,4096]{0,1:T(8,128)}) %all-gather.8.cloned.1.call-update) | async-done | bytes 8388624 | tf_op jit(solution)/shard_map/all_gather | solution.py:73
  167.1 0.0 copy-start.3
  167.1 15.6 %fusion.44 = f32[512,128]{1,0:T(8,128)S(1)} fusion(f32[512,4096]{0,1:T(8,128)} %all-gather.8.cloned.1.call-done, f32[128,4096]{1,0:T(8,128)S(1)} %copy-done), kind=kOutput, calls=%fused_computation.67 | convolution fusion | flops 3221225472 | bytes 10747904 | tf_op jit(solution)/shard_map/dot_general | solution.py:74
  182.7 0.5 fusion.20
  183.2 0.0 copy-done.3
  183.2 1.2 fusion.4
  184.4 2.1 convolution_bitcast_fusion.1
  186.5 0.6 fusion.10
  187.1 0.1 copy.30
  187.1 0.6 multiply_reduce_fusion.3
  187.7 1.4 maximum_bitcast_fusion
  189.1 0.8 select_maximum_fusion
  189.8 0.0 all-gather.12.cloned.1.call-update
  189.9 0.3 all-gather.10.cloned.1.call-start
  190.1 37.1 %all-gather.12.cloned.1.call-done = f32[4160,128]{1,0:T(8,128)} async-done(((f32[520,128]{1,0:T(8,128)}), f32[4160,128]{1,0:T(8,128)}) %all-gather.12.cloned.1.call-update) | async-done | bytes 2129936 | tf_op jit(solution)/shard_map/all_gather | solution.py:62
  227.2 1.7 slice.60
  229.0 0.8 slice_reduce_fusion
  229.7 9.5 %convolution_bitcast_fusion.3 = f32[512,128]{0,1:T(8,128)S(1)} fusion(f32[4096,128]{1,0:T(8,128)S(1)} %bitcast.59, f32[512,4096]{1,0:T(8,128)} %param.14), kind=kOutput, calls=%fused_computation.14 | convolution fusion | flops 3221225472 | bytes 10747904 | tf_op jit(solution)/shard_map/dot_general | solution.py:67
  239.3 0.1 copy.31
  239.4 20.5 %all_gather.26 = f32[520,256]{0,1:T(8,128)} all-gather(f32[520,128]{0,1:T(8,128)S(1)} %pad_maximum_fusion), channel_id=1, replica_groups=mesh['sensor'=8,'tx'=4,'ty'=4,'tz'=2] {'tz'}, dimensions={1}, use_global_device_ids=true | all-gather | bytes 798720 | tf_op jit(solution)/shard_map/all_gather | solution.py:72
  259.9 0.0 all-gather.10.cloned.1.call-update
  259.9 84.8 %all-gather.10.cloned.1.call-done = f32[520,4096]{0,1:T(8,128)} async-done(((f32[520,256]{0,1:T(8,128)}), f32[520,4096]{0,1:T(8,128)}) %all-gather.10.cloned.1.call-update) | async-done | bytes 8519696 | tf_op jit(solution)/shard_map/all_gather | solution.py:73
  344.7 3.0 slice.62
  347.7 1.8 reduce_sum.105
  349.5 0.5 fusion.42
  350.0 15.6 %fusion = f32[512,128]{1,0:T(8,128)S(1)} fusion(f32[128,4096]{1,0:T(8,128)S(1)} %copy-done, f32[520,4096]{0,1:T(8,128)} %all-gather.10.cloned.1.call-done), kind=kOutput, calls=%fused_computation.1 | convolution fusion | flops 3221225472 | bytes 10747904 | tf_op jit(solution)/shard_map/dot_general | solution.py:74
  365.6 0.5 fusion.18
  366.1 0.0 copy-done.4
  366.1 1.2 fusion.5
  368.6 0.7 multiply_reduce_fusion.1
  369.3 2.0 pad_maximum_fusion.1
  371.3 75.9 %psum.7 = f32[3]{0:T(128)S(1)} all-reduce(f32[3]{0:T(128)S(1)} %pad_maximum_fusion.1), channel_id=1, replica_groups=mesh['sensor'=8,'tx'=4,'ty'=4,'tz'=2] {'sensor','tx','ty','tz'}, use_global_device_ids=true, to_apply=%region_11.0 | all-reduce | flops 3 | bytes 24 | tf_op jit(solution)/shard_map/psum | solution.py:108
  447.2 0.7 fusion.43
  451.7 0.6 multiply_subtract_fusion
  (5 shorter events, 0.1 us)
Async XLA Ops:
  7.2 11.3 %copy-start = (f32[128,4096]{1,0:T(8,128)S(1)}, f32[128,4096]{1,0:T(8,128)}, u32[]{:S(2)}) copy-start(f32[128,4096]{1,0:T(8,128)} %param.15) | copy-start | bytes 6291460
  7.2 57.0 %all-gather.6.cloned.1.call-start = ((), (), s32[]{:S(2)}) async-start(), calls=%async_computation | async-start | bytes 2359296 | tf_op jit(solution)/shard_map/all_gather | solution.py:58
  10.5 5.5 %copy-start.7 = (s32[16]{0:T(128)S(1)}, s32[16]{0:T(128)}, u32[]{:S(2)}) copy-start(s32[16]{0:T(128)} %param.13) | copy-start | bytes 196
  13.7 4.8 %copy-start.1 = (f32[16,128,128]{2,1,0:T(8,128)S(1)}, f32[16,128,128]{2,1,0:T(8,128)}, u32[]{:S(2)}) copy-start(f32[16,128,128]{2,1,0:T(8,128)} %param.12) | copy-start | bytes 3145732
  13.7 5.8 %copy-start.5 = (f32[16,128]{1,0:T(8,128)S(1)}, f32[16,128]{1,0:T(8,128)}, u32[]{:S(2)}) copy-start(f32[16,128]{1,0:T(8,128)} %param.9) | copy-start | bytes 24580
  13.7 5.9 %copy-start.6 = (f32[16,128]{1,0:T(8,128)S(1)}, f32[16,128]{1,0:T(8,128)}, u32[]{:S(2)}) copy-start(f32[16,128]{1,0:T(8,128)} %param.10) | copy-start | bytes 24580
  16.0 3.6 copy-start.2
  23.1 144.0 %all-gather.8.cloned.1.call-start = ((), (), s32[]{:S(2)}) async-start(), calls=%async_computation.1 | async-start | bytes 8912896 | tf_op jit(solution)/shard_map/all_gather | solution.py:73
  91.3 135.9 %all-gather.12.cloned.1.call-start = ((), (), s32[]{:S(2)}) async-start(), calls=%async_computation.3 | async-start | bytes 2396160 | tf_op jit(solution)/shard_map/all_gather | solution.py:62
  167.1 16.1 %copy-start.3 = (f32[16,64,128]{2,1,0:T(8,128)S(1)}, f32[16,64,128]{2,1,0:T(8,128)}, u32[]{:S(2)}) copy-start(f32[16,64,128]{2,1,0:T(8,128)} %param.11) | copy-start | bytes 1572868
  189.9 154.9 %all-gather.10.cloned.1.call-start = ((), (), s32[]{:S(2)}) async-start(), calls=%async_computation.2 | async-start | bytes 11141120 | tf_op jit(solution)/shard_map/all_gather | solution.py:73
  350.0 16.1 %copy-start.4 = (f32[16,64,128]{2,1,0:T(8,128)S(1)}, f32[16,64,128]{2,1,0:T(8,128)}, u32[]{:S(2)}) copy-start(f32[16,64,128]{2,1,0:T(8,128)} %param.11) | copy-start | bytes 1572868
Sparse Core Ops, SparseCore 0:
  23.2 40.9 all-gather.5
  91.4 75.6 all-gather.7
  190.0 37.1 all-gather.11
  260.1 84.6 all-gather.9

commit v3 on v2

--- a/solution.py
+++ b/solution.py
@@ -16,6 +16,16 @@
         + lax.axis_index("ty") * lax.axis_size("tz")
         + lax.axis_index("tz")
     )
+
+
+def butterfly_sum(value):
+    for axis in ALL:
+        size = lax.axis_size(axis)
+        stride = 1
+        while stride < size:
+            value = value + lax.ppermute(value, axis, [(i, i ^ stride) for i in range(size)])
+            stride *= 2
+    return value
 
 
 def on_device(
@@ -105,15 +115,14 @@
     residual1 = residual0 - step0 * image0
     precond1 = inverse * residual1
     image_precond1 = image0 - step0 * image_scaled
-    second = lax.psum(
+    second = butterfly_sum(
         jnp.stack(
             [
                 jnp.sum(residual1 * precond1),
                 jnp.sum(precond1 * image_precond1),
                 jnp.sum(precond1 * image0 + direction0 * image_precond1),
             ]
-        ),
-        ALL,
+        )
     )
     inner1 = second[0]
     ratio = inner1 / inner0

time: 459 us -> 432 us (0.941)
  the two profiles are of different devices: /device:TPU:1 before, /device:TPU:2 now
where the time goes in v3:
time: 432 us; the launch traced here: 430 us
  waiting for transfers between devices  259 us (60%)
  matrix products  62.7 us (15%)
  blocking collectives  45.8 us (11%)
  between operations  19.4 us (4%)
  local copies, waits for them, and re-layouts  15.6 us (4%)
  starting transfers between devices  14.9 us (3%)
  other arithmetic  12.4 us (3%)
    all_gather x2, waiting for transfers between devices, operator_apply(): gathered = lax.all_gather(gathered, ('tx', 'ty'), axis=1, tiled=True)  159 us
    all_gather x2, blocking collectives, operator_apply(): gathered = lax.all_gather(left_product, 'tz', axis=1, tiled=True)  45.8 us
    all_gather x1, waiting for transfers between devices, operator_apply(): full_field = lax.all_gather(grid_field, 'sensor', axis=0, tiled=True)  41.8 us
    all_gather x1, waiting for transfers between devices, operator_apply(): lax.all_gather(jnp.concatenate([grid_field, pad], axis=0), 'sensor', axis...  38.7 us
    dot_general x2, matrix products, operator_apply(): lax.dot_general(gathered[:sensor_dev], time_kernel, (((1,), (1,)), ((), (...  31.2 us
    ppermute x8, waiting for transfers between devices, butterfly_sum(): lax.ppermute(value, axis, [(i, i ^ stride) for i in range(size)])  19.5 us
    dot_general x2, matrix products, operator_apply(): jnp.dot(sensor_kernel, full_field, precision=PRECISE, preferred_element_t...  19.4 us
    ppermute x8, starting transfers between devices, butterfly_sum(): lax.ppermute(value, axis, [(i, i ^ stride) for i in range(size)])  14.5 us
  transfers between devices with their start and end apart: 12, of which 12 were waited for; matrix products, arithmetic and copies ran while one was open for 0% of the time, Pallas kernels for 0%

profile of v3, /device:TPU:2, one launch (start us, length us, event | category | flops | bytes accessed | tf_op | source)
XLA Modules:
  0.0 429.6 jit_solution(14464365540728397645)
XLA Ops:
  7.2 0.0 all-gather.6.cloned.1.call-start
  7.2 1.4 constant_dynamic-slice_fusion
  8.7 1.8 reshape.62
  10.4 3.3 copy.22
  13.7 2.2 gather_fusion
  16.0 0.5 fusion.22
  16.5 2.0 fusion.6
  18.5 1.1 fusion.3
  19.6 2.1 convolution_bitcast_fusion.2
  21.7 0.6 fusion.13
  22.3 0.8 copy.26
  23.1 0.0 all-gather.8.cloned.1.call-start
  23.1 41.8 %all-gather.6.cloned.1.call-done = f32[4096,128]{1,0:T(8,128)} async-done(((f32[512,128]{1,0:T(8,128)}), f32[4096,128]{1,0:T(8,128)}) %all-gather.6.cloned.1.call-update) | async-done | bytes 2097168 | tf_op jit(solution)/shard_map/all_gather | solution.py:68
  65.0 9.9 %convolution_bitcast_fusion.4 = f32[512,128]{0,1:T(8,128)S(1)} fusion(f32[4096,128]{1,0:T(8,128)} %all-gather.6.cloned.1.call-done, f32[512,4096]{1,0:T(8,128)} %param.14), kind=kOutput, calls=%fused_computation.15 | convolution fusion | flops 3221225472 | bytes 10747904 | tf_op jit(solution)/shard_map/dot_general | solution.py:77
  74.8 16.7 %all_gather.22 = f32[512,256]{0,1:T(8,128)} all-gather(f32[512,128]{0,1:T(8,128)S(1)} %convolution_bitcast_fusion.4), channel_id=1, replica_groups=mesh['sensor'=8,'tx'=4,'ty'=4,'tz'=2] {'tz'}, dimensions={1}, use_global_device_ids=true | all-gather | bytes 786432 | tf_op jit(solution)/shard_map/all_gather | solution.py:82
  91.6 0.0 all-gather.8.cloned.1.call-update
  91.6 0.3 all-gather.12.cloned.1.call-start
  91.9 74.5 %all-gather.8.cloned.1.call-done = f32[512,4096]{0,1:T(8,128)} async-done(((f32[512,256]{0,1:T(8,128)}), f32[512,4096]{0,1:T(8,128)}) %all-gather.8.cloned.1.call-update) | async-done | bytes 8388624 | tf_op jit(solution)/shard_map/all_gather | solution.py:83
  166.4 15.6 %fusion.44 = f32[512,128]{1,0:T(8,128)S(1)} fusion(f32[512,4096]{0,1:T(8,128)} %all-gather.8.cloned.1.call-done, f32[128,4096]{1,0:T(8,128)S(1)} %copy-done), kind=kOutput, calls=%fused_computation.67 | convolution fusion | flops 3221225472 | bytes 10747904 | tf_op jit(solution)/shard_map/dot_general | solution.py:84
  182.0 0.5 fusion.20
  182.5 1.2 fusion.4
  183.7 2.1 convolution_bitcast_fusion.1
  185.8 0.6 fusion.10
  186.4 0.1 copy.30
  186.4 0.6 multiply_reduce_fusion.3
  187.0 1.4 maximum_bitcast_fusion
  188.4 0.7 select_maximum_fusion
  189.2 0.0 all-gather.10.cloned.1.call-start
  189.2 38.7 %all-gather.12.cloned.1.call-done = f32[4160,128]{1,0:T(8,128)} async-done(((f32[520,128]{1,0:T(8,128)}), f32[4160,128]{1,0:T(8,128)}) %all-gather.12.cloned.1.call-update) | async-done | bytes 2129936 | tf_op jit(solution)/shard_map/all_gather | solution.py:72
  227.9 1.7 slice.60
  229.7 0.8 slice_reduce_fusion
  230.4 9.5 %convolution_bitcast_fusion.3 = f32[512,128]{0,1:T(8,128)S(1)} fusion(f32[4096,128]{1,0:T(8,128)S(1)} %bitcast.59, f32[512,4096]{1,0:T(8,128)} %param.14), kind=kOutput, calls=%fused_computation.14 | convolution fusion | flops 3221225472 | bytes 10747904 | tf_op jit(solution)/shard_map/dot_general | solution.py:77
  240.0 0.1 copy.31
  240.1 29.0 %all_gather.26 = f32[520,256]{0,1:T(8,128)} all-gather(f32[520,128]{0,1:T(8,128)S(1)} %pad_maximum_fusion), channel_id=1, replica_groups=mesh['sensor'=8,'tx'=4,'ty'=4,'tz'=2] {'tz'}, dimensions={1}, use_global_device_ids=true | all-gather | bytes 798720 | tf_op jit(solution)/shard_map/all_gather | solution.py:82
  269.1 0.0 all-gather.10.cloned.1.call-update
  269.2 84.2 %all-gather.10.cloned.1.call-done = f32[520,4096]{0,1:T(8,128)} async-done(((f32[520,256]{0,1:T(8,128)}), f32[520,4096]{0,1:T(8,128)}) %all-gather.10.cloned.1.call-update) | async-done | bytes 8519696 | tf_op jit(solution)/shard_map/all_gather | solution.py:83
  353.4 3.0 slice.62
  356.4 1.8 reduce_sum.105
  358.2 0.5 fusion.42
  358.7 15.6 %fusion = f32[512,128]{1,0:T(8,128)S(1)} fusion(f32[128,4096]{1,0:T(8,128)S(1)} %copy-done, f32[520,4096]{0,1:T(8,128)} %all-gather.10.cloned.1.call-done), kind=kOutput, calls=%fused_computation.1 | convolution fusion | flops 3221225472 | bytes 10747904 | tf_op jit(solution)/shard_map/dot_general | solution.py:84
  374.3 0.5 fusion.18
  374.8 1.2 fusion.5
  377.3 0.7 multiply_reduce_fusion.1
  378.0 1.9 pad_maximum_fusion.1
  379.9 0.0 collective-permute-start
  379.9 1.1 collective-permute-done
  381.1 1.9 fusion.58
  383.0 1.6 collective-permute-start.1
  384.6 2.0 collective-permute-done.1
  386.6 1.9 fusion.59
  388.5 2.6 collective-permute-start.2
  391.1 1.9 collective-permute-done.2
  393.0 0.6 collective-permute-start.3
  393.6 3.0 collective-permute-done.3
  396.6 2.1 collective-permute-start.4
  398.7 3.0 collective-permute-done.4
  401.7 0.2 collective-permute-start.5
  401.9 3.3 collective-permute-done.5
  405.3 1.7 collective-permute-start.6
  407.0 3.3 collective-permute-done.6
  410.3 5.7 %collective-permute-start.7 = (f32[3]{0:T(128)S(1)}, f32[3]{0:T(128)S(1)}, u32[]{:S(2)}, u32[]{:S(2)}) collective-permute-start(f32[3]{0:T(128)S(1)} %add.83), channel_id=1, source_target_pairs={{0,1},{1,0},{2,3},{3,2},{4,5},{5,4},{6,7},{7,6},{8,9},{9,8},{10,11... | collective-permute-start | bytes 44 | tf_op jit(solution)/shard_map/ppermute | solution.py:26
  416.1 1.7 collective-permute-done.7
  417.8 0.7 fusion.43
  422.3 0.6 multiply_subtract_fusion
  (28 shorter events, 0.1 us)
Async XLA Ops:
  7.2 11.3 %copy-start = (f32[128,4096]{1,0:T(8,128)S(1)}, f32[128,4096]{1,0:T(8,128)}, u32[]{:S(2)}) copy-start(f32[128,4096]{1,0:T(8,128)} %param.15) | copy-start | bytes 6291460
  7.2 57.8 %all-gather.6.cloned.1.call-start = ((), (), s32[]{:S(2)}) async-start(), calls=%async_computation | async-start | bytes 2359296 | tf_op jit(solution)/shard_map/all_gather | solution.py:68
  10.4 5.5 %copy-start.7 = (s32[16]{0:T(128)S(1)}, s32[16]{0:T(128)}, u32[]{:S(2)}) copy-start(s32[16]{0:T(128)} %param.13) | copy-start | bytes 196
  13.7 4.8 %copy-start.1 = (f32[16,128,128]{2,1,0:T(8,128)S(1)}, f32[16,128,128]{2,1,0:T(8,128)}, u32[]{:S(2)}) copy-start(f32[16,128,128]{2,1,0:T(8,128)} %param.12) | copy-start | bytes 3145732
  13.7 5.8 %copy-start.5 = (f32[16,128]{1,0:T(8,128)S(1)}, f32[16,128]{1,0:T(8,128)}, u32[]{:S(2)}) copy-start(f32[16,128]{1,0:T(8,128)} %param.9) | copy-start | bytes 24580
  13.7 5.9 %copy-start.6 = (f32[16,128]{1,0:T(8,128)S(1)}, f32[16,128]{1,0:T(8,128)}, u32[]{:S(2)}) copy-start(f32[16,128]{1,0:T(8,128)} %param.10) | copy-start | bytes 24580
  16.0 3.6 copy-start.2
  23.1 143.3 %all-gather.8.cloned.1.call-start = ((), (), s32[]{:S(2)}) async-start(), calls=%async_computation.1 | async-start | bytes 8912896 | tf_op jit(solution)/shard_map/all_gather | solution.py:83
  91.6 136.3 %all-gather.12.cloned.1.call-start = ((), (), s32[]{:S(2)}) async-start(), calls=%async_computation.3 | async-start | bytes 2396160 | tf_op jit(solution)/shard_map/all_gather | solution.py:72
  166.4 16.1 %copy-start.3 = (f32[16,64,128]{2,1,0:T(8,128)S(1)}, f32[16,64,128]{2,1,0:T(8,128)}, u32[]{:S(2)}) copy-start(f32[16,64,128]{2,1,0:T(8,128)} %param.11) | copy-start | bytes 1572868
  189.2 164.2 %all-gather.10.cloned.1.call-start = ((), (), s32[]{:S(2)}) async-start(), calls=%async_computation.2 | async-start | bytes 11141120 | tf_op jit(solution)/shard_map/all_gather | solution.py:83
  358.7 16.1 %copy-start.4 = (f32[16,64,128]{2,1,0:T(8,128)S(1)}, f32[16,64,128]{2,1,0:T(8,128)}, u32[]{:S(2)}) copy-start(f32[16,64,128]{2,1,0:T(8,128)} %param.11) | copy-start | bytes 1572868
  379.9 1.2 collective-permute-start
  383.0 3.6 collective-permute-start.1
  388.5 4.5 %collective-permute-start.2 = (f32[3]{0:T(128)S(1)}, f32[3]{0:T(128)S(1)}, u32[]{:S(2)}, u32[]{:S(2)}) collective-permute-start(f32[3]{0:T(128)S(1)} %fusion.59), channel_id=1, source_target_pairs={{0,128},{32,160},{64,192},{96,224},{128,0},{160,32},{192,64},{224,... | collective-permute-start | bytes 44 | tf_op jit(solution)/shard_map/ppermute | solution.py:26
  393.0 3.6 collective-permute-start.3
  396.6 5.1 %collective-permute-start.4 = (f32[3]{0:T(128)S(1)}, f32[3]{0:T(128)S(1)}, u32[]{:S(2)}, u32[]{:S(2)}) collective-permute-start(f32[3]{0:T(128)S(1)} %add.80), channel_id=1, source_target_pairs={{0,16},{8,24},{16,0},{24,8},{1,17},{9,25},{17,1},{25,9},{2,18},{10... | collective-permute-start | bytes 44 | tf_op jit(solution)/shard_map/ppermute | solution.py:26
  401.7 3.6 collective-permute-start.5
  405.3 5.1 %collective-permute-start.6 = (f32[3]{0:T(128)S(1)}, f32[3]{0:T(128)S(1)}, u32[]{:S(2)}, u32[]{:S(2)}) collective-permute-start(f32[3]{0:T(128)S(1)} %add.82), channel_id=1, source_target_pairs={{0,4},{2,6},{4,0},{6,2},{1,5},{3,7},{5,1},{7,3},{8,12},{10,14},{12... | collective-permute-start | bytes 44 | tf_op jit(solution)/shard_map/ppermute | solution.py:26
  410.3 7.5 %collective-permute-start.7 = (f32[3]{0:T(128)S(1)}, f32[3]{0:T(128)S(1)}, u32[]{:S(2)}, u32[]{:S(2)}) collective-permute-start(f32[3]{0:T(128)S(1)} %add.83), channel_id=1, source_target_pairs={{0,1},{1,0},{2,3},{3,2},{4,5},{5,4},{6,7},{7,6},{8,9},{9,8},{10,11... | collective-permute-start | bytes 44 | tf_op jit(solution)/shard_map/ppermute | solution.py:26
Sparse Core Ops, SparseCore 0:
  23.2 41.7 all-gather.5
  91.7 74.6 all-gather.7
  189.3 38.5 all-gather.11
  269.3 84.0 all-gather.9

commit v4 on v3

--- a/solution.py
+++ b/solution.py
@@ -4,7 +4,7 @@
 import numpy as np
 from jax.sharding import Mesh, PartitionSpec as P
 
-PRECISE = lax.Precision.HIGHEST
+PRECISE = lax.Precision.HIGH
 PAY_ROWS = 8
 TM = ("tx", "ty", "tz")
 ALL = ("sensor",) + TM

time: 432 us -> 401 us (0.928)
  the two profiles are of different devices: /device:TPU:2 before, /device:TPU:1 now
where the time goes in v4:
time: 401 us; the launch traced here: 393 us
  waiting for transfers between devices  248 us (62%)
  matrix products  42.5 us (11%)
  blocking collectives  37.9 us (9%)
  between operations  19.2 us (5%)
  starting transfers between devices  18 us (4%)
  local copies, waits for them, and re-layouts  15.6 us (4%)
  other arithmetic  12.4 us (3%)
    all_gather x2, waiting for transfers between devices, operator_apply(): gathered = lax.all_gather(gathered, ('tx', 'ty'), axis=1, tiled=True)  160 us
    all_gather x1, waiting for transfers between devices, operator_apply(): full_field = lax.all_gather(grid_field, 'sensor', axis=0, tiled=True)  41 us
    all_gather x2, blocking collectives, operator_apply(): gathered = lax.all_gather(left_product, 'tz', axis=1, tiled=True)  37.9 us
    all_gather x1, waiting for transfers between devices, operator_apply(): lax.all_gather(jnp.concatenate([grid_field, pad], axis=0), 'sensor', axis...  37.3 us
    dot_general x2, matrix products, operator_apply(): lax.dot_general(gathered[:sensor_dev], time_kernel, (((1,), (1,)), ((), (...  18.2 us
    ppermute x8, starting transfers between devices, butterfly_sum(): lax.ppermute(value, axis, [(i, i ^ stride) for i in range(size)])  17.6 us
    dot_general x2, matrix products, operator_apply(): jnp.dot(sensor_kernel, full_field, precision=PRECISE, preferred_element_t...  16.2 us
    ppermute x8, waiting for transfers between devices, butterfly_sum(): lax.ppermute(value, axis, [(i, i ^ stride) for i in range(size)])  8.95 us
  transfers between devices with their start and end apart: 12, of which 12 were waited for; matrix products, arithmetic and copies ran while one was open for 0% of the time, Pallas kernels for 0%

profile of v4, /device:TPU:1, one launch (start us, length us, event | category | flops | bytes accessed | tf_op | source)
XLA Modules:
  0.0 393.3 jit_solution(16358520355360214378)
XLA Ops:
  7.2 0.0 all-gather.6.cloned.1.call-start
  7.2 1.4 constant_dynamic-slice_fusion
  8.7 1.8 reshape.62
  10.4 3.3 copy.22
  13.7 2.2 gather_fusion
  16.0 0.4 fusion.22
  16.4 1.8 fusion.6
  18.2 0.6 fusion.3
  18.8 1.1 convolution_bitcast_fusion.2
  20.0 0.5 fusion.13
  20.5 0.8 copy.26
  21.3 0.0 all-gather.8.cloned.1.call-start
  21.3 41.0 %all-gather.6.cloned.1.call-done = f32[4096,128]{1,0:T(8,128)} async-done(((f32[512,128]{1,0:T(8,128)}), f32[4096,128]{1,0:T(8,128)}) %all-gather.6.cloned.1.call-update) | async-done | bytes 2097168 | tf_op jit(solution)/shard_map/all_gather | solution.py:68
  62.3 8.4 %convolution_bitcast_fusion.4 = f32[512,128]{0,1:T(8,128)S(1)} fusion(f32[4096,128]{1,0:T(8,128)} %all-gather.6.cloned.1.call-done, f32[512,4096]{1,0:T(8,128)} %param.14), kind=kOutput, calls=%fused_computation.15 | convolution fusion | flops 1610612736 | bytes 10747904 | tf_op jit(solution)/shard_map/dot_general | solution.py:77
  70.7 17.2 %all_gather.22 = f32[512,256]{0,1:T(8,128)} all-gather(f32[512,128]{0,1:T(8,128)S(1)} %convolution_bitcast_fusion.4), channel_id=1, replica_groups=mesh['sensor'=8,'tx'=4,'ty'=4,'tz'=2] {'tz'}, dimensions={1}, use_global_device_ids=true | all-gather | bytes 786432 | tf_op jit(solution)/shard_map/all_gather | solution.py:82
  87.9 0.0 all-gather.8.cloned.1.call-update
  87.9 0.2 all-gather.12.cloned.1.call-start
  88.2 75.6 %all-gather.8.cloned.1.call-done = f32[512,4096]{0,1:T(8,128)} async-done(((f32[512,256]{0,1:T(8,128)}), f32[512,4096]{0,1:T(8,128)}) %all-gather.8.cloned.1.call-update) | async-done | bytes 8388624 | tf_op jit(solution)/shard_map/all_gather | solution.py:83
  163.8 9.1 %fusion.44 = f32[512,128]{1,0:T(8,128)S(1)} fusion(f32[512,4096]{0,1:T(8,128)} %all-gather.8.cloned.1.call-done, f32[128,4096]{1,0:T(8,128)S(1)} %copy-done), kind=kOutput, calls=%fused_computation.67 | convolution fusion | flops 1610612736 | bytes 10747904 | tf_op jit(solution)/shard_map/dot_general | solution.py:84
  172.9 0.4 fusion.20
  173.3 0.7 fusion.4
  173.9 1.2 convolution_bitcast_fusion.1
  175.1 0.5 fusion.10
  175.6 0.1 copy.30
  175.6 0.6 multiply_reduce_fusion.3
  176.2 1.4 maximum_bitcast_fusion
  177.6 0.7 select_maximum_fusion
  178.4 0.0 all-gather.10.cloned.1.call-start
  178.4 37.3 %all-gather.12.cloned.1.call-done = f32[4160,128]{1,0:T(8,128)} async-done(((f32[520,128]{1,0:T(8,128)}), f32[4160,128]{1,0:T(8,128)}) %all-gather.12.cloned.1.call-update) | async-done | bytes 2129936 | tf_op jit(solution)/shard_map/all_gather | solution.py:72
  215.7 1.7 slice.60
  217.4 0.8 slice_reduce_fusion
  218.2 7.9 %convolution_bitcast_fusion.3 = f32[512,128]{0,1:T(8,128)S(1)} fusion(f32[4096,128]{1,0:T(8,128)S(1)} %bitcast.59, f32[512,4096]{1,0:T(8,128)} %param.14), kind=kOutput, calls=%fused_computation.14 | convolution fusion | flops 1610612736 | bytes 10747904 | tf_op jit(solution)/shard_map/dot_general | solution.py:77
  226.1 0.1 copy.31
  226.2 20.7 %all_gather.26 = f32[520,256]{0,1:T(8,128)} all-gather(f32[520,128]{0,1:T(8,128)S(1)} %pad_maximum_fusion), channel_id=1, replica_groups=mesh['sensor'=8,'tx'=4,'ty'=4,'tz'=2] {'tz'}, dimensions={1}, use_global_device_ids=true | all-gather | bytes 798720 | tf_op jit(solution)/shard_map/all_gather | solution.py:82
  247.0 0.0 all-gather.10.cloned.1.call-update
  247.0 84.8 %all-gather.10.cloned.1.call-done = f32[520,4096]{0,1:T(8,128)} async-done(((f32[520,256]{0,1:T(8,128)}), f32[520,4096]{0,1:T(8,128)}) %all-gather.10.cloned.1.call-update) | async-done | bytes 8519696 | tf_op jit(solution)/shard_map/all_gather | solution.py:83
  331.8 3.0 slice.62
  334.8 1.8 reduce_sum.105
  336.5 0.5 fusion.42
  337.1 9.1 %fusion = f32[512,128]{1,0:T(8,128)S(1)} fusion(f32[128,4096]{1,0:T(8,128)S(1)} %copy-done, f32[520,4096]{0,1:T(8,128)} %all-gather.10.cloned.1.call-done), kind=kOutput, calls=%fused_computation.1 | convolution fusion | flops 1610612736 | bytes 10747904 | tf_op jit(solution)/shard_map/dot_general | solution.py:84
  346.2 0.4 fusion.18
  346.6 0.7 fusion.5
  348.6 0.7 multiply_reduce_fusion.1
  349.2 1.9 pad_maximum_fusion.1
  351.2 0.9 collective-permute-start
  352.0 0.8 collective-permute-done
  352.9 1.9 fusion.58
  354.8 1.3 collective-permute-start.1
  356.1 1.1 collective-permute-done.1
  357.2 1.9 fusion.59
  359.2 2.3 collective-permute-start.2
  361.5 1.1 collective-permute-done.2
  362.5 1.2 collective-permute-start.3
  363.7 1.2 collective-permute-done.3
  364.9 2.7 collective-permute-start.4
  367.6 1.2 collective-permute-done.4
  368.9 1.1 collective-permute-start.5
  370.0 1.3 collective-permute-done.5
  371.3 2.7 collective-permute-start.6
  374.0 1.2 collective-permute-done.6
  375.2 5.5 %collective-permute-start.7 = (f32[3]{0:T(128)S(1)}, f32[3]{0:T(128)S(1)}, u32[]{:S(2)}, u32[]{:S(2)}) collective-permute-start(f32[3]{0:T(128)S(1)} %add.83), channel_id=1, source_target_pairs={{0,1},{1,0},{2,3},{3,2},{4,5},{5,4},{6,7},{7,6},{8,9},{9,8},{10,11... | collective-permute-start | bytes 44 | tf_op jit(solution)/shard_map/ppermute | solution.py:26
  380.7 1.0 collective-permute-done.7
  381.6 0.7 fusion.43
  386.1 0.6 multiply_subtract_fusion
  (28 shorter events, 0.1 us)
Async XLA Ops:
  7.2 11.0 %copy-start = (f32[128,4096]{1,0:T(8,128)S(1)}, f32[128,4096]{1,0:T(8,128)}, u32[]{:S(2)}) copy-start(f32[128,4096]{1,0:T(8,128)} %param.15) | copy-start | bytes 6291460
  7.2 55.2 %all-gather.6.cloned.1.call-start = ((), (), s32[]{:S(2)}) async-start(), calls=%async_computation | async-start | bytes 2359296 | tf_op jit(solution)/shard_map/all_gather | solution.py:68
  10.4 5.5 %copy-start.7 = (s32[16]{0:T(128)S(1)}, s32[16]{0:T(128)}, u32[]{:S(2)}) copy-start(s32[16]{0:T(128)} %param.13) | copy-start | bytes 196
  13.7 4.4 %copy-start.1 = (f32[16,128,128]{2,1,0:T(8,128)S(1)}, f32[16,128,128]{2,1,0:T(8,128)}, u32[]{:S(2)}) copy-start(f32[16,128,128]{2,1,0:T(8,128)} %param.12) | copy-start | bytes 3145732
  13.7 5.1 %copy-start.5 = (f32[16,128]{1,0:T(8,128)S(1)}, f32[16,128]{1,0:T(8,128)}, u32[]{:S(2)}) copy-start(f32[16,128]{1,0:T(8,128)} %param.9) | copy-start | bytes 24580
  13.7 5.1 %copy-start.6 = (f32[16,128]{1,0:T(8,128)S(1)}, f32[16,128]{1,0:T(8,128)}, u32[]{:S(2)}) copy-start(f32[16,128]{1,0:T(8,128)} %param.10) | copy-start | bytes 24580
  16.0 2.8 copy-start.2
  21.3 142.5 %all-gather.8.cloned.1.call-start = ((), (), s32[]{:S(2)}) async-start(), calls=%async_computation.1 | async-start | bytes 8912896 | tf_op jit(solution)/shard_map/all_gather | solution.py:83
  87.9 127.8 %all-gather.12.cloned.1.call-start = ((), (), s32[]{:S(2)}) async-start(), calls=%async_computation.3 | async-start | bytes 2396160 | tf_op jit(solution)/shard_map/all_gather | solution.py:72
  163.7 9.5 %copy-start.3 = (f32[16,64,128]{2,1,0:T(8,128)S(1)}, f32[16,64,128]{2,1,0:T(8,128)}, u32[]{:S(2)}) copy-start(f32[16,64,128]{2,1,0:T(8,128)} %param.11) | copy-start | bytes 1572868
  178.4 153.4 %all-gather.10.cloned.1.call-start = ((), (), s32[]{:S(2)}) async-start(), calls=%async_computation.2 | async-start | bytes 11141120 | tf_op jit(solution)/shard_map/all_gather | solution.py:83
  337.1 9.5 %copy-start.4 = (f32[16,64,128]{2,1,0:T(8,128)S(1)}, f32[16,64,128]{2,1,0:T(8,128)}, u32[]{:S(2)}) copy-start(f32[16,64,128]{2,1,0:T(8,128)} %param.11) | copy-start | bytes 1572868
  351.2 1.7 collective-permute-start
  354.8 2.4 collective-permute-start.1
  359.2 3.3 collective-permute-start.2
  362.5 2.4 collective-permute-start.3
  364.9 3.9 collective-permute-start.4
  368.9 2.4 collective-permute-start.5
  371.3 3.9 collective-permute-start.6
  375.2 6.4 %collective-permute-start.7 = (f32[3]{0:T(128)S(1)}, f32[3]{0:T(128)S(1)}, u32[]{:S(2)}, u32[]{:S(2)}) collective-permute-start(f32[3]{0:T(128)S(1)} %add.83), channel_id=1, source_target_pairs={{0,1},{1,0},{2,3},{3,2},{4,5},{5,4},{6,7},{7,6},{8,9},{9,8},{10,11... | collective-permute-start | bytes 44 | tf_op jit(solution)/shard_map/ppermute | solution.py:26
Sparse Core Ops, SparseCore 0:
  21.4 40.9 all-gather.5
  88.1 75.6 all-gather.7
  178.5 37.1 all-gather.11
  247.1 84.6 all-gather.9

commit v5 on v2

--- a/solution.py
+++ b/solution.py
@@ -16,6 +16,15 @@
         + lax.axis_index("ty") * lax.axis_size("tz")
         + lax.axis_index("tz")
     )
+
+
+def all_device_sum(value):
+    count = 1
+    for axis in ALL:
+        count *= lax.axis_size(axis)
+    copies = jnp.broadcast_to(value[None, :], (count, value.shape[0]))
+    rows = lax.all_to_all(copies, ALL, 0, 0, tiled=True)
+    return jnp.sum(rows, axis=0)
 
 
 def on_device(
@@ -105,15 +114,14 @@
     residual1 = residual0 - step0 * image0
     precond1 = inverse * residual1
     image_precond1 = image0 - step0 * image_scaled
-    second = lax.psum(
+    second = all_device_sum(
         jnp.stack(
             [
                 jnp.sum(residual1 * precond1),
                 jnp.sum(precond1 * image_precond1),
                 jnp.sum(precond1 * image0 + direction0 * image_precond1),
             ]
-        ),
-        ALL,
+        )
     )
     inner1 = second[0]
     ratio = inner1 / inner0

time: 459 us -> 409 us (0.89)
  blocking collectives: 114 us -> 62.5 us
    psum x1 -> x0, blocking collectives: 75.9 us -> none  [on_device(): lax.psum(jnp.stack([jnp.sum(residual1 * precond1), jnp.sum(precond1 * ima...]
    all_to_all x0 -> x1, blocking collectives: none -> 24.6 us  [all_device_sum(): rows = lax.all_to_all(copies, ALL, 0, 0, tiled=True)]
where the time goes in v5:
time: 409 us; the launch traced here: 408 us
  waiting for transfers between devices  239 us (58%)
  matrix products  62.7 us (15%)
  blocking collectives  62.5 us (15%)
  between operations  19.2 us (5%)
  local copies, waits for them, and re-layouts  15.7 us (4%)
  other arithmetic  8.84 us (2%)
    all_gather x2, waiting for transfers between devices, operator_apply(): gathered = lax.all_gather(gathered, ('tx', 'ty'), axis=1, tiled=True)  160 us
    all_gather x1, waiting for transfers between devices, operator_apply(): full_field = lax.all_gather(grid_field, 'sensor', axis=0, tiled=True)  41 us
    all_gather x2, blocking collectives, operator_apply(): gathered = lax.all_gather(left_product, 'tz', axis=1, tiled=True)  37.9 us
    all_gather x1, waiting for transfers between devices, operator_apply(): lax.all_gather(jnp.concatenate([grid_field, pad], axis=0), 'sensor', axis...  37.3 us
    dot_general x2, matrix products, operator_apply(): lax.dot_general(gathered[:sensor_dev], time_kernel, (((1,), (1,)), ((), (...  31.2 us
    all_to_all x1, blocking collectives, all_device_sum(): rows = lax.all_to_all(copies, ALL, 0, 0, tiled=True)  24.6 us
    dot_general x2, matrix products, operator_apply(): jnp.dot(sensor_kernel, full_field, precision=PRECISE, preferred_element_t...  19.4 us
  transfers between devices with their start and end apart: 4, of which 4 were waited for; matrix products, arithmetic and copies ran while one was open for 0% of the time, Pallas kernels for 0%

profile of v5, /device:TPU:1, one launch (start us, length us, event | category | flops | bytes accessed | tf_op | source)
XLA Modules:
  0.0 408.1 jit_solution(1086271385789186239)
XLA Ops:
  7.2 0.0 copy-start
  7.2 0.0 all-gather.6.cloned.1.call-start
  7.2 1.4 constant_dynamic-slice_fusion
  8.7 1.8 reshape.68
  10.5 0.0 copy-start.7
  10.5 3.3 copy.59
  13.7 0.0 copy-start.5
  13.7 0.0 copy-start.6
  13.7 2.2 gather_fusion
  16.0 0.0 copy-done.7
  16.0 0.0 copy-start.2
  16.0 0.5 fusion.22
  16.5 2.0 fusion.6
  18.5 0.0 copy-done
  18.5 0.0 copy-done.1
  18.5 1.0 fusion.3
  19.6 0.0 copy-done.5
  19.6 0.0 copy-done.6
  19.6 0.0 copy-done.2
  19.6 2.1 convolution_bitcast_fusion.2
  21.7 0.6 fusion.13
  22.3 0.8 copy.63
  23.1 0.0 all-gather.6.cloned.1.call-update
  23.1 0.0 all-gather.8.cloned.1.call-start
  23.1 41.0 %all-gather.6.cloned.1.call-done = f32[4096,128]{1,0:T(8,128)} async-done(((f32[512,128]{1,0:T(8,128)}), f32[4096,128]{1,0:T(8,128)}) %all-gather.6.cloned.1.call-update) | async-done | bytes 2097168 | tf_op jit(solution)/shard_map/all_gather | solution.py:67
  64.2 9.9 %convolution_bitcast_fusion.4 = f32[512,128]{0,1:T(8,128)S(1)} fusion(f32[4096,128]{1,0:T(8,128)} %all-gather.6.cloned.1.call-done, f32[512,4096]{1,0:T(8,128)} %param.14), kind=kOutput, calls=%fused_computation.15 | convolution fusion | flops 3221225472 | bytes 10747904 | tf_op jit(solution)/shard_map/dot_general | solution.py:76
  74.1 17.2 %all_gather.22 = f32[512,256]{0,1:T(8,128)} all-gather(f32[512,128]{0,1:T(8,128)S(1)} %convolution_bitcast_fusion.4), channel_id=1, replica_groups=mesh['sensor'=8,'tx'=4,'ty'=4,'tz'=2] {'tz'}, dimensions={1}, use_global_device_ids=true | all-gather | bytes 786432 | tf_op jit(solution)/shard_map/all_gather | solution.py:81
  91.3 0.0 all-gather.8.cloned.1.call-update
  91.3 0.2 all-gather.12.cloned.1.call-start
  91.5 75.6 %all-gather.8.cloned.1.call-done = f32[512,4096]{0,1:T(8,128)} async-done(((f32[512,256]{0,1:T(8,128)}), f32[512,4096]{0,1:T(8,128)}) %all-gather.8.cloned.1.call-update) | async-done | bytes 8388624 | tf_op jit(solution)/shard_map/all_gather | solution.py:82
  167.1 15.6 %fusion.44 = f32[512,128]{1,0:T(8,128)S(1)} fusion(f32[512,4096]{0,1:T(8,128)} %all-gather.8.cloned.1.call-done, f32[128,4096]{1,0:T(8,128)S(1)} %copy-done), kind=kOutput, calls=%fused_computation.67 | convolution fusion | flops 3221225472 | bytes 10747904 | tf_op jit(solution)/shard_map/dot_general | solution.py:83
  182.7 0.5 fusion.20
  183.2 0.0 copy-done.3
  183.2 1.2 fusion.4
  184.4 2.1 convolution_bitcast_fusion.1
  186.5 0.6 fusion.10
  187.1 0.1 copy.67
  187.1 0.6 multiply_reduce_fusion.3
  187.7 1.4 maximum_bitcast_fusion
  189.1 0.8 select_maximum_fusion
  189.8 0.0 all-gather.12.cloned.1.call-update
  189.9 0.0 all-gather.10.cloned.1.call-start
  189.9 37.3 %all-gather.12.cloned.1.call-done = f32[4160,128]{1,0:T(8,128)} async-done(((f32[520,128]{1,0:T(8,128)}), f32[4160,128]{1,0:T(8,128)}) %all-gather.12.cloned.1.call-update) | async-done | bytes 2129936 | tf_op jit(solution)/shard_map/all_gather | solution.py:71
  227.2 1.7 slice.60
  229.0 0.8 slice_reduce_fusion
  229.7 9.5 %convolution_bitcast_fusion.3 = f32[512,128]{0,1:T(8,128)S(1)} fusion(f32[4096,128]{1,0:T(8,128)S(1)} %bitcast.59, f32[512,4096]{1,0:T(8,128)} %param.14), kind=kOutput, calls=%fused_computation.14 | convolution fusion | flops 3221225472 | bytes 10747904 | tf_op jit(solution)/shard_map/dot_general | solution.py:76
  239.3 0.1 copy.68
  239.4 20.7 %all_gather.26 = f32[520,256]{0,1:T(8,128)} all-gather(f32[520,128]{0,1:T(8,128)S(1)} %pad_maximum_fusion), channel_id=1, replica_groups=mesh['sensor'=8,'tx'=4,'ty'=4,'tz'=2] {'tz'}, dimensions={1}, use_global_device_ids=true | all-gather | bytes 798720 | tf_op jit(solution)/shard_map/all_gather | solution.py:81
  260.1 0.0 all-gather.10.cloned.1.call-update
  260.2 84.8 %all-gather.10.cloned.1.call-done = f32[520,4096]{0,1:T(8,128)} async-done(((f32[520,256]{0,1:T(8,128)}), f32[520,4096]{0,1:T(8,128)}) %all-gather.10.cloned.1.call-update) | async-done | bytes 8519696 | tf_op jit(solution)/shard_map/all_gather | solution.py:82
  344.9 3.0 slice.62
  348.0 1.8 reduce_sum.114
  349.7 0.5 fusion.42
  350.2 15.6 %fusion = f32[512,128]{1,0:T(8,128)S(1)} fusion(f32[128,4096]{1,0:T(8,128)S(1)} %copy-done, f32[520,4096]{0,1:T(8,128)} %all-gather.10.cloned.1.call-done), kind=kOutput, calls=%fused_computation.1 | convolution fusion | flops 3221225472 | bytes 10747904 | tf_op jit(solution)/shard_map/dot_general | solution.py:83
  365.8 0.5 fusion.18
  366.3 0.0 copy-done.4
  366.3 1.2 fusion.5
  368.8 0.7 multiply_reduce_fusion.1
  369.5 2.0 pad_maximum_fusion.1
  371.5 0.1 broadcast_in_dim.2
  371.6 24.6 %all_to_all.6 = f32[256,1,3]{2,1,0:T(1,128)S(1)} all-to-all(f32[256,1,3]{2,1,0:T(1,128)S(1)} %broadcast_in_dim.2), channel_id=1, replica_groups=mesh['sensor'=8,'tx'=4,'ty'=4,'tz'=2] {'sensor','tx','ty','tz'}, dimensions={0} | all-to-all | bytes 6144 | tf_op jit(solution)/shard_map/all_to_all | solution.py:26
  396.2 0.3 reduce_sum.119
  396.5 0.7 fusion.43
  401.0 0.6 multiply_subtract_fusion
  (7 shorter events, 0.1 us)
Async XLA Ops:
  7.2 11.3 %copy-start = (f32[128,4096]{1,0:T(8,128)S(1)}, f32[128,4096]{1,0:T(8,128)}, u32[]{:S(2)}) copy-start(f32[128,4096]{1,0:T(8,128)} %param.15) | copy-start | bytes 6291460
  7.2 57.0 %all-gather.6.cloned.1.call-start = ((), (), s32[]{:S(2)}) async-start(), calls=%async_computation.1 | async-start | bytes 2359296 | tf_op jit(solution)/shard_map/all_gather | solution.py:67
  10.5 5.5 %copy-start.7 = (s32[16]{0:T(128)S(1)}, s32[16]{0:T(128)}, u32[]{:S(2)}) copy-start(s32[16]{0:T(128)} %param.13) | copy-start | bytes 196
  13.7 4.8 %copy-start.1 = (f32[16,128,128]{2,1,0:T(8,128)S(1)}, f32[16,128,128]{2,1,0:T(8,128)}, u32[]{:S(2)}) copy-start(f32[16,128,128]{2,1,0:T(8,128)} %param.12) | copy-start | bytes 3145732
  13.7 5.8 %copy-start.5 = (f32[16,128]{1,0:T(8,128)S(1)}, f32[16,128]{1,0:T(8,128)}, u32[]{:S(2)}) copy-start(f32[16,128]{1,0:T(8,128)} %param.9) | copy-start | bytes 24580
  13.7 5.9 %copy-start.6 = (f32[16,128]{1,0:T(8,128)S(1)}, f32[16,128]{1,0:T(8,128)}, u32[]{:S(2)}) copy-start(f32[16,128]{1,0:T(8,128)} %param.10) | copy-start | bytes 24580
  16.0 3.6 copy-start.2
  23.1 144.0 %all-gather.8.cloned.1.call-start = ((), (), s32[]{:S(2)}) async-start(), calls=%async_computation.2 | async-start | bytes 8912896 | tf_op jit(solution)/shard_map/all_gather | solution.py:82
  91.3 135.9 %all-gather.12.cloned.1.call-start = ((), (), s32[]{:S(2)}) async-start(), calls=%async_computation.4 | async-start | bytes 2396160 | tf_op jit(solution)/shard_map/all_gather | solution.py:71
  167.1 16.1 %copy-start.3 = (f32[16,64,128]{2,1,0:T(8,128)S(1)}, f32[16,64,128]{2,1,0:T(8,128)}, u32[]{:S(2)}) copy-start(f32[16,64,128]{2,1,0:T(8,128)} %param.11) | copy-start | bytes 1572868
  189.9 155.1 %all-gather.10.cloned.1.call-start = ((), (), s32[]{:S(2)}) async-start(), calls=%async_computation.3 | async-start | bytes 11141120 | tf_op jit(solution)/shard_map/all_gather | solution.py:82
  350.2 16.1 %copy-start.4 = (f32[16,64,128]{2,1,0:T(8,128)S(1)}, f32[16,64,128]{2,1,0:T(8,128)}, u32[]{:S(2)}) copy-start(f32[16,64,128]{2,1,0:T(8,128)} %param.11) | copy-start | bytes 1572868
Sparse Core Ops, SparseCore 0:
  23.2 40.9 all-gather.5
  91.4 75.6 all-gather.7
  190.0 37.1 all-gather.11
  260.3 84.6 all-gather.9

commit v6 on v5

--- a/solution.py
+++ b/solution.py
@@ -68,20 +68,19 @@
         else:
             pad = jnp.zeros((PAY_ROWS, time_dev), jnp.float32)
             pad = pad.at[0, : payload.shape[0]].set(payload)
-            both = lax.all_gather(
-                jnp.concatenate([grid_field, pad], axis=0), "sensor", axis=0, tiled=False
-            )
-            full_field = both[:, :sensor_dev, :].reshape(-1, time_dev)
-            sensor_sum = jnp.sum(both[:, sensor_dev:, :], axis=0)
+            full_field, pads = lax.all_gather((grid_field, pad), "sensor", axis=0, tiled=True)
+            pad = jnp.sum(pads.reshape(-1, PAY_ROWS, time_dev), axis=0)
         left_product = jnp.dot(
             sensor_kernel, full_field, precision=PRECISE, preferred_element_type=jnp.float32
         )
-        if payload is not None:
-            left_product = jnp.concatenate([left_product, sensor_sum], axis=0)
-        gathered = lax.all_gather(left_product, "tz", axis=1, tiled=True)
-        gathered = lax.all_gather(gathered, ("tx", "ty"), axis=1, tiled=True)
+        if payload is None:
+            gathered = lax.all_gather(left_product, "tz", axis=1, tiled=True)
+            gathered = lax.all_gather(gathered, ("tx", "ty"), axis=1, tiled=True)
+        else:
+            gathered, pad = lax.all_gather((left_product, pad), "tz", axis=1, tiled=True)
+            gathered, pad = lax.all_gather((gathered, pad), ("tx", "ty"), axis=1, tiled=True)
         smooth = lax.dot_general(
-            gathered[:sensor_dev],
+            gathered,
             time_kernel,
             (((1,), (1,)), ((), ())),
             precision=PRECISE,
@@ -94,9 +93,7 @@
         image = jnp.sum(sensor_weights * interp_cols, axis=1) + noise_var * vector
         if payload is None:
             return image, None
-        totals = jnp.sum(
-            gathered[sensor_dev:].reshape(PAY_ROWS, n_tm, time_dev), axis=1
-        )[0, : payload.shape[0]]
+        totals = jnp.sum(pad.reshape(PAY_ROWS, n_tm, time_dev), axis=1)[0, : payload.shape[0]]
         return image, totals
 
     residual0 = readings

time: 409 us -> 385 us (0.941)
  waiting for transfers between devices: 239 us -> 184 us
  blocking collectives: 62.5 us -> 101 us
  local copies, waits for them, and re-layouts: 15.7 us -> 11.6 us
    all_gather x2 -> x1, waiting for transfers between devices: 160 us -> 75.6 us  [operator_apply(): gathered = lax.all_gather(gathered, ('tx', 'ty'), axis=1, tiled=True)]
    all_gather x0 -> x4, blocking collectives: none -> 59.1 us  [the longest x2 24.3 us: operator_apply(): lax.all_gather((left_product, pad), 'tz', axis=1, tiled=True)]
    all_gather x1 -> x2, waiting for transfers between devices: 37.3 us -> 67.4 us  [the longest x1 37.1 us: operator_apply(): lax.all_gather((grid_field, pad), 'sensor', axis=0, tiled=True)]
    all_gather x2 -> x1, blocking collectives: 37.9 us -> 17.2 us  [operator_apply(): gathered = lax.all_gather(left_product, 'tz', axis=1, tiled=True)]
    slice x2 -> x0, local copies, waits for them, and re-layouts: 4.76 us -> none  [the longest x1 3.02 us: operator_apply(): gathered[sensor_dev:].reshape(PAY_ROWS, n_tm, time_dev)]
  transfers between devices with their start and end apart: 4 -> 4, of which waited for: 4 -> 4; matrix products, arithmetic and copies ran while one was open for 0% -> 1% of each run, Pallas kernels for 0% -> 0%
where the time goes in v6:
time: 385 us
  waiting for transfers between devices  184 us (48%)
  blocking collectives  101 us (26%)
  matrix products  63.2 us (16%)
  between operations  19.2 us (5%)
  local copies, waits for them, and re-layouts  11.6 us (3%)
  other arithmetic  5.58 us (1%)
    all_gather x1, waiting for transfers between devices, operator_apply(): gathered = lax.all_gather(gathered, ('tx', 'ty'), axis=1, tiled=True)  75.6 us
    all_gather x1, waiting for transfers between devices, operator_apply(): full_field = lax.all_gather(grid_field, 'sensor', axis=0, tiled=True)  41 us
    all_gather x1, waiting for transfers between devices, operator_apply(): lax.all_gather((grid_field, pad), 'sensor', axis=0, tiled=True)  37.1 us
    dot_general x2, matrix products, operator_apply(): lax.dot_general(gathered, time_kernel, (((1,), (1,)), ((), ())), precisio...  31.2 us
    all_gather x1, waiting for transfers between devices, operator_apply(): lax.all_gather((gathered, pad), ('tx', 'ty'), axis=1, tiled=True)  30.3 us
    all_to_all x1, blocking collectives, all_device_sum(): rows = lax.all_to_all(copies, ALL, 0, 0, tiled=True)  24.4 us
    all_gather x2, blocking collectives, operator_apply(): lax.all_gather((left_product, pad), 'tz', axis=1, tiled=True)  24.3 us
    dot_general x2, matrix products, operator_apply(): jnp.dot(sensor_kernel, full_field, precision=PRECISE, preferred_element_t...  19.7 us
  transfers between devices with their start and end apart: 4, of which 4 were waited for; matrix products, arithmetic and copies ran while one was open for 1% of the time, Pallas kernels for 0%

profile of v6, /device:TPU:1, one launch (start us, length us, event | category | flops | bytes accessed | tf_op | source)
XLA Modules:
  0.0 384.8 jit_solution(8374476407365329065)
XLA Ops:
  7.2 0.0 copy-start
  7.2 0.0 all-gather.5.cloned.1.call-start
  7.2 1.4 constant_dynamic-slice_fusion
  8.7 1.8 reshape.68
  10.5 0.0 copy-start.7
  10.5 3.3 copy.45
  13.7 0.0 copy-start.1
  13.7 0.0 copy-start.5
  13.7 0.0 copy-start.6
  13.7 2.2 gather_fusion
  16.0 0.0 copy-done.7
  16.0 0.0 copy-start.2
  16.0 0.5 fusion.20
  16.5 2.1 fusion.4
  18.6 0.0 copy-done
  18.6 0.0 copy-done.1
  18.6 1.0 fusion.1
  19.7 0.0 copy-done.5
  19.7 0.0 copy-done.6
  19.7 0.0 copy-done.2
  19.7 2.1 convolution_bitcast_fusion.2
  21.8 0.6 fusion.11
  22.4 0.8 copy.49
  23.2 0.0 all-gather.5.cloned.1.call-update
  23.2 0.0 all-gather.7.cloned.1.call-start
  23.2 41.0 %all-gather.5.cloned.1.call-done = f32[4096,128]{1,0:T(8,128)} async-done(((f32[512,128]{1,0:T(8,128)}), f32[4096,128]{1,0:T(8,128)}) %all-gather.5.cloned.1.call-update) | async-done | bytes 2097168 | tf_op jit(solution)/shard_map/all_gather | solution.py:67
  64.3 9.9 %convolution_bitcast_fusion.4 = f32[512,128]{0,1:T(8,128)S(1)} fusion(f32[4096,128]{1,0:T(8,128)} %all-gather.5.cloned.1.call-done, f32[512,4096]{1,0:T(8,128)} %param.14), kind=kOutput, calls=%fused_computation.13 | convolution fusion | flops 3221225472 | bytes 10747904 | tf_op jit(solution)/shard_map/dot_general | solution.py:73
  74.2 17.2 %all_gather.28 = f32[512,256]{0,1:T(8,128)} all-gather(f32[512,128]{0,1:T(8,128)S(1)} %convolution_bitcast_fusion.4), channel_id=1, replica_groups=mesh['sensor'=8,'tx'=4,'ty'=4,'tz'=2] {'tz'}, dimensions={1}, use_global_device_ids=true | all-gather | bytes 786432 | tf_op jit(solution)/shard_map/all_gather | solution.py:77
  91.3 0.0 all-gather.7.cloned.1.call-update
  91.4 0.2 all-gather.9.cloned.1.call-start
  91.6 75.6 %all-gather.7.cloned.1.call-done = f32[512,4096]{0,1:T(8,128)} async-done(((f32[512,256]{0,1:T(8,128)}), f32[512,4096]{0,1:T(8,128)}) %all-gather.7.cloned.1.call-update) | async-done | bytes 8388624 | tf_op jit(solution)/shard_map/all_gather | solution.py:78
  167.2 0.0 copy-start.3
  167.2 15.6 %fusion.42 = f32[512,128]{1,0:T(8,128)S(1)} fusion(f32[512,4096]{0,1:T(8,128)} %all-gather.7.cloned.1.call-done, f32[128,4096]{1,0:T(8,128)S(1)} %copy-done), kind=kOutput, calls=%fused_computation.63 | convolution fusion | flops 3221225472 | bytes 10747904 | tf_op jit(solution)/shard_map/dot_general | solution.py:82
  182.8 0.5 fusion.18
  183.2 0.0 copy-done.3
  183.3 1.2 fusion.2
  184.5 2.1 convolution_bitcast_fusion.1
  186.5 0.6 fusion.8
  187.1 0.8 copy.53
  187.9 0.0 all-gather.9.cloned.1.call-update
  187.9 0.0 all-gather.11.cloned.1.call-start
  188.0 37.1 %all-gather.9.cloned.1.call-done = f32[4096,128]{1,0:T(8,128)} async-done(((f32[512,128]{1,0:T(8,128)}), f32[4096,128]{1,0:T(8,128)}) %all-gather.9.cloned.1.call-update) | async-done | bytes 2097168 | tf_op jit(solution)/shard_map/all_gather | solution.py:71
  225.1 9.9 %convolution_bitcast_fusion.3 = f32[512,128]{0,1:T(8,128)S(1)} fusion(f32[4096,128]{1,0:T(8,128)} %all-gather.9.cloned.1.call-done, f32[512,4096]{1,0:T(8,128)} %param.14), kind=kOutput, calls=%fused_computation.12 | convolution fusion | flops 3221225472 | bytes 10747904 | tf_op jit(solution)/shard_map/dot_general | solution.py:73
  235.0 17.2 %all_gather.34 = f32[512,256]{0,1:T(8,128)} all-gather(f32[512,128]{0,1:T(8,128)S(1)} %convolution_bitcast_fusion.3), channel_id=1, replica_groups=mesh['sensor'=8,'tx'=4,'ty'=4,'tz'=2] {'tz'}, dimensions={1}, use_global_device_ids=true | all-gather | bytes 786432 | tf_op jit(solution)/shard_map/all_gather | solution.py:80
  252.2 0.0 all-gather.11.cloned.1.call-update
  252.2 0.6 multiply_reduce_fusion.3
  252.8 1.4 maximum_bitcast_fusion
  254.2 15.8 %all_gather.30 = f32[64,128]{1,0:T(8,128)S(1)} all-gather(f32[8,128]{1,0:T(8,128)S(1)} %scatter.4), channel_id=1, replica_groups=mesh['sensor'=8,'tx'=4,'ty'=4,'tz'=2] {'sensor'}, dimensions={0}, use_global_device_ids=true | all-gather | bytes 36864 | tf_op jit(solution)/shard_map/all_gather | solution.py:71
  270.0 7.1 %all_gather.31 = f32[8,256]{1,0:T(8,128)S(1)} all-gather(f32[8,128]{1,0:T(8,128)S(1)} %bitcast_reduce_fusion.1), channel_id=1, replica_groups=mesh['sensor'=8,'tx'=4,'ty'=4,'tz'=2] {'tz'}, dimensions={1}, use_global_device_ids=true | all-gather | bytes 12288 | tf_op jit(solution)/shard_map/all_gather | solution.py:80
  277.1 19.0 %all_gather.32 = f32[8,4096]{1,0:T(8,128)S(1)} all-gather(f32[8,256]{1,0:T(8,128)S(1)} %all_gather.31), channel_id=1, replica_groups=mesh['sensor'=8,'tx'=4,'ty'=4,'tz'=2] {'tx','ty'}, dimensions={1}, use_global_device_ids=true | all-gather | bytes 139264 | tf_op jit(solution)/shard_map/all_gather | solution.py:81
  296.2 0.6 fusion.40
  298.1 30.3 %all-gather.11.cloned.1.call-done = f32[512,4096]{0,1:T(8,128)} async-done(((f32[512,256]{0,1:T(8,128)}), f32[512,4096]{0,1:T(8,128)}) %all-gather.11.cloned.1.call-update) | async-done | bytes 8388624 | tf_op jit(solution)/shard_map/all_gather | solution.py:81
  328.4 0.0 copy-start.4
  328.4 15.6 %fusion.43 = f32[512,128]{1,0:T(8,128)S(1)} fusion(f32[512,4096]{0,1:T(8,128)} %all-gather.11.cloned.1.call-done, f32[128,4096]{1,0:T(8,128)S(1)} %copy-done), kind=kOutput, calls=%fused_computation.64 | convolution fusion | flops 3221225472 | bytes 10747904 | tf_op jit(solution)/shard_map/dot_general | solution.py:82
  344.0 0.5 fusion.16
  344.5 0.0 copy-done.4
  344.5 1.2 fusion.3
  345.7 0.7 multiply_reduce_fusion.1
  346.4 2.0 pad_maximum_fusion
  348.3 0.1 broadcast_in_dim.2
  348.4 24.4 %all_to_all.6 = f32[256,1,3]{2,1,0:T(1,128)S(1)} all-to-all(f32[256,1,3]{2,1,0:T(1,128)S(1)} %broadcast_in_dim.2), channel_id=1, replica_groups=mesh['sensor'=8,'tx'=4,'ty'=4,'tz'=2] {'sensor','tx','ty','tz'}, dimensions={0} | all-to-all | bytes 6144 | tf_op jit(solution)/shard_map/all_to_all | solution.py:26
  372.8 0.3 reduce_sum.119
  373.1 0.7 fusion.41
  377.6 0.6 multiply_subtract_fusion
  (6 shorter events, 0.1 us)
Async XLA Ops:
  7.2 11.4 %copy-start = (f32[128,4096]{1,0:T(8,128)S(1)}, f32[128,4096]{1,0:T(8,128)}, u32[]{:S(2)}) copy-start(f32[128,4096]{1,0:T(8,128)} %param.15) | copy-start | bytes 6291460
  7.2 57.1 %all-gather.5.cloned.1.call-start = ((), (), s32[]{:S(2)}) async-start(), calls=%async_computation.1 | async-start | bytes 2359296 | tf_op jit(solution)/shard_map/all_gather | solution.py:67
  10.5 5.5 %copy-start.7 = (s32[16]{0:T(128)S(1)}, s32[16]{0:T(128)}, u32[]{:S(2)}) copy-start(s32[16]{0:T(128)} %param.13) | copy-start | bytes 196
  13.7 4.9 %copy-start.1 = (f32[16,128,128]{2,1,0:T(8,128)S(1)}, f32[16,128,128]{2,1,0:T(8,128)}, u32[]{:S(2)}) copy-start(f32[16,128,128]{2,1,0:T(8,128)} %param.12) | copy-start | bytes 3145732
  13.7 5.9 %copy-start.5 = (f32[16,128]{1,0:T(8,128)S(1)}, f32[16,128]{1,0:T(8,128)}, u32[]{:S(2)}) copy-start(f32[16,128]{1,0:T(8,128)} %param.9) | copy-start | bytes 24580
  13.7 5.9 %copy-start.6 = (f32[16,128]{1,0:T(8,128)S(1)}, f32[16,128]{1,0:T(8,128)}, u32[]{:S(2)}) copy-start(f32[16,128]{1,0:T(8,128)} %param.10) | copy-start | bytes 24580
  16.0 3.7 copy-start.2
  23.2 144.0 %all-gather.7.cloned.1.call-start = ((), (), s32[]{:S(2)}) async-start(), calls=%async_computation.2 | async-start | bytes 8912896 | tf_op jit(solution)/shard_map/all_gather | solution.py:78
  91.4 133.8 %all-gather.9.cloned.1.call-start = ((), (), s32[]{:S(2)}) async-start(), calls=%async_computation.3 | async-start | bytes 2359296 | tf_op jit(solution)/shard_map/all_gather | solution.py:71
  167.2 16.1 %copy-start.3 = (f32[16,64,128]{2,1,0:T(8,128)S(1)}, f32[16,64,128]{2,1,0:T(8,128)}, u32[]{:S(2)}) copy-start(f32[16,64,128]{2,1,0:T(8,128)} %param.11) | copy-start | bytes 1572868
  187.9 140.5 %all-gather.11.cloned.1.call-start = ((), (), s32[]{:S(2)}) async-start(), calls=%async_computation.4 | async-start | bytes 8912896 | tf_op jit(solution)/shard_map/all_gather | solution.py:81
  328.4 16.1 %copy-start.4 = (f32[16,64,128]{2,1,0:T(8,128)S(1)}, f32[16,64,128]{2,1,0:T(8,128)}, u32[]{:S(2)}) copy-start(f32[16,64,128]{2,1,0:T(8,128)} %param.11) | copy-start | bytes 1572868
Sparse Core Ops, SparseCore 0:
  23.3 40.9 all-gather.4
  91.5 75.6 all-gather.6
  188.1 37.0 all-gather.8
  252.4 75.9 all-gather.10

commit v7 on v6

--- a/solution.py
+++ b/solution.py
@@ -37,11 +37,15 @@
     n_tm = time_kernel.shape[1] // time_dev
     window_ids = jnp.arange(win_count, dtype=jnp.int32)
     onehot = (window_index[:, None] == window_ids[None, :]).astype(jnp.float32)
-    own_square = lax.dynamic_slice_in_dim(
-        sensor_kernel, lax.axis_index("sensor") * sensor_dev, sensor_dev, 1
+    first_col = lax.axis_index("sensor") * sensor_dev
+    window_kernel = jnp.stack(
+        [
+            lax.dynamic_slice(
+                sensor_kernel, (w * win_rows, first_col + w * win_rows), (win_rows, win_rows)
+            )
+            for w in range(win_count)
+        ]
     )
-    own_square = own_square.reshape(win_count, win_rows, win_count, win_rows)
-    window_kernel = own_square[window_ids, :, window_ids, :]
     block_kernel = jnp.einsum("bw,wik->bik", onehot, window_kernel, precision=PRECISE)
     sensor_quad = jnp.sum(
         sensor_weights

time: 385 us -> 381 us (0.990)
  local copies, waits for them, and re-layouts: 11.6 us -> 5.88 us
    reshape x2 -> x0, local copies, waits for them, and re-layouts: 5.04 us -> none  [on_device(): own_square = own_square.reshape(win_count, win_rows, win_count, win_rows)]
where the time goes in v7:
time: 381 us
  waiting for transfers between devices  184 us (48%)
  blocking collectives  101 us (27%)
  matrix products  64.8 us (17%)
  between operations  19.2 us (5%)
  local copies, waits for them, and re-layouts  5.88 us (2%)
  other arithmetic  5.57 us (1%)
    all_gather x1, waiting for transfers between devices, operator_apply(): gathered = lax.all_gather(gathered, ('tx', 'ty'), axis=1, tiled=True)  75.6 us
    all_gather x1, waiting for transfers between devices, operator_apply(): full_field = lax.all_gather(grid_field, 'sensor', axis=0, tiled=True)  41 us
    all_gather x1, waiting for transfers between devices, operator_apply(): lax.all_gather((grid_field, pad), 'sensor', axis=0, tiled=True)  37.1 us
    dot_general x2, matrix products, operator_apply(): lax.dot_general(gathered, time_kernel, (((1,), (1,)), ((), ())), precisio...  31.2 us
    all_gather x1, waiting for transfers between devices, operator_apply(): lax.all_gather((gathered, pad), ('tx', 'ty'), axis=1, tiled=True)  30.3 us
    all_to_all x1, blocking collectives, all_device_sum(): rows = lax.all_to_all(copies, ALL, 0, 0, tiled=True)  24.4 us
    all_gather x2, blocking collectives, operator_apply(): lax.all_gather((left_product, pad), 'tz', axis=1, tiled=True)  24.3 us
    dot_general x2, matrix products, operator_apply(): jnp.dot(sensor_kernel, full_field, precision=PRECISE, preferred_element_t...  19.7 us
  transfers between devices with their start and end apart: 4, of which 4 were waited for; matrix products, arithmetic and copies ran while one was open for 1% of the time, Pallas kernels for 0%

profile of v7, /device:TPU:1, one launch (start us, length us, event | category | flops | bytes accessed | tf_op | source)
XLA Modules:
  0.0 380.7 jit_solution(4952242145544564473)
XLA Ops:
  7.2 0.0 copy-start
  7.2 0.0 copy-start.1
  7.2 0.0 copy-start.5
  7.2 0.0 copy-start.4
  7.2 0.0 all-gather.5.cloned.1.call-start
  7.3 1.8 constant_dynamic-slice_fusion.1
  9.1 1.2 stack.56
  10.2 1.1 fusion.27
  11.3 0.0 copy-start.6
  11.3 2.1 fusion.4
  13.4 0.0 copy-done
  13.4 0.0 copy-done.1
  13.4 1.0 fusion.1
  14.5 0.0 copy-done.5
  14.5 0.0 copy-done.4
  14.5 3.1 convolution_bitcast_fusion.2
  17.7 0.0 copy-done.6
  17.7 0.6 fusion.11
  18.3 0.8 copy.32
  19.0 0.0 all-gather.5.cloned.1.call-update
  19.1 0.0 all-gather.7.cloned.1.call-start
  19.1 41.0 %all-gather.5.cloned.1.call-done = f32[4096,128]{1,0:T(8,128)} async-done(((f32[512,128]{1,0:T(8,128)}), f32[4096,128]{1,0:T(8,128)}) %all-gather.5.cloned.1.call-update) | async-done | bytes 2097168 | tf_op jit(solution)/shard_map/all_gather | solution.py:71
  60.2 9.9 %convolution_bitcast_fusion.4 = f32[512,128]{0,1:T(8,128)S(1)} fusion(f32[4096,128]{1,0:T(8,128)} %all-gather.5.cloned.1.call-done, f32[512,4096]{1,0:T(8,128)} %param.14), kind=kOutput, calls=%fused_computation.12 | convolution fusion | flops 3221225472 | bytes 10747904 | tf_op jit(solution)/shard_map/dot_general | solution.py:77
  70.0 17.2 %all_gather.28 = f32[512,256]{0,1:T(8,128)} all-gather(f32[512,128]{0,1:T(8,128)S(1)} %convolution_bitcast_fusion.4), channel_id=1, replica_groups=mesh['sensor'=8,'tx'=4,'ty'=4,'tz'=2] {'tz'}, dimensions={1}, use_global_device_ids=true | all-gather | bytes 786432 | tf_op jit(solution)/shard_map/all_gather | solution.py:81
  87.2 0.0 all-gather.7.cloned.1.call-update
  87.3 0.2 all-gather.9.cloned.1.call-start
  87.5 75.6 %all-gather.7.cloned.1.call-done = f32[512,4096]{0,1:T(8,128)} async-done(((f32[512,256]{0,1:T(8,128)}), f32[512,4096]{0,1:T(8,128)}) %all-gather.7.cloned.1.call-update) | async-done | bytes 8388624 | tf_op jit(solution)/shard_map/all_gather | solution.py:82
  163.1 0.0 copy-start.2
  163.1 15.6 %fusion.41 = f32[512,128]{1,0:T(8,128)S(1)} fusion(f32[512,4096]{0,1:T(8,128)} %all-gather.7.cloned.1.call-done, f32[128,4096]{1,0:T(8,128)S(1)} %copy-done), kind=kOutput, calls=%fused_computation.67 | convolution fusion | flops 3221225472 | bytes 10747904 | tf_op jit(solution)/shard_map/dot_general | solution.py:86
  178.7 0.5 fusion.18
  179.1 0.0 copy-done.2
  179.1 1.2 fusion.2
  180.4 2.1 convolution_bitcast_fusion.1
  182.4 0.6 fusion.8
  183.0 0.8 copy.36
  183.8 0.0 all-gather.9.cloned.1.call-update
  183.8 0.0 all-gather.11.cloned.1.call-start
  183.9 37.1 %all-gather.9.cloned.1.call-done = f32[4096,128]{1,0:T(8,128)} async-done(((f32[512,128]{1,0:T(8,128)}), f32[4096,128]{1,0:T(8,128)}) %all-gather.9.cloned.1.call-update) | async-done | bytes 2097168 | tf_op jit(solution)/shard_map/all_gather | solution.py:75
  221.0 9.9 %convolution_bitcast_fusion.3 = f32[512,128]{0,1:T(8,128)S(1)} fusion(f32[4096,128]{1,0:T(8,128)} %all-gather.9.cloned.1.call-done, f32[512,4096]{1,0:T(8,128)} %param.14), kind=kOutput, calls=%fused_computation.11 | convolution fusion | flops 3221225472 | bytes 10747904 | tf_op jit(solution)/shard_map/dot_general | solution.py:77
  230.9 17.2 %all_gather.34 = f32[512,256]{0,1:T(8,128)} all-gather(f32[512,128]{0,1:T(8,128)S(1)} %convolution_bitcast_fusion.3), channel_id=1, replica_groups=mesh['sensor'=8,'tx'=4,'ty'=4,'tz'=2] {'tz'}, dimensions={1}, use_global_device_ids=true | all-gather | bytes 786432 | tf_op jit(solution)/shard_map/all_gather | solution.py:84
  248.1 0.0 all-gather.11.cloned.1.call-update
  248.1 0.6 multiply_reduce_fusion.3
  248.7 1.4 maximum_bitcast_fusion
  250.1 15.8 %all_gather.30 = f32[64,128]{1,0:T(8,128)S(1)} all-gather(f32[8,128]{1,0:T(8,128)S(1)} %scatter.4), channel_id=1, replica_groups=mesh['sensor'=8,'tx'=4,'ty'=4,'tz'=2] {'sensor'}, dimensions={0}, use_global_device_ids=true | all-gather | bytes 36864 | tf_op jit(solution)/shard_map/all_gather | solution.py:75
  265.9 7.1 %all_gather.31 = f32[8,256]{1,0:T(8,128)S(1)} all-gather(f32[8,128]{1,0:T(8,128)S(1)} %bitcast_reduce_fusion.1), channel_id=1, replica_groups=mesh['sensor'=8,'tx'=4,'ty'=4,'tz'=2] {'tz'}, dimensions={1}, use_global_device_ids=true | all-gather | bytes 12288 | tf_op jit(solution)/shard_map/all_gather | solution.py:84
  273.0 19.0 %all_gather.32 = f32[8,4096]{1,0:T(8,128)S(1)} all-gather(f32[8,256]{1,0:T(8,128)S(1)} %all_gather.31), channel_id=1, replica_groups=mesh['sensor'=8,'tx'=4,'ty'=4,'tz'=2] {'tx','ty'}, dimensions={1}, use_global_device_ids=true | all-gather | bytes 139264 | tf_op jit(solution)/shard_map/all_gather | solution.py:85
  292.1 0.6 fusion.39
  294.0 30.3 %all-gather.11.cloned.1.call-done = f32[512,4096]{0,1:T(8,128)} async-done(((f32[512,256]{0,1:T(8,128)}), f32[512,4096]{0,1:T(8,128)}) %all-gather.11.cloned.1.call-update) | async-done | bytes 8388624 | tf_op jit(solution)/shard_map/all_gather | solution.py:85
  324.3 0.0 copy-start.3
  324.3 15.6 %fusion.42 = f32[512,128]{1,0:T(8,128)S(1)} fusion(f32[512,4096]{0,1:T(8,128)} %all-gather.11.cloned.1.call-done, f32[128,4096]{1,0:T(8,128)S(1)} %copy-done), kind=kOutput, calls=%fused_computation.68 | convolution fusion | flops 3221225472 | bytes 10747904 | tf_op jit(solution)/shard_map/dot_general | solution.py:86
  339.9 0.5 fusion.16
  340.4 0.0 copy-done.3
  340.4 1.2 fusion.3
  341.6 0.7 multiply_reduce_fusion.1
  342.2 2.0 pad_maximum_fusion
  344.2 0.1 broadcast_in_dim.2
  344.3 24.4 %all_to_all.6 = f32[256,1,3]{2,1,0:T(1,128)S(1)} all-to-all(f32[256,1,3]{2,1,0:T(1,128)S(1)} %broadcast_in_dim.2), channel_id=1, replica_groups=mesh['sensor'=8,'tx'=4,'ty'=4,'tz'=2] {'sensor','tx','ty','tz'}, dimensions={0} | all-to-all | bytes 6144 | tf_op jit(solution)/shard_map/all_to_all | solution.py:26
  368.7 0.3 reduce_sum.119
  369.0 0.7 fusion.40
  373.5 0.6 multiply_subtract_fusion
  (5 shorter events, 0.1 us)
Async XLA Ops:
  7.2 6.3 %copy-start = (f32[128,4096]{1,0:T(8,128)S(1)}, f32[128,4096]{1,0:T(8,128)}, u32[]{:S(2)}) copy-start(f32[128,4096]{1,0:T(8,128)} %param.15) | copy-start | bytes 6291460
  7.2 6.3 %copy-start.1 = (f32[16,128,128]{2,1,0:T(8,128)S(1)}, f32[16,128,128]{2,1,0:T(8,128)}, u32[]{:S(2)}) copy-start(f32[16,128,128]{2,1,0:T(8,128)} %param.12) | copy-start | bytes 3145732
  7.2 7.3 %copy-start.5 = (f32[16,128]{1,0:T(8,128)S(1)}, f32[16,128]{1,0:T(8,128)}, u32[]{:S(2)}) copy-start(f32[16,128]{1,0:T(8,128)} %param.10) | copy-start | bytes 24580
  7.2 7.3 %copy-start.4 = (f32[16,128]{1,0:T(8,128)S(1)}, f32[16,128]{1,0:T(8,128)}, u32[]{:S(2)}) copy-start(f32[16,128]{1,0:T(8,128)} %param.9) | copy-start | bytes 24580
  7.2 53.0 %all-gather.5.cloned.1.call-start = ((), (), s32[]{:S(2)}) async-start(), calls=%async_computation.1 | async-start | bytes 2359296 | tf_op jit(solution)/shard_map/all_gather | solution.py:71
  11.3 6.3 %copy-start.6 = (s32[16]{0:T(128)S(1)}, s32[16]{0:T(128)}, u32[]{:S(2)}) copy-start(s32[16]{0:T(128)} %param.13) | copy-start | bytes 196
  19.1 144.0 %all-gather.7.cloned.1.call-start = ((), (), s32[]{:S(2)}) async-start(), calls=%async_computation.2 | async-start | bytes 8912896 | tf_op jit(solution)/shard_map/all_gather | solution.py:82
  87.3 133.8 %all-gather.9.cloned.1.call-start = ((), (), s32[]{:S(2)}) async-start(), calls=%async_computation.3 | async-start | bytes 2359296 | tf_op jit(solution)/shard_map/all_gather | solution.py:75
  163.1 16.1 %copy-start.2 = (f32[16,64,128]{2,1,0:T(8,128)S(1)}, f32[16,64,128]{2,1,0:T(8,128)}, u32[]{:S(2)}) copy-start(f32[16,64,128]{2,1,0:T(8,128)} %param.11) | copy-start | bytes 1572868
  183.8 140.5 %all-gather.11.cloned.1.call-start = ((), (), s32[]{:S(2)}) async-start(), calls=%async_computation.4 | async-start | bytes 8912896 | tf_op jit(solution)/shard_map/all_gather | solution.py:85
  324.3 16.1 %copy-start.3 = (f32[16,64,128]{2,1,0:T(8,128)S(1)}, f32[16,64,128]{2,1,0:T(8,128)}, u32[]{:S(2)}) copy-start(f32[16,64,128]{2,1,0:T(8,128)} %param.11) | copy-start | bytes 1572868
Sparse Core Ops, SparseCore 0:
  19.2 40.9 all-gather.4
  87.4 75.6 all-gather.6
  184.0 37.0 all-gather.8
  248.3 75.9 all-gather.10

commit v8 on v7

--- a/solution.py
+++ b/solution.py
@@ -74,14 +74,27 @@
             pad = pad.at[0, : payload.shape[0]].set(payload)
             full_field, pads = lax.all_gather((grid_field, pad), "sensor", axis=0, tiled=True)
             pad = jnp.sum(pads.reshape(-1, PAY_ROWS, time_dev), axis=0)
-        left_product = jnp.dot(
-            sensor_kernel, full_field, precision=PRECISE, preferred_element_type=jnp.float32
+        half = sensor_dev // 2
+        swap = [(0, 1), (1, 0)]
+        own_parts, other_parts = [], []
+        for rows in (slice(0, half), slice(half, sensor_dev)):
+            part = jnp.dot(
+                sensor_kernel[rows], full_field, precision=PRECISE,
+                preferred_element_type=jnp.float32,
+            )
+            own_parts.append(part)
+            other_parts.append(lax.ppermute(part, "tz", swap))
+        own = jnp.concatenate(own_parts, axis=0)
+        other = jnp.concatenate(other_parts, axis=0)
+        gathered = jnp.where(
+            lax.axis_index("tz") == 0,
+            jnp.concatenate([own, other], axis=1),
+            jnp.concatenate([other, own], axis=1),
         )
         if payload is None:
-            gathered = lax.all_gather(left_product, "tz", axis=1, tiled=True)
             gathered = lax.all_gather(gathered, ("tx", "ty"), axis=1, tiled=True)
         else:
-            gathered, pad = lax.all_gather((left_product, pad), "tz", axis=1, tiled=True)
+            pad = lax.all_gather(pad, "tz", axis=1, tiled=True)
             gathered, pad = lax.all_gather((gathered, pad), ("tx", "ty"), axis=1, tiled=True)
         smooth = lax.dot_general(
             gathered,

time: 381 us -> 391 us (1.026); the launches traced: 381 us -> 384 us
  blocking collectives: 101 us -> 67.9 us
  waiting for transfers between devices: 184 us -> 199 us
  starting transfers between devices: 0.35 us -> 11.6 us
  matrix products: 64.8 us -> 71 us
    all_gather x3 -> x1, blocking collectives: 41.5 us -> 7.11 us  [operator_apply(): pad = lax.all_gather(pad, 'tz', axis=1, tiled=True)]
    ppermute x0 -> x4, waiting for transfers between devices: none -> 15.2 us  [operator_apply(): other_parts.append(lax.ppermute(part, 'tz', swap))]
    ppermute x0 -> x4, starting transfers between devices: none -> 11.3 us  [operator_apply(): other_parts.append(lax.ppermute(part, 'tz', swap))]
    dot_general x2 -> x4, matrix products: 19.7 us -> 24.4 us  [operator_apply(): jnp.dot(sensor_kernel[rows], full_field, precision=PRECISE, preferred_ele...]
  transfers between devices with their start and end apart: 4 -> 8, of which waited for: 4 -> 6; matrix products, arithmetic and copies ran while one was open for 1% -> 4% of each run, Pallas kernels for 0% -> 0%
where the time goes in v8:
time: 391 us; the launch traced here: 384 us
  waiting for transfers between devices  199 us (51%)
  matrix products  71 us (18%)
  blocking collectives  67.9 us (17%)
  between operations  19.7 us (5%)
  starting transfers between devices  11.6 us (3%)
  other arithmetic  8.11 us (2%)
  local copies, waits for them, and re-layouts  6.89 us (2%)
    all_gather x1, waiting for transfers between devices, operator_apply(): gathered = lax.all_gather(gathered, ('tx', 'ty'), axis=1, tiled=True)  76.2 us
    all_gather x1, waiting for transfers between devices, operator_apply(): full_field = lax.all_gather(grid_field, 'sensor', axis=0, tiled=True)  41 us
    all_gather x1, waiting for transfers between devices, operator_apply(): lax.all_gather((grid_field, pad), 'sensor', axis=0, tiled=True)  36.9 us
    dot_general x2, matrix products, operator_apply(): lax.dot_general(gathered, time_kernel, (((1,), (1,)), ((), ())), precisio...  31.2 us
    all_gather x1, waiting for transfers between devices, operator_apply(): lax.all_gather((gathered, pad), ('tx', 'ty'), axis=1, tiled=True)  29.2 us
    dot_general x4, matrix products, operator_apply(): jnp.dot(sensor_kernel[rows], full_field, precision=PRECISE, preferred_ele...  24.4 us
    all_to_all x1, blocking collectives, all_device_sum(): rows = lax.all_to_all(copies, ALL, 0, 0, tiled=True)  24.3 us
    all_gather x1, blocking collectives, operator_apply(): lax.all_gather((gathered, pad), ('tx', 'ty'), axis=1, tiled=True)  19.6 us
  transfers between devices with their start and end apart: 8, of which 6 were waited for; matrix products, arithmetic and copies ran while one was open for 4% of the time, Pallas kernels for 0%

profile of v8, /device:TPU:1, one launch (start us, length us, event | category | flops | bytes accessed | tf_op | source)
XLA Modules:
  0.0 383.8 jit_solution(15829564000689351036)
XLA Ops:
  7.2 0.0 copy-start
  7.2 0.0 copy-start.8
  7.2 0.0 copy-start.1
  7.2 0.0 all-gather.5.cloned.1.call-start
  7.3 1.8 constant_dynamic-slice_fusion.1
  9.1 1.2 stack.56
  10.3 1.1 fusion.47
  11.4 2.1 fusion.12
  13.5 2.6 fusion.9
  16.1 0.7 fusion.58
  16.8 3.1 convolution_bitcast_fusion.2
  19.9 0.6 fusion.31
  20.5 0.8 copy.32
  21.3 0.0 all-gather.5.cloned.1.call-update
  21.3 0.0 all-gather.7.cloned.1.call-start
  21.4 41.0 %all-gather.5.cloned.1.call-done = f32[4096,128]{1,0:T(8,128)} async-done(((f32[512,128]{1,0:T(8,128)}), f32[4096,128]{1,0:T(8,128)}) %all-gather.5.cloned.1.call-update) | async-done | bytes 2097168 | tf_op jit(solution)/shard_map/all_gather | solution.py:71
  62.4 6.4 %fusion.13 = f32[256,128]{0,1:T(8,128)S(1)} fusion(f32[4096,128]{1,0:T(8,128)} %all-gather.5.cloned.1.call-done, f32[512,4096]{1,0:T(8,128)} %param.14), kind=kOutput, calls=%fused_computation.19 | convolution fusion | flops 1610612736 | bytes 6422528 | tf_op jit(solution)/shard_map/dot_general | solution.py:81
  68.8 4.1 %collective-permute-start = (f32[256,128]{0,1:T(8,128)S(1)}, f32[256,128]{0,1:T(8,128)S(1)}, u32[]{:S(2)}, u32[]{:S(2)}) collective-permute-start(f32[256,128]{0,1:T(8,128)S(1)} %fusion.13), channel_id=1, source_target_pairs={{0,1},{1,0},{2,3},{3,2},{4,5},{5,4},{6,7},{7,6},{8,9},{9,8},{10,11... | collective-permute-start | bytes 393224 | tf_op jit(solution)/shard_map/ppermute | solution.py:86
  72.9 5.8 %fusion.19 = f32[256,128]{0,1:T(8,128)S(1)} fusion(f32[4096,128]{1,0:T(8,128)S(1)} %copy-done.4, f32[512,4096]{1,0:T(8,128)} %param.14), kind=kOutput, calls=%fused_computation.21 | convolution fusion | flops 1610612736 | bytes 6422528 | tf_op jit(solution)/shard_map/dot_general | solution.py:81
  78.7 1.6 collective-permute-start.1
  80.4 0.0 collective-permute-done
  80.4 7.6 %collective-permute-done.1 = f32[256,128]{0,1:T(8,128)} collective-permute-done((f32[256,128]{0,1:T(8,128)S(1)}, f32[256,128]{0,1:T(8,128)}, u32[]{:S(2)}, u32[]{:S(2)}) %collective-permute-start.1) | collective-permute-done | bytes 131104 | tf_op jit(solution)/shard_map/ppermute | solution.py:86
  88.0 0.9 constant_dynamic-update-slice_fusion
  88.9 0.9 maximum_select_fusion
  89.8 0.0 all-gather.7.cloned.1.call-update
  89.9 0.0 copy-start.9
  89.9 0.0 copy-start.7
  89.9 0.0 all-gather.9.cloned.1.call-start
  89.9 76.2 %all-gather.7.cloned.1.call-done = f32[512,4096]{0,1:T(8,128)} async-done(((f32[512,256]{0,1:T(8,128)}), f32[512,4096]{0,1:T(8,128)}) %all-gather.7.cloned.1.call-update) | async-done | bytes 8388624 | tf_op jit(solution)/shard_map/all_gather | solution.py:95
  166.1 15.6 %fusion.61 = f32[512,128]{1,0:T(8,128)S(1)} fusion(f32[512,4096]{0,1:T(8,128)} %all-gather.7.cloned.1.call-done, f32[128,4096]{1,0:T(8,128)S(1)} %copy-done), kind=kOutput, calls=%fused_computation.83 | convolution fusion | flops 3221225472 | bytes 10747904 | tf_op jit(solution)/shard_map/dot_general | solution.py:99
  181.7 0.5 fusion.38
  182.2 1.2 fusion.10
  183.4 2.1 convolution_bitcast_fusion.1
  185.5 0.6 fusion.28
  186.1 0.8 copy.36
  186.9 0.0 all-gather.9.cloned.1.call-update
  186.9 0.3 all-gather.11.cloned.1.call-start
  187.1 36.9 %all-gather.9.cloned.1.call-done = f32[4096,128]{1,0:T(8,128)} async-done(((f32[512,128]{1,0:T(8,128)}), f32[4096,128]{1,0:T(8,128)}) %all-gather.9.cloned.1.call-update) | async-done | bytes 2097168 | tf_op jit(solution)/shard_map/all_gather | solution.py:75
  224.1 6.4 %fusion.16 = f32[256,128]{0,1:T(8,128)S(1)} fusion(f32[4096,128]{1,0:T(8,128)} %all-gather.9.cloned.1.call-done, f32[512,4096]{1,0:T(8,128)} %param.14), kind=kOutput, calls=%fused_computation.20 | convolution fusion | flops 1610612736 | bytes 6422528 | tf_op jit(solution)/shard_map/dot_general | solution.py:81
  230.5 0.0 copy-start.6
  230.5 3.9 %collective-permute-start.2 = (f32[256,128]{0,1:T(8,128)S(1)}, f32[256,128]{0,1:T(8,128)S(1)}, u32[]{:S(2)}, u32[]{:S(2)}) collective-permute-start(f32[256,128]{0,1:T(8,128)S(1)} %fusion.16), channel_id=1, source_target_pairs={{0,1},{1,0},{2,3},{3,2},{4,5},{5,4},{6,7},{7,6},{8,9},{9,8},{10,11... | collective-permute-start | bytes 393224 | tf_op jit(solution)/shard_map/ppermute | solution.py:86
  234.4 5.8 %fusion.22 = f32[256,128]{0,1:T(8,128)S(1)} fusion(f32[4096,128]{1,0:T(8,128)S(1)} %copy-done.5, f32[512,4096]{1,0:T(8,128)} %param.14), kind=kOutput, calls=%fused_computation.22 | convolution fusion | flops 1610612736 | bytes 6422528 | tf_op jit(solution)/shard_map/dot_general | solution.py:81
  240.2 1.6 collective-permute-start.3
  241.9 0.0 collective-permute-done.2
  241.9 7.5 %collective-permute-done.3 = f32[256,128]{0,1:T(8,128)S(1)} collective-permute-done((f32[256,128]{0,1:T(8,128)S(1)}, f32[256,128]{0,1:T(8,128)S(1)}, u32[]{:S(2)}, u32[]{:S(2)}) %collective-permute-start.3) | collective-permute-done | bytes 131104 | tf_op jit(solution)/shard_map/ppermute | solution.py:86
  249.4 0.9 maximum_select_fusion.1
  250.4 0.0 all-gather.11.cloned.1.call-update
  250.4 0.6 multiply_reduce_fusion.3
  251.0 1.4 maximum_bitcast_fusion
  252.4 16.9 %all_gather.23 = f32[64,128]{1,0:T(8,128)S(1)} all-gather(f32[8,128]{1,0:T(8,128)S(1)} %scatter.4), channel_id=1, replica_groups=mesh['sensor'=8,'tx'=4,'ty'=4,'tz'=2] {'sensor'}, dimensions={0}, use_global_device_ids=true | all-gather | bytes 36864 | tf_op jit(solution)/shard_map/all_gather | solution.py:75
  269.2 7.1 %all_gather.24 = f32[8,256]{1,0:T(8,128)S(1)} all-gather(f32[8,128]{1,0:T(8,128)S(1)} %bitcast_reduce_fusion.1), channel_id=1, replica_groups=mesh['sensor'=8,'tx'=4,'ty'=4,'tz'=2] {'tz'}, dimensions={1}, use_global_device_ids=true | all-gather | bytes 12288 | tf_op jit(solution)/shard_map/all_gather | solution.py:97
  276.3 19.6 %all_gather.25 = f32[8,4096]{1,0:T(8,128)S(1)} all-gather(f32[8,256]{1,0:T(8,128)S(1)} %all_gather.24), channel_id=1, replica_groups=mesh['sensor'=8,'tx'=4,'ty'=4,'tz'=2] {'tx','ty'}, dimensions={1}, use_global_device_ids=true | all-gather | bytes 139264 | tf_op jit(solution)/shard_map/all_gather | solution.py:98
  295.9 0.6 fusion.59
  297.9 29.2 %all-gather.11.cloned.1.call-done = f32[512,4096]{0,1:T(8,128)} async-done(((f32[512,256]{0,1:T(8,128)}), f32[512,4096]{0,1:T(8,128)}) %all-gather.11.cloned.1.call-update) | async-done | bytes 8388624 | tf_op jit(solution)/shard_map/all_gather | solution.py:98
  327.0 15.6 %fusion.62 = f32[512,128]{1,0:T(8,128)S(1)} fusion(f32[512,4096]{0,1:T(8,128)} %all-gather.11.cloned.1.call-done, f32[128,4096]{1,0:T(8,128)S(1)} %copy-done), kind=kOutput, calls=%fused_computation.84 | convolution fusion | flops 3221225472 | bytes 10747904 | tf_op jit(solution)/shard_map/dot_general | solution.py:99
  342.6 0.5 fusion.36
  343.1 1.2 fusion.11
  344.3 0.7 multiply_reduce_fusion.1
  345.0 2.0 pad_maximum_fusion
  346.9 0.1 broadcast_in_dim.2
  347.0 24.3 %all_to_all.6 = f32[256,1,3]{2,1,0:T(1,128)S(1)} all-to-all(f32[256,1,3]{2,1,0:T(1,128)S(1)} %broadcast_in_dim.2), channel_id=1, replica_groups=mesh['sensor'=8,'tx'=4,'ty'=4,'tz'=2] {'sensor','tx','ty','tz'}, dimensions={0} | all-to-all | bytes 6144 | tf_op jit(solution)/shard_map/all_to_all | solution.py:26
  371.4 0.3 reduce_sum.119
  371.7 0.7 fusion.60
  376.2 0.6 multiply_subtract_fusion
  (21 shorter events, 0.1 us)
Async XLA Ops:
  7.2 6.3 %copy-start = (f32[128,4096]{1,0:T(8,128)S(1)}, f32[128,4096]{1,0:T(8,128)}, u32[]{:S(2)}) copy-start(f32[128,4096]{1,0:T(8,128)} %param.15) | copy-start | bytes 6291460
  7.2 12.7 %copy-start.8 = (s32[16]{0:T(128)S(1)}, s32[16]{0:T(128)}, u32[]{:S(2)}) copy-start(s32[16]{0:T(128)} %param.13) | copy-start | bytes 196
  7.2 9.6 %copy-start.1 = (f32[16,128,128]{2,1,0:T(8,128)S(1)}, f32[16,128,128]{2,1,0:T(8,128)}, u32[]{:S(2)}) copy-start(f32[16,128,128]{2,1,0:T(8,128)} %param.12) | copy-start | bytes 3145732
  7.2 55.2 %all-gather.5.cloned.1.call-start = ((), (), s32[]{:S(2)}) async-start(), calls=%async_computation.1 | async-start | bytes 2359296 | tf_op jit(solution)/shard_map/all_gather | solution.py:71
  21.3 144.8 %all-gather.7.cloned.1.call-start = ((), (), s32[]{:S(2)}) async-start(), calls=%async_computation.2 | async-start | bytes 8912896 | tf_op jit(solution)/shard_map/all_gather | solution.py:95
  62.4 10.5 %copy-start.4 = (f32[4096,128]{1,0:T(8,128)S(1)}, f32[4096,128]{1,0:T(8,128)}, u32[]{:S(2)}) copy-start(f32[4096,128]{1,0:T(8,128)} %all-gather.5.cloned.1.call-done) | copy-start | bytes 6291460
  68.8 11.5 %collective-permute-start = (f32[256,128]{0,1:T(8,128)S(1)}, f32[256,128]{0,1:T(8,128)S(1)}, u32[]{:S(2)}, u32[]{:S(2)}) collective-permute-start(f32[256,128]{0,1:T(8,128)S(1)} %fusion.13), channel_id=1, source_target_pairs={{0,1},{1,0},{2,3},{3,2},{4,5},{5,4},{6,7},{7,6},{8,9},{9,8},{10,11... | collective-permute-start | bytes 393224 | tf_op jit(solution)/shard_map/ppermute | solution.py:86
  78.7 9.3 %collective-permute-start.1 = (f32[256,128]{0,1:T(8,128)S(1)}, f32[256,128]{0,1:T(8,128)}, u32[]{:S(2)}, u32[]{:S(2)}) collective-permute-start(f32[256,128]{0,1:T(8,128)S(1)} %fusion.19), channel_id=1, source_target_pairs={{0,1},{1,0},{2,3},{3,2},{4,5},{5,4},{6,7},{7,6},{8,9},{9,8},{10,11... | collective-permute-start | bytes 393224 | tf_op jit(solution)/shard_map/ppermute | solution.py:86
  89.9 91.8 %copy-start.9 = (s32[16]{0:T(128)S(1)}, s32[16]{0:T(128)}, u32[]{:S(2)}) copy-start(s32[16]{0:T(128)} %param.13) | copy-start | bytes 196
  89.9 93.5 %copy-start.7 = (f32[16,128]{1,0:T(8,128)S(1)}, f32[16,128]{1,0:T(8,128)}, u32[]{:S(2)}) copy-start(f32[16,128]{1,0:T(8,128)} %param.10) | copy-start | bytes 24580
  89.9 134.2 %all-gather.9.cloned.1.call-start = ((), (), s32[]{:S(2)}) async-start(), calls=%async_computation.3 | async-start | bytes 2359296 | tf_op jit(solution)/shard_map/all_gather | solution.py:75
  166.1 16.1 %copy-start.2 = (f32[16,64,128]{2,1,0:T(8,128)S(1)}, f32[16,64,128]{2,1,0:T(8,128)}, u32[]{:S(2)}) copy-start(f32[16,64,128]{2,1,0:T(8,128)} %param.11) | copy-start | bytes 1572868
  186.9 140.2 %all-gather.11.cloned.1.call-start = ((), (), s32[]{:S(2)}) async-start(), calls=%async_computation.4 | async-start | bytes 8912896 | tf_op jit(solution)/shard_map/all_gather | solution.py:98
  224.1 10.4 %copy-start.5 = (f32[4096,128]{1,0:T(8,128)S(1)}, f32[4096,128]{1,0:T(8,128)}, u32[]{:S(2)}) copy-start(f32[4096,128]{1,0:T(8,128)} %all-gather.9.cloned.1.call-done) | copy-start | bytes 6291460
  230.5 19.9 %copy-start.6 = (f32[16,128]{1,0:T(8,128)S(1)}, f32[16,128]{1,0:T(8,128)}, u32[]{:S(2)}) copy-start(f32[16,128]{1,0:T(8,128)} %param.9) | copy-start | bytes 24580
  230.5 11.4 %collective-permute-start.2 = (f32[256,128]{0,1:T(8,128)S(1)}, f32[256,128]{0,1:T(8,128)S(1)}, u32[]{:S(2)}, u32[]{:S(2)}) collective-permute-start(f32[256,128]{0,1:T(8,128)S(1)} %fusion.16), channel_id=1, source_target_pairs={{0,1},{1,0},{2,3},{3,2},{4,5},{5,4},{6,7},{7,6},{8,9},{9,8},{10,11... | collective-permute-start | bytes 393224 | tf_op jit(solution)/shard_map/ppermute | solution.py:86
  240.2 9.2 %collective-permute-start.3 = (f32[256,128]{0,1:T(8,128)S(1)}, f32[256,128]{0,1:T(8,128)S(1)}, u32[]{:S(2)}, u32[]{:S(2)}) collective-permute-start(f32[256,128]{0,1:T(8,128)S(1)} %fusion.22), channel_id=1, source_target_pairs={{0,1},{1,0},{2,3},{3,2},{4,5},{5,4},{6,7},{7,6},{8,9},{9,8},{10,11... | collective-permute-start | bytes 393224 | tf_op jit(solution)/shard_map/ppermute | solution.py:86
  327.0 16.1 %copy-start.3 = (f32[16,64,128]{2,1,0:T(8,128)S(1)}, f32[16,64,128]{2,1,0:T(8,128)}, u32[]{:S(2)}) copy-start(f32[16,64,128]{2,1,0:T(8,128)} %param.11) | copy-start | bytes 1572868
Sparse Core Ops, SparseCore 0:
  21.4 40.9 all-gather.4
  90.0 76.0 all-gather.6
  187.0 37.0 all-gather.8
  250.5 76.4 all-gather.10

commit v9 on v7

--- a/solution.py
+++ b/solution.py
@@ -8,6 +8,7 @@
 PAY_ROWS = 8
 TM = ("tx", "ty", "tz")
 ALL = ("sensor",) + TM
+Z_SWAP = [(0, 1), (1, 0)]
 
 
 def tm_index():
@@ -61,6 +62,14 @@
     )
     inverse = 1.0 / (sensor_quad * time_quad + noise_var)
 
+    n_tx, n_ty, n_tz = lax.axis_size("tx"), lax.axis_size("ty"), lax.axis_size("tz")
+    z_now = lax.axis_index("tz")
+    by_half = time_kernel.reshape(time_dev, n_tx, n_ty, n_tz, time_dev)
+    own_cols = lax.dynamic_index_in_dim(by_half, z_now, axis=3, keepdims=False)
+    own_cols = own_cols.reshape(time_dev, -1)
+    other_cols = lax.dynamic_index_in_dim(by_half, 1 - z_now, axis=3, keepdims=False)
+    partner_cols = lax.ppermute(other_cols.reshape(time_dev, -1), "tz", Z_SWAP)
+
     def operator_apply(vector, payload=None):
         scaled = vector[:, None, :] * time_weights
         contrib = jnp.einsum("bir,bjr->bij", sensor_weights, scaled, precision=PRECISE)
@@ -78,17 +87,21 @@
             sensor_kernel, full_field, precision=PRECISE, preferred_element_type=jnp.float32
         )
         if payload is None:
-            gathered = lax.all_gather(left_product, "tz", axis=1, tiled=True)
-            gathered = lax.all_gather(gathered, ("tx", "ty"), axis=1, tiled=True)
+            half_rows = lax.all_gather(left_product, ("tx", "ty"), axis=1, tiled=True)
         else:
-            gathered, pad = lax.all_gather((left_product, pad), "tz", axis=1, tiled=True)
-            gathered, pad = lax.all_gather((gathered, pad), ("tx", "ty"), axis=1, tiled=True)
-        smooth = lax.dot_general(
-            gathered,
-            time_kernel,
-            (((1,), (1,)), ((), ())),
-            precision=PRECISE,
-            preferred_element_type=jnp.float32,
+            half_rows, pad = lax.all_gather((left_product, pad), ("tx", "ty"), axis=1, tiled=True)
+            pad = jnp.sum(pad.reshape(PAY_ROWS, -1, time_dev), axis=1)
+        for_partner = jnp.dot(
+            half_rows, partner_cols.T, precision=PRECISE, preferred_element_type=jnp.float32
+        )
+        if payload is None:
+            from_partner = lax.ppermute(for_partner, "tz", Z_SWAP)
+        else:
+            from_partner, pad_partner = lax.ppermute((for_partner, pad), "tz", Z_SWAP)
+            pad = pad + pad_partner
+        smooth = (
+            jnp.dot(half_rows, own_cols.T, precision=PRECISE, preferred_element_type=jnp.float32)
+            + from_partner
         )
         field_rows = jnp.einsum(
             "bw,wij->bij", onehot, smooth.reshape(win_count, win_rows, time_dev), precision=PRECISE
@@ -97,7 +110,7 @@
         image = jnp.sum(sensor_weights * interp_cols, axis=1) + noise_var * vector
         if payload is None:
             return image, None
-        totals = jnp.sum(pad.reshape(PAY_ROWS, n_tm, time_dev), axis=1)[0, : payload.shape[0]]
+        totals = pad[0, : payload.shape[0]]
         return image, totals
 
     residual0 = readings

time: 381 us -> 345 us (0.906); the launches traced: 381 us -> 341 us
  waiting for transfers between devices: 184 us -> 139 us
  blocking collectives: 101 us -> 63.9 us
  starting transfers between devices: 0.35 us -> 17.8 us
  local copies, waits for them, and re-layouts: 5.88 us -> 21.3 us
  matrix products: 64.8 us -> 72.7 us
    all_gather x2, waiting for transfers between devices: 106 us -> 12.4 us  [the longest x1 12.4 us: operator_apply(): lax.all_gather((left_product, pad), ('tx', 'ty'), axis=1, tiled=True)]
    ppermute x0 -> x4, waiting for transfers between devices: none -> 49.6 us  [the longest x1 45.2 us: on_device(): partner_cols = lax.ppermute(other_cols.reshape(time_dev, -1), 'tz', Z_SWAP)]
    all_gather x4 -> x1, blocking collectives: 60.5 us -> 18.4 us  [operator_apply(): lax.all_gather((left_product, pad), ('tx', 'ty'), axis=1, tiled=True)]
    ppermute x0 -> x4, starting transfers between devices: none -> 16.6 us  [the longest x2 9.67 us: operator_apply(): from_partner, pad_partner = lax.ppermute((for_partner, pad), 'tz', Z_SWAP)]
    dynamic_slice x0 -> x1, local copies, waits for them, and re-layouts: none -> 9.76 us  [on_device(): lax.dynamic_index_in_dim(by_half, 1 - z_now, axis=3, keepdims=False)]
    dot_general x2, matrix products: 19.7 us -> 27 us  [operator_apply(): jnp.dot(sensor_kernel, full_field, precision=PRECISE, preferred_element_t...]
    reshape x0 -> x3, local copies, waits for them, and re-layouts: none -> 7.14 us  [the longest x1 4.03 us: on_device(): by_half = time_kernel.reshape(time_dev, n_tx, n_ty, n_tz, time_dev)]
    all_to_all x1, blocking collectives: 24.4 us -> 29.3 us  [all_device_sum(): rows = lax.all_to_all(copies, ALL, 0, 0, tiled=True)]
  transfers between devices with their start and end apart: 4 -> 8, of which waited for: 4 -> 7; matrix products, arithmetic and copies ran while one was open for 1% -> 10% of each run, Pallas kernels for 0% -> 0%
where the time goes in v9:
time: 345 us; the launch traced here: 341 us
  waiting for transfers between devices  139 us (40%)
  matrix products  72.7 us (21%)
  blocking collectives  63.9 us (19%)
  local copies, waits for them, and re-layouts  21.3 us (6%)
  between operations  19.4 us (6%)
  starting transfers between devices  17.8 us (5%)
  other arithmetic  6.33 us (2%)
    ppermute x1, waiting for transfers between devices, on_device(): partner_cols = lax.ppermute(other_cols.reshape(time_dev, -1), 'tz', Z_SWAP)  45.2 us
    all_gather x1, waiting for transfers between devices, operator_apply(): full_field = lax.all_gather(grid_field, 'sensor', axis=0, tiled=True)  40.6 us
    all_gather x1, waiting for transfers between devices, operator_apply(): lax.all_gather((grid_field, pad), 'sensor', axis=0, tiled=True)  36.6 us
    all_to_all x1, blocking collectives, all_device_sum(): rows = lax.all_to_all(copies, ALL, 0, 0, tiled=True)  29.3 us
    dot_general x2, matrix products, operator_apply(): jnp.dot(sensor_kernel, full_field, precision=PRECISE, preferred_element_t...  27 us
    all_gather x1, blocking collectives, operator_apply(): lax.all_gather((left_product, pad), ('tx', 'ty'), axis=1, tiled=True)  18.4 us
    dot_general x2, matrix products, operator_apply(): jnp.dot(half_rows, partner_cols.T, precision=PRECISE, preferred_element_t...  17.7 us
    all_gather x1, blocking collectives, operator_apply(): lax.all_gather((grid_field, pad), 'sensor', axis=0, tiled=True)  16.2 us
  transfers between devices with their start and end apart: 8, of which 7 were waited for; matrix products, arithmetic and copies ran while one was open for 10% of the time, Pallas kernels for 0%

profile of v9, /device:TPU:1, one launch (start us, length us, event | category | flops | bytes accessed | tf_op | source)
XLA Modules:
  0.0 340.7 jit_solution(7534127232706876911)
XLA Ops:
  7.2 0.0 copy-start.6
  7.2 0.0 copy-start.3
  7.2 0.0 copy-start
  7.2 0.0 all-gather.5.cloned.1.call-start
  7.3 1.1 constant_dynamic-slice_fusion.1
  8.4 0.4 stack.56
  8.8 1.1 fusion.27
  9.9 2.1 fusion.4
  12.0 2.6 fusion.1
  14.5 0.7 fusion.38
  15.3 2.1 convolution_bitcast_fusion.2
  17.4 0.6 fusion.11
  18.0 0.8 copy.32
  18.8 0.0 all-gather.5.cloned.1.call-update
  18.8 0.5 all-gather.7.cloned.1.call-start
  19.3 40.6 %all-gather.5.cloned.1.call-done = f32[4096,128]{1,0:T(8,128)} async-done(((f32[512,128]{1,0:T(8,128)}), f32[4096,128]{1,0:T(8,128)}) %all-gather.5.cloned.1.call-update) | async-done | bytes 2097168 | tf_op jit(solution)/shard_map/all_gather | solution.py:80
  59.9 13.5 %convolution_bitcast_fusion.4 = f32[512,128]{0,1:T(8,128)} fusion(f32[4096,128]{1,0:T(8,128)} %all-gather.5.cloned.1.call-done, f32[512,4096]{1,0:T(8,128)} %param.14), kind=kOutput, calls=%fused_computation.12 | convolution fusion | flops 3221225472 | bytes 10747904 | tf_op jit(solution)/shard_map/dot_general | solution.py:86
  73.4 0.0 all-gather.7.cloned.1.call-update
  73.4 0.2 all-gather.9.cloned.1.call-start
  73.7 4.0 %reshape.77 = f32[128,4,4,2,128]{4,3,2,1,0:T(2,128)} reshape(f32[128,4096]{1,0:T(8,128)} %param.15) | data formatting | bytes 4194304 | tf_op jit(solution)/shard_map/reshape | solution.py:67
  77.7 9.8 %dynamic-slice_reduce_fusion = (f32[128,4,4,128]{3,2,1,0:T(4,128)S(1)}, f32[128,4,4,128]{3,2,1,0:T(4,128)}) fusion(f32[128,4,4,2,128]{4,3,2,1,0:T(2,128)} %reshape.77, s32[]{:T(128)S(6)} %select_n.44, s32[]{:T(128)S(6)} %select_n.43), kind=kLoop, calls=%fused_computation.14 | loop fusion | bytes 4194312 | tf_op jit(solution)/shard_map/jit(dynamic_index_in_dim)/dynamic_slice | solution.py:70
  87.5 1.4 reshape.79
  88.9 3.8 %collective-permute-start = (f32[128,2048]{1,0:T(8,128)}, f32[128,2048]{1,0:T(8,128)}, u32[]{:S(2)}, u32[]{:S(2)}) collective-permute-start(f32[128,2048]{1,0:T(8,128)} %reshape.79), channel_id=1, source_target_pairs={{0,1},{1,0},{2,3},{3,2},{4,5},{5,4},{6,7},{7,6},{8,9},{9,8},{10,11... | collective-permute-start | bytes 3145736 | tf_op jit(solution)/shard_map/ppermute | solution.py:71
  92.7 1.7 reshape.78
  94.4 45.2 %collective-permute-done = f32[128,2048]{1,0:T(8,128)} collective-permute-done((f32[128,2048]{1,0:T(8,128)}, f32[128,2048]{1,0:T(8,128)}, u32[]{:S(2)}, u32[]{:S(2)}) %collective-permute-start) | collective-permute-done | bytes 1048608 | tf_op jit(solution)/shard_map/ppermute | solution.py:71
  139.6 8.9 %fusion.42 = f32[512,128]{1,0:T(8,128)S(1)} fusion(f32[512,2048]{0,1:T(8,128)} %all-gather.7.cloned.1.call-done, f32[128,2048]{1,0:T(8,128)} %collective-permute-done), kind=kOutput, calls=%fused_computation.70 | convolution fusion | flops 1610612736 | bytes 5505024 | tf_op jit(solution)/shard_map/dot_general | solution.py:94
  148.4 0.0 copy-start.5
  148.5 3.1 collective-permute-start.1
  151.6 0.0 copy-done.1
  151.6 6.8 %fusion.41 = f32[512,128]{1,0:T(8,128)S(1)} fusion(f32[512,2048]{0,1:T(8,128)S(1)} %copy-done.1, f32[128,2048]{1,0:T(8,128)S(1)} %reshape.78), kind=kOutput, calls=%fused_computation.69 | convolution fusion | flops 1610612736 | bytes 5505024 | tf_op jit(solution)/shard_map/dot_general | solution.py:103
  158.4 1.4 collective-permute-done.1
  159.8 0.5 fusion.18
  160.3 1.2 fusion.2
  161.5 2.1 convolution_bitcast_fusion.1
  163.6 0.6 fusion.8
  164.2 0.8 copy.36
  165.0 0.0 all-gather.9.cloned.1.call-update
  165.0 0.0 copy-start.4
  165.0 0.4 all-gather.11.cloned.1.call-start
  165.5 36.6 %all-gather.9.cloned.1.call-done = f32[4096,128]{1,0:T(8,128)} async-done(((f32[512,128]{1,0:T(8,128)}), f32[4096,128]{1,0:T(8,128)}) %all-gather.9.cloned.1.call-update) | async-done | bytes 2097168 | tf_op jit(solution)/shard_map/all_gather | solution.py:84
  202.0 13.5 %convolution_bitcast_fusion.3 = f32[512,128]{0,1:T(8,128)} fusion(f32[4096,128]{1,0:T(8,128)} %all-gather.9.cloned.1.call-done, f32[512,4096]{1,0:T(8,128)} %param.14), kind=kOutput, calls=%fused_computation.11 | convolution fusion | flops 3221225472 | bytes 10747904 | tf_op jit(solution)/shard_map/dot_general | solution.py:86
  215.6 0.0 all-gather.11.cloned.1.call-update
  215.6 0.0 copy-done.4
  215.6 0.6 multiply_reduce_fusion.3
  216.2 1.4 maximum_bitcast_fusion
  217.6 16.2 %all_gather.20 = f32[64,128]{1,0:T(8,128)S(1)} all-gather(f32[8,128]{1,0:T(8,128)S(1)} %scatter.4), channel_id=1, replica_groups=mesh['sensor'=8,'tx'=4,'ty'=4,'tz'=2] {'sensor'}, dimensions={0}, use_global_device_ids=true | all-gather | bytes 36864 | tf_op jit(solution)/shard_map/all_gather | solution.py:84
  233.8 18.4 %all_gather.21 = f32[8,2048]{1,0:T(8,128)S(1)} all-gather(f32[8,128]{1,0:T(8,128)S(1)} %bitcast_reduce_fusion.1), channel_id=1, replica_groups=mesh['sensor'=8,'tx'=4,'ty'=4,'tz'=2] {'tx','ty'}, dimensions={1}, use_global_device_ids=true | all-gather | bytes 69632 | tf_op jit(solution)/shard_map/all_gather | solution.py:92
  252.2 4.2 %collective-permute-start.2 = (f32[8,128]{1,0:T(8,128)S(1)}, f32[8,128]{1,0:T(8,128)S(1)}, u32[]{:S(2)}, u32[]{:S(2)}) collective-permute-start(f32[8,128]{1,0:T(8,128)S(1)} %bitcast_reduce_fusion), channel_id=1, source_target_pairs={{0,1},{1,0},{2,3},{3,2},{4,5},{5,4},{6,7},{7,6},{8,9},{9,8},{10,11... | collective-permute-start | bytes 12296 | tf_op jit(solution)/shard_map/ppermute | solution.py:100
  256.4 2.4 collective-permute-done.2
  258.9 0.6 fusion.39
  260.8 12.4 %all-gather.11.cloned.1.call-done = f32[512,2048]{0,1:T(8,128)} async-done(((f32[512,128]{0,1:T(8,128)}), f32[512,2048]{0,1:T(8,128)}) %all-gather.11.cloned.1.call-update) | async-done | bytes 4194320 | tf_op jit(solution)/shard_map/all_gather | solution.py:92
  273.2 8.9 %fusion.44 = f32[512,128]{1,0:T(8,128)S(1)} fusion(f32[512,2048]{0,1:T(8,128)} %all-gather.11.cloned.1.call-done, f32[128,2048]{1,0:T(8,128)} %collective-permute-done), kind=kOutput, calls=%fused_computation.72 | convolution fusion | flops 1610612736 | bytes 5505024 | tf_op jit(solution)/shard_map/dot_general | solution.py:94
  282.1 5.5 %collective-permute-start.3 = (f32[512,128]{1,0:T(8,128)S(1)}, f32[512,128]{1,0:T(8,128)S(1)}, u32[]{:S(2)}, u32[]{:S(2)}) collective-permute-start(f32[512,128]{1,0:T(8,128)S(1)} %fusion.44), channel_id=1, source_target_pairs={{0,1},{1,0},{2,3},{3,2},{4,5},{5,4},{6,7},{7,6},{8,9},{9,8},{10,11... | collective-permute-start | bytes 786440 | tf_op jit(solution)/shard_map/ppermute | solution.py:100
  287.5 6.8 %fusion.43 = f32[512,128]{1,0:T(8,128)S(1)} fusion(f32[512,2048]{0,1:T(8,128)S(1)} %copy-done.2, f32[128,2048]{1,0:T(8,128)S(1)} %reshape.78), kind=kOutput, calls=%fused_computation.71 | convolution fusion | flops 1610612736 | bytes 5505024 | tf_op jit(solution)/shard_map/dot_general | solution.py:103
  294.3 0.6 collective-permute-done.3
  294.9 0.5 fusion.16
  295.4 1.2 fusion.3
  296.6 0.7 multiply_reduce_fusion.1
  297.3 2.0 pad_maximum_fusion
  299.2 0.1 broadcast_in_dim.2
  299.3 29.3 %all_to_all.6 = f32[256,1,3]{2,1,0:T(1,128)S(1)} all-to-all(f32[256,1,3]{2,1,0:T(1,128)S(1)} %broadcast_in_dim.2), channel_id=1, replica_groups=mesh['sensor'=8,'tx'=4,'ty'=4,'tz'=2] {'sensor','tx','ty','tz'}, dimensions={0} | all-to-all | bytes 6144 | tf_op jit(solution)/shard_map/all_to_all | solution.py:27
  328.5 0.3 reduce_sum.119
  328.8 0.7 fusion.40
  333.4 0.6 multiply_subtract_fusion
  (15 shorter events, 0.1 us)
Async XLA Ops:
  7.2 10.2 %copy-start.6 = (s32[16]{0:T(128)S(1)}, s32[16]{0:T(128)}, u32[]{:S(2)}) copy-start(s32[16]{0:T(128)} %param.13) | copy-start | bytes 196
  7.2 8.1 %copy-start.3 = (f32[16,64,128]{2,1,0:T(8,128)S(1)}, f32[16,64,128]{2,1,0:T(8,128)}, u32[]{:S(2)}) copy-start(f32[16,64,128]{2,1,0:T(8,128)} %param.11) | copy-start | bytes 1572868
  7.2 8.1 %copy-start = (f32[16,128,128]{2,1,0:T(8,128)S(1)}, f32[16,128,128]{2,1,0:T(8,128)}, u32[]{:S(2)}) copy-start(f32[16,128,128]{2,1,0:T(8,128)} %param.12) | copy-start | bytes 3145732
  7.2 52.7 %all-gather.5.cloned.1.call-start = ((), (), s32[]{:S(2)}) async-start(), calls=%async_computation.1 | async-start | bytes 2359296 | tf_op jit(solution)/shard_map/all_gather | solution.py:80
  18.8 120.8 %all-gather.7.cloned.1.call-start = ((), (), s32[]{:S(2)}) async-start(), calls=%async_computation.2 | async-start | bytes 4456448 | tf_op jit(solution)/shard_map/all_gather | solution.py:90
  73.4 128.6 %all-gather.9.cloned.1.call-start = ((), (), s32[]{:S(2)}) async-start(), calls=%async_computation.3 | async-start | bytes 2359296 | tf_op jit(solution)/shard_map/all_gather | solution.py:84
  88.9 50.7 %collective-permute-start = (f32[128,2048]{1,0:T(8,128)}, f32[128,2048]{1,0:T(8,128)}, u32[]{:S(2)}, u32[]{:S(2)}) collective-permute-start(f32[128,2048]{1,0:T(8,128)} %reshape.79), channel_id=1, source_target_pairs={{0,1},{1,0},{2,3},{3,2},{4,5},{5,4},{6,7},{7,6},{8,9},{9,8},{10,11... | collective-permute-start | bytes 3145736 | tf_op jit(solution)/shard_map/ppermute | solution.py:71
  139.6 12.0 %copy-start.1 = (f32[512,2048]{0,1:T(8,128)S(1)}, f32[512,2048]{0,1:T(8,128)}, u32[]{:S(2)}) copy-start(f32[512,2048]{0,1:T(8,128)} %all-gather.7.cloned.1.call-done) | copy-start | bytes 12582916
  148.4 13.0 %copy-start.5 = (f32[16,128]{1,0:T(8,128)S(1)}, f32[16,128]{1,0:T(8,128)}, u32[]{:S(2)}) copy-start(f32[16,128]{1,0:T(8,128)} %param.10) | copy-start | bytes 24580
  148.5 11.3 %collective-permute-start.1 = (f32[512,128]{1,0:T(8,128)S(1)}, f32[512,128]{1,0:T(8,128)S(1)}, u32[]{:S(2)}, u32[]{:S(2)}) collective-permute-start(f32[512,128]{1,0:T(8,128)S(1)} %fusion.42), channel_id=1, source_target_pairs={{0,1},{1,0},{2,3},{3,2},{4,5},{5,4},{6,7},{7,6},{8,9},{9,8},{10,11... | collective-permute-start | bytes 786440 | tf_op jit(solution)/shard_map/ppermute | solution.py:98
  165.0 50.6 %copy-start.4 = (f32[16,128]{1,0:T(8,128)S(1)}, f32[16,128]{1,0:T(8,128)}, u32[]{:S(2)}) copy-start(f32[16,128]{1,0:T(8,128)} %param.9) | copy-start | bytes 24580
  165.0 108.2 %all-gather.11.cloned.1.call-start = ((), (), s32[]{:S(2)}) async-start(), calls=%async_computation.4 | async-start | bytes 4456448 | tf_op jit(solution)/shard_map/all_gather | solution.py:92
  252.2 6.6 %collective-permute-start.2 = (f32[8,128]{1,0:T(8,128)S(1)}, f32[8,128]{1,0:T(8,128)S(1)}, u32[]{:S(2)}, u32[]{:S(2)}) collective-permute-start(f32[8,128]{1,0:T(8,128)S(1)} %bitcast_reduce_fusion), channel_id=1, source_target_pairs={{0,1},{1,0},{2,3},{3,2},{4,5},{5,4},{6,7},{7,6},{8,9},{9,8},{10,11... | collective-permute-start | bytes 12296 | tf_op jit(solution)/shard_map/ppermute | solution.py:100
  273.2 14.4 %copy-start.2 = (f32[512,2048]{0,1:T(8,128)S(1)}, f32[512,2048]{0,1:T(8,128)}, u32[]{:S(2)}) copy-start(f32[512,2048]{0,1:T(8,128)} %all-gather.11.cloned.1.call-done) | copy-start | bytes 12582916
  282.1 12.8 %collective-permute-start.3 = (f32[512,128]{1,0:T(8,128)S(1)}, f32[512,128]{1,0:T(8,128)S(1)}, u32[]{:S(2)}, u32[]{:S(2)}) collective-permute-start(f32[512,128]{1,0:T(8,128)S(1)} %fusion.44), channel_id=1, source_target_pairs={{0,1},{1,0},{2,3},{3,2},{4,5},{5,4},{6,7},{7,6},{8,9},{9,8},{10,11... | collective-permute-start | bytes 786440 | tf_op jit(solution)/shard_map/ppermute | solution.py:100
Sparse Core Ops, SparseCore 0:
  18.9 40.9 all-gather.4
  73.6 57.3 all-gather.6
  165.1 36.8 all-gather.8
  215.7 57.4 all-gather.10

commit v10 on v9

--- a/solution.py
+++ b/solution.py
@@ -65,10 +65,12 @@
     n_tx, n_ty, n_tz = lax.axis_size("tx"), lax.axis_size("ty"), lax.axis_size("tz")
     z_now = lax.axis_index("tz")
     by_half = time_kernel.reshape(time_dev, n_tx, n_ty, n_tz, time_dev)
-    own_cols = lax.dynamic_index_in_dim(by_half, z_now, axis=3, keepdims=False)
-    own_cols = own_cols.reshape(time_dev, -1)
-    other_cols = lax.dynamic_index_in_dim(by_half, 1 - z_now, axis=3, keepdims=False)
-    partner_cols = lax.ppermute(other_cols.reshape(time_dev, -1), "tz", Z_SWAP)
+    half0 = by_half[:, :, :, 0, :].reshape(time_dev, -1)
+    half1 = by_half[:, :, :, 1, :].reshape(time_dev, -1)
+    own_cols = jnp.where(z_now == 0, half0, half1)
+    other_cols = jnp.where(z_now == 0, half1, half0)
+    other_cols, readings = lax.optimization_barrier((other_cols, readings))
+    partner_cols = lax.ppermute(other_cols, "tz", Z_SWAP)
 
     def operator_apply(vector, payload=None):
         scaled = vector[:, None, :] * time_weights
@@ -76,8 +78,10 @@
         grid_field = jnp.einsum("bw,bij->wij", onehot, contrib, precision=PRECISE).reshape(
             sensor_dev, time_dev
         )
+        kernel_cols = partner_cols
         if payload is None:
             full_field = lax.all_gather(grid_field, "sensor", axis=0, tiled=True)
+            full_field, kernel_cols = lax.optimization_barrier((full_field, kernel_cols))
         else:
             pad = jnp.zeros((PAY_ROWS, time_dev), jnp.float32)
             pad = pad.at[0, : payload.shape[0]].set(payload)
@@ -92,7 +96,7 @@
             half_rows, pad = lax.all_gather((left_product, pad), ("tx", "ty"), axis=1, tiled=True)
             pad = jnp.sum(pad.reshape(PAY_ROWS, -1, time_dev), axis=1)
         for_partner = jnp.dot(
-            half_rows, partner_cols.T, precision=PRECISE, preferred_element_type=jnp.float32
+            half_rows, kernel_cols.T, precision=PRECISE, preferred_element_type=jnp.float32
         )
         if payload is None:
             from_partner = lax.ppermute(for_partner, "tz", Z_SWAP)

time: 345 us -> 391 us (1.13)
  waiting for transfers between devices: 139 us -> 179 us
  local copies, waits for them, and re-layouts: 21.3 us -> 11.4 us
  other arithmetic: 6.33 us -> 15.2 us
  starting transfers between devices: 17.8 us -> 24.1 us
    all_gather x1, waiting for transfers between devices: 0.01 us -> 54.5 us  [operator_apply(): half_rows = lax.all_gather(left_product, ('tx', 'ty'), axis=1, tiled=True)]
    all_gather x1, waiting for transfers between devices: 40.6 us -> 14.5 us  [operator_apply(): full_field = lax.all_gather(grid_field, 'sensor', axis=0, tiled=True)]
    dynamic_slice x1 -> x0, local copies, waits for them, and re-layouts: 9.76 us -> none  [on_device(): lax.dynamic_index_in_dim(by_half, 1 - z_now, axis=3, keepdims=False)]
    select_n x0 -> x1, other arithmetic: none -> 9.59 us  [on_device(): own_cols = jnp.where(z_now == 0, half0, half1)]
    ppermute x1, waiting for transfers between devices: 45.2 us -> 52.4 us  [on_device(): partner_cols = lax.ppermute(other_cols, 'tz', Z_SWAP)]
    all_gather x1, waiting for transfers between devices: 36.6 us -> 41.6 us  [operator_apply(): lax.all_gather((grid_field, pad), 'sensor', axis=0, tiled=True)]
    ppermute x1, starting transfers between devices: 3.82 us -> 8.27 us  [on_device(): partner_cols = lax.ppermute(other_cols, 'tz', Z_SWAP)]
  transfers between devices with their start and end apart: 8 -> 8, of which waited for: 7 -> 8; matrix products, arithmetic and copies ran while one was open for 10% -> 5% of each run, Pallas kernels for 0% -> 0%
where the time goes in v10:
time: 391 us; the launch traced here: 384 us
  waiting for transfers between devices  179 us (46%)
  matrix products  70.1 us (18%)
  blocking collectives  63.9 us (16%)
  starting transfers between devices  24.1 us (6%)
  between operations  19.6 us (5%)
  other arithmetic  15.2 us (4%)
  local copies, waits for them, and re-layouts  11.4 us (3%)
    all_gather x1, waiting for transfers between devices, operator_apply(): half_rows = lax.all_gather(left_product, ('tx', 'ty'), axis=1, tiled=True)  54.5 us
    ppermute x1, waiting for transfers between devices, on_device(): partner_cols = lax.ppermute(other_cols, 'tz', Z_SWAP)  52.4 us
    all_gather x1, waiting for transfers between devices, operator_apply(): lax.all_gather((grid_field, pad), 'sensor', axis=0, tiled=True)  41.6 us
    all_to_all x1, blocking collectives, all_device_sum(): rows = lax.all_to_all(copies, ALL, 0, 0, tiled=True)  29.3 us
    dot_general x2, matrix products, operator_apply(): jnp.dot(sensor_kernel, full_field, precision=PRECISE, preferred_element_t...  27 us
    all_gather x1, blocking collectives, operator_apply(): lax.all_gather((left_product, pad), ('tx', 'ty'), axis=1, tiled=True)  18.4 us
    dot_general x2, matrix products, operator_apply(): jnp.dot(half_rows, kernel_cols.T, precision=PRECISE, preferred_element_ty...  17.7 us
    all_gather x1, blocking collectives, operator_apply(): lax.all_gather((grid_field, pad), 'sensor', axis=0, tiled=True)  16.2 us
  transfers between devices with their start and end apart: 8, of which 8 were waited for; matrix products, arithmetic and copies ran while one was open for 5% of the time, Pallas kernels for 0%

profile of v10, /device:TPU:1, one launch (start us, length us, event | category | flops | bytes accessed | tf_op | source)
XLA Modules:
  0.0 383.5 jit_solution(7861579927982327589)
XLA Ops:
  7.2 0.0 all-gather.5.cloned.1.call-start
  7.2 4.1 %reshape.72 = f32[128,4,4,2,128]{4,3,2,1,0:T(2,128)} reshape(f32[128,4096]{1,0:T(8,128)} %param.15) | data formatting | bytes 4194304 | tf_op jit(solution)/shard_map/reshape | solution.py:67
  11.3 0.0 copy-start.6
  11.3 9.6 %fusion.6 = (f32[128,4,4,128]{3,2,1,0:T(4,128)}, f32[128,4,4,128]{3,2,1,0:T(4,128)S(1)}) fusion(pred[]{:T(512)S(6)} %eq.8, f32[128,4,4,2,128]{4,3,2,1,0:T(2,128)} %reshape.72), kind=kLoop, calls=%fused_computation.16 | loop fusion | flops 524288 | bytes 4194305 | tf_op jit(solution)/shard_map/jit(_where)/select_n | solution.py:70
  20.9 1.4 select_n.47
  22.3 0.0 copy-done
  22.3 2.0 fusion.1
  24.3 1.0 constant_dynamic-slice_fusion.1
  25.3 0.4 stack.56
  25.7 0.0 copy-done.7
  25.7 0.4 fusion.29
  26.1 0.0 copy-done.3
  26.1 0.8 fusion.4
  26.9 0.0 copy-done.5
  26.9 0.0 copy-done.6
  27.0 2.1 convolution_bitcast_fusion.2
  29.0 0.6 fusion.13
  29.6 0.8 copy.32
  30.4 0.0 all-gather.5.cloned.1.call-update
  30.4 0.0 all-gather.7.cloned.1.call-start
  30.5 8.3 %collective-permute-start = (f32[128,2048]{1,0:T(8,128)S(1)}, f32[128,2048]{1,0:T(8,128)}, u32[]{:S(2)}, u32[]{:S(2)}) collective-permute-start(f32[128,2048]{1,0:T(8,128)S(1)} %copy-done.4), channel_id=1, source_target_pairs={{0,1},{1,0},{2,3},{3,2},{4,5},{5,4},{6,7},{7,6},{8,9},{9,8},{10,11... | collective-permute-start | bytes 3145736 | tf_op jit(solution)/shard_map/ppermute | solution.py:73
  38.8 52.4 %collective-permute-done = f32[128,2048]{1,0:T(8,128)} collective-permute-done((f32[128,2048]{1,0:T(8,128)S(1)}, f32[128,2048]{1,0:T(8,128)}, u32[]{:S(2)}, u32[]{:S(2)}) %collective-permute-start) | collective-permute-done | bytes 1048608 | tf_op jit(solution)/shard_map/ppermute | solution.py:73
  91.1 14.5 %all-gather.5.cloned.1.call-done = f32[4096,128]{1,0:T(8,128)} async-done(((f32[512,128]{1,0:T(8,128)}), f32[4096,128]{1,0:T(8,128)}) %all-gather.5.cloned.1.call-update) | async-done | bytes 2097168 | tf_op jit(solution)/shard_map/all_gather | solution.py:83
  105.6 13.5 %convolution_bitcast_fusion.4 = f32[512,128]{0,1:T(8,128)} fusion(f32[4096,128]{1,0:T(8,128)} %all-gather.5.cloned.1.call-done, f32[512,4096]{1,0:T(8,128)} %param.14), kind=kOutput, calls=%fused_computation.14 | convolution fusion | flops 3221225472 | bytes 10747904 | tf_op jit(solution)/shard_map/dot_general | solution.py:90
  119.1 0.0 all-gather.7.cloned.1.call-update
  119.2 0.0 all-gather.9.cloned.1.call-start
  119.2 1.6 select_n.58
  120.9 54.5 %all-gather.7.cloned.1.call-done = f32[512,2048]{0,1:T(8,128)} async-done(((f32[512,128]{0,1:T(8,128)}), f32[512,2048]{0,1:T(8,128)}) %all-gather.7.cloned.1.call-update) | async-done | bytes 4194320 | tf_op jit(solution)/shard_map/all_gather | solution.py:94
  175.4 8.9 %fusion.44 = f32[512,128]{1,0:T(8,128)S(1)} fusion(f32[512,2048]{0,1:T(8,128)} %all-gather.7.cloned.1.call-done, f32[128,2048]{1,0:T(8,128)} %collective-permute-done), kind=kOutput, calls=%fused_computation.72 | convolution fusion | flops 1610612736 | bytes 5505024 | tf_op jit(solution)/shard_map/dot_general | solution.py:98
  184.3 5.7 %collective-permute-start.1 = (f32[512,128]{1,0:T(8,128)S(1)}, f32[512,128]{1,0:T(8,128)S(1)}, u32[]{:S(2)}, u32[]{:S(2)}) collective-permute-start(f32[512,128]{1,0:T(8,128)S(1)} %fusion.44), channel_id=1, source_target_pairs={{0,1},{1,0},{2,3},{3,2},{4,5},{5,4},{6,7},{7,6},{8,9},{9,8},{10,11... | collective-permute-start | bytes 786440 | tf_op jit(solution)/shard_map/ppermute | solution.py:102
  190.0 0.0 copy-done.2
  190.0 6.8 %fusion.43 = f32[512,128]{1,0:T(8,128)S(1)} fusion(f32[512,2048]{0,1:T(8,128)S(1)} %copy-done.2, f32[128,2048]{1,0:T(8,128)S(1)} %select_n.58), kind=kOutput, calls=%fused_computation.71 | convolution fusion | flops 1610612736 | bytes 5505024 | tf_op jit(solution)/shard_map/dot_general | solution.py:107
  196.8 0.6 collective-permute-done.1
  197.4 0.5 fusion.20
  197.9 1.2 fusion.2
  199.1 2.1 convolution_bitcast_fusion.1
  201.2 0.6 fusion.10
  201.8 0.8 copy.36
  202.5 0.0 all-gather.9.cloned.1.call-update
  202.6 0.3 all-gather.11.cloned.1.call-start
  202.8 41.6 %all-gather.9.cloned.1.call-done = f32[4096,128]{1,0:T(8,128)} async-done(((f32[512,128]{1,0:T(8,128)}), f32[4096,128]{1,0:T(8,128)}) %all-gather.9.cloned.1.call-update) | async-done | bytes 2097168 | tf_op jit(solution)/shard_map/all_gather | solution.py:88
  244.4 13.5 %convolution_bitcast_fusion.3 = f32[512,128]{0,1:T(8,128)} fusion(f32[4096,128]{1,0:T(8,128)} %all-gather.9.cloned.1.call-done, f32[512,4096]{1,0:T(8,128)} %param.14), kind=kOutput, calls=%fused_computation.13 | convolution fusion | flops 3221225472 | bytes 10747904 | tf_op jit(solution)/shard_map/dot_general | solution.py:90
  257.9 0.0 all-gather.11.cloned.1.call-update
  257.9 0.6 multiply_reduce_fusion.3
  258.5 1.4 maximum_bitcast_fusion
  259.9 16.2 %all_gather.20 = f32[64,128]{1,0:T(8,128)S(1)} all-gather(f32[8,128]{1,0:T(8,128)S(1)} %scatter.4), channel_id=1, replica_groups=mesh['sensor'=8,'tx'=4,'ty'=4,'tz'=2] {'sensor'}, dimensions={0}, use_global_device_ids=true | all-gather | bytes 36864 | tf_op jit(solution)/shard_map/all_gather | solution.py:88
  276.1 18.4 %all_gather.21 = f32[8,2048]{1,0:T(8,128)S(1)} all-gather(f32[8,128]{1,0:T(8,128)S(1)} %bitcast_reduce_fusion.1), channel_id=1, replica_groups=mesh['sensor'=8,'tx'=4,'ty'=4,'tz'=2] {'tx','ty'}, dimensions={1}, use_global_device_ids=true | all-gather | bytes 69632 | tf_op jit(solution)/shard_map/all_gather | solution.py:96
  294.6 4.0 %collective-permute-start.2 = (f32[8,128]{1,0:T(8,128)S(1)}, f32[8,128]{1,0:T(8,128)S(1)}, u32[]{:S(2)}, u32[]{:S(2)}) collective-permute-start(f32[8,128]{1,0:T(8,128)S(1)} %bitcast_reduce_fusion), channel_id=1, source_target_pairs={{0,1},{1,0},{2,3},{3,2},{4,5},{5,4},{6,7},{7,6},{8,9},{9,8},{10,11... | collective-permute-start | bytes 12296 | tf_op jit(solution)/shard_map/ppermute | solution.py:104
  298.6 2.4 collective-permute-done.2
  301.0 0.6 fusion.41
  302.9 12.5 %all-gather.11.cloned.1.call-done = f32[512,2048]{0,1:T(8,128)} async-done(((f32[512,128]{0,1:T(8,128)}), f32[512,2048]{0,1:T(8,128)}) %all-gather.11.cloned.1.call-update) | async-done | bytes 4194320 | tf_op jit(solution)/shard_map/all_gather | solution.py:96
  315.5 8.9 %fusion.46 = f32[512,128]{1,0:T(8,128)S(1)} fusion(f32[512,2048]{0,1:T(8,128)} %all-gather.11.cloned.1.call-done, f32[128,2048]{1,0:T(8,128)} %collective-permute-done), kind=kOutput, calls=%fused_computation.74 | convolution fusion | flops 1610612736 | bytes 5505024 | tf_op jit(solution)/shard_map/dot_general | solution.py:98
  324.4 5.7 %collective-permute-start.3 = (f32[512,128]{1,0:T(8,128)S(1)}, f32[512,128]{1,0:T(8,128)S(1)}, u32[]{:S(2)}, u32[]{:S(2)}) collective-permute-start(f32[512,128]{1,0:T(8,128)S(1)} %fusion.46), channel_id=1, source_target_pairs={{0,1},{1,0},{2,3},{3,2},{4,5},{5,4},{6,7},{7,6},{8,9},{9,8},{10,11... | collective-permute-start | bytes 786440 | tf_op jit(solution)/shard_map/ppermute | solution.py:104
  330.1 6.8 %fusion.45 = f32[512,128]{1,0:T(8,128)S(1)} fusion(f32[512,2048]{0,1:T(8,128)S(1)} %copy-done.1, f32[128,2048]{1,0:T(8,128)S(1)} %select_n.58), kind=kOutput, calls=%fused_computation.73 | convolution fusion | flops 1610612736 | bytes 5505024 | tf_op jit(solution)/shard_map/dot_general | solution.py:107
  336.9 0.6 collective-permute-done.3
  337.5 0.5 fusion.18
  337.9 1.2 fusion.3
  339.1 0.7 multiply_reduce_fusion.1
  339.8 2.0 pad_maximum_fusion
  341.8 0.1 broadcast_in_dim.2
  341.9 29.3 %all_to_all.6 = f32[256,1,3]{2,1,0:T(1,128)S(1)} all-to-all(f32[256,1,3]{2,1,0:T(1,128)S(1)} %broadcast_in_dim.2), channel_id=1, replica_groups=mesh['sensor'=8,'tx'=4,'ty'=4,'tz'=2] {'sensor','tx','ty','tz'}, dimensions={0} | all-to-all | bytes 6144 | tf_op jit(solution)/shard_map/all_to_all | solution.py:27
  371.1 0.3 reduce_sum.119
  371.4 0.7 fusion.42
  375.9 0.6 multiply_subtract_fusion
  (17 shorter events, 0.1 us)
Async XLA Ops:
  7.2 98.5 %all-gather.5.cloned.1.call-start = ((), (), s32[]{:S(2)}) async-start(), calls=%async_computation.1 | async-start | bytes 2359296 | tf_op jit(solution)/shard_map/all_gather | solution.py:83
  11.3 11.0 %copy-start = (f32[16,128,128]{2,1,0:T(8,128)S(1)}, f32[16,128,128]{2,1,0:T(8,128)}, u32[]{:S(2)}) copy-start(f32[16,128,128]{2,1,0:T(8,128)} %param.12) | copy-start | bytes 3145732
  11.3 14.4 %copy-start.7 = (s32[16]{0:T(128)S(1)}, s32[16]{0:T(128)}, u32[]{:S(2)}) copy-start(s32[16]{0:T(128)} %param.13) | copy-start | bytes 196
  11.3 14.9 %copy-start.3 = (f32[16,64,128]{2,1,0:T(8,128)S(1)}, f32[16,64,128]{2,1,0:T(8,128)}, u32[]{:S(2)}) copy-start(f32[16,64,128]{2,1,0:T(8,128)} %param.11) | copy-start | bytes 1572868
  11.3 15.7 %copy-start.5 = (f32[16,128]{1,0:T(8,128)S(1)}, f32[16,128]{1,0:T(8,128)}, u32[]{:S(2)}) copy-start(f32[16,128]{1,0:T(8,128)} %param.9) | copy-start | bytes 24580
  11.3 15.7 %copy-start.6 = (f32[16,128]{1,0:T(8,128)S(1)}, f32[16,128]{1,0:T(8,128)}, u32[]{:S(2)}) copy-start(f32[16,128]{1,0:T(8,128)} %param.10) | copy-start | bytes 24580
  22.3 8.2 %copy-start.4 = (f32[128,2048]{1,0:T(8,128)S(1)}, f32[128,2048]{1,0:T(8,128)}, u32[]{:S(2)}) copy-start(f32[128,2048]{1,0:T(8,128)} %select_n.47) | copy-start | bytes 3145732
  30.4 145.0 %all-gather.7.cloned.1.call-start = ((), (), s32[]{:S(2)}) async-start(), calls=%async_computation.2 | async-start | bytes 4456448 | tf_op jit(solution)/shard_map/all_gather | solution.py:94
  30.5 60.6 %collective-permute-start = (f32[128,2048]{1,0:T(8,128)S(1)}, f32[128,2048]{1,0:T(8,128)}, u32[]{:S(2)}, u32[]{:S(2)}) collective-permute-start(f32[128,2048]{1,0:T(8,128)S(1)} %copy-done.4), channel_id=1, source_target_pairs={{0,1},{1,0},{2,3},{3,2},{4,5},{5,4},{6,7},{7,6},{8,9},{9,8},{10,11... | collective-permute-start | bytes 3145736 | tf_op jit(solution)/shard_map/ppermute | solution.py:73
  119.2 125.2 %all-gather.9.cloned.1.call-start = ((), (), s32[]{:S(2)}) async-start(), calls=%async_computation.3 | async-start | bytes 2359296 | tf_op jit(solution)/shard_map/all_gather | solution.py:88
  175.4 14.6 %copy-start.2 = (f32[512,2048]{0,1:T(8,128)S(1)}, f32[512,2048]{0,1:T(8,128)}, u32[]{:S(2)}) copy-start(f32[512,2048]{0,1:T(8,128)} %all-gather.7.cloned.1.call-done) | copy-start | bytes 12582916
  184.3 13.1 %collective-permute-start.1 = (f32[512,128]{1,0:T(8,128)S(1)}, f32[512,128]{1,0:T(8,128)S(1)}, u32[]{:S(2)}, u32[]{:S(2)}) collective-permute-start(f32[512,128]{1,0:T(8,128)S(1)} %fusion.44), channel_id=1, source_target_pairs={{0,1},{1,0},{2,3},{3,2},{4,5},{5,4},{6,7},{7,6},{8,9},{9,8},{10,11... | collective-permute-start | bytes 786440 | tf_op jit(solution)/shard_map/ppermute | solution.py:102
  202.6 112.9 %all-gather.11.cloned.1.call-start = ((), (), s32[]{:S(2)}) async-start(), calls=%async_computation.4 | async-start | bytes 4456448 | tf_op jit(solution)/shard_map/all_gather | solution.py:96
  294.6 6.5 %collective-permute-start.2 = (f32[8,128]{1,0:T(8,128)S(1)}, f32[8,128]{1,0:T(8,128)S(1)}, u32[]{:S(2)}, u32[]{:S(2)}) collective-permute-start(f32[8,128]{1,0:T(8,128)S(1)} %bitcast_reduce_fusion), channel_id=1, source_target_pairs={{0,1},{1,0},{2,3},{3,2},{4,5},{5,4},{6,7},{7,6},{8,9},{9,8},{10,11... | collective-permute-start | bytes 12296 | tf_op jit(solution)/shard_map/ppermute | solution.py:104
  315.5 14.6 %copy-start.1 = (f32[512,2048]{0,1:T(8,128)S(1)}, f32[512,2048]{0,1:T(8,128)}, u32[]{:S(2)}) copy-start(f32[512,2048]{0,1:T(8,128)} %all-gather.11.cloned.1.call-done) | copy-start | bytes 12582916
  324.4 13.1 %collective-permute-start.3 = (f32[512,128]{1,0:T(8,128)S(1)}, f32[512,128]{1,0:T(8,128)S(1)}, u32[]{:S(2)}, u32[]{:S(2)}) collective-permute-start(f32[512,128]{1,0:T(8,128)S(1)} %fusion.46), channel_id=1, source_target_pairs={{0,1},{1,0},{2,3},{3,2},{4,5},{5,4},{6,7},{7,6},{8,9},{9,8},{10,11... | collective-permute-start | bytes 786440 | tf_op jit(solution)/shard_map/ppermute | solution.py:104
Sparse Core Ops, SparseCore 0:
  30.6 75.0 all-gather.4
  119.3 56.0 all-gather.6
  202.7 41.6 all-gather.8
  258.0 57.3 all-gather.10

commit v11 on v10

--- a/solution.py
+++ b/solution.py
@@ -69,7 +69,6 @@
     half1 = by_half[:, :, :, 1, :].reshape(time_dev, -1)
     own_cols = jnp.where(z_now == 0, half0, half1)
     other_cols = jnp.where(z_now == 0, half1, half0)
-    other_cols, readings = lax.optimization_barrier((other_cols, readings))
     partner_cols = lax.ppermute(other_cols, "tz", Z_SWAP)
 
     def operator_apply(vector, payload=None):
@@ -78,10 +77,8 @@
         grid_field = jnp.einsum("bw,bij->wij", onehot, contrib, precision=PRECISE).reshape(
             sensor_dev, time_dev
         )
-        kernel_cols = partner_cols
         if payload is None:
             full_field = lax.all_gather(grid_field, "sensor", axis=0, tiled=True)
-            full_field, kernel_cols = lax.optimization_barrier((full_field, kernel_cols))
         else:
             pad = jnp.zeros((PAY_ROWS, time_dev), jnp.float32)
             pad = pad.at[0, : payload.shape[0]].set(payload)
@@ -96,7 +93,7 @@
             half_rows, pad = lax.all_gather((left_product, pad), ("tx", "ty"), axis=1, tiled=True)
             pad = jnp.sum(pad.reshape(PAY_ROWS, -1, time_dev), axis=1)
         for_partner = jnp.dot(
-            half_rows, kernel_cols.T, precision=PRECISE, preferred_element_type=jnp.float32
+            half_rows, partner_cols.T, precision=PRECISE, preferred_element_type=jnp.float32
         )
         if payload is None:
             from_partner = lax.ppermute(for_partner, "tz", Z_SWAP)

time: 391 us -> 345 us (0.88)
  waiting for transfers between devices: 179 us -> 139 us
  starting transfers between devices: 24.1 us -> 17.8 us
    all_gather x1, waiting for transfers between devices: 54.5 us -> 0.01 us  [operator_apply(): half_rows = lax.all_gather(left_product, ('tx', 'ty'), axis=1, tiled=True)]
    all_gather x1, waiting for transfers between devices: 14.5 us -> 40.6 us  [operator_apply(): full_field = lax.all_gather(grid_field, 'sensor', axis=0, tiled=True)]
    ppermute x1, waiting for transfers between devices: 52.4 us -> 45.2 us  [on_device(): partner_cols = lax.ppermute(other_cols, 'tz', Z_SWAP)]
    all_gather x1, waiting for transfers between devices: 41.6 us -> 36.8 us  [operator_apply(): lax.all_gather((grid_field, pad), 'sensor', axis=0, tiled=True)]
    ppermute x1, starting transfers between devices: 8.27 us -> 3.82 us  [on_device(): partner_cols = lax.ppermute(other_cols, 'tz', Z_SWAP)]
  transfers between devices with their start and end apart: 8 -> 8, of which waited for: 8 -> 7; matrix products, arithmetic and copies ran while one was open for 5% -> 10% of each run, Pallas kernels for 0% -> 0%
where the time goes in v11:
time: 345 us; the launch traced here: 341 us
  waiting for transfers between devices  139 us (40%)
  matrix products  72.7 us (21%)
  blocking collectives  63.9 us (19%)
  between operations  19.4 us (6%)
  starting transfers between devices  17.8 us (5%)
  other arithmetic  16.2 us (5%)
  local copies, waits for them, and re-layouts  11.6 us (3%)
    ppermute x1, waiting for transfers between devices, on_device(): partner_cols = lax.ppermute(other_cols, 'tz', Z_SWAP)  45.2 us
    all_gather x1, waiting for transfers between devices, operator_apply(): full_field = lax.all_gather(grid_field, 'sensor', axis=0, tiled=True)  40.6 us
    all_gather x1, waiting for transfers between devices, operator_apply(): lax.all_gather((grid_field, pad), 'sensor', axis=0, tiled=True)  36.8 us
    all_to_all x1, blocking collectives, all_device_sum(): rows = lax.all_to_all(copies, ALL, 0, 0, tiled=True)  29.3 us
    dot_general x2, matrix products, operator_apply(): jnp.dot(sensor_kernel, full_field, precision=PRECISE, preferred_element_t...  27 us
    all_gather x1, blocking collectives, operator_apply(): lax.all_gather((left_product, pad), ('tx', 'ty'), axis=1, tiled=True)  18.4 us
    dot_general x2, matrix products, operator_apply(): jnp.dot(half_rows, partner_cols.T, precision=PRECISE, preferred_element_t...  17.7 us
    all_gather x1, blocking collectives, operator_apply(): lax.all_gather((grid_field, pad), 'sensor', axis=0, tiled=True)  16.2 us
  transfers between devices with their start and end apart: 8, of which 7 were waited for; matrix products, arithmetic and copies ran while one was open for 10% of the time, Pallas kernels for 0%

profile of v11, /device:TPU:1, one launch (start us, length us, event | category | flops | bytes accessed | tf_op | source)
XLA Modules:
  0.0 340.8 jit_solution(13116118506280312515)
XLA Ops:
  7.2 0.0 copy-start.6
  7.2 0.0 copy-start.3
  7.2 0.0 copy-start
  7.2 0.0 all-gather.5.cloned.1.call-start
  7.3 1.1 constant_dynamic-slice_fusion.1
  8.4 0.4 stack.56
  8.8 1.1 fusion.29
  9.9 2.1 fusion.4
  12.0 2.6 fusion.1
  14.5 0.7 fusion.40
  15.3 0.0 copy-done.3
  15.3 0.0 copy-done
  15.3 2.1 convolution_bitcast_fusion.2
  17.4 0.6 fusion.13
  18.0 0.8 copy.32
  18.8 0.0 all-gather.5.cloned.1.call-update
  18.8 0.5 all-gather.7.cloned.1.call-start
  19.3 40.6 %all-gather.5.cloned.1.call-done = f32[4096,128]{1,0:T(8,128)} async-done(((f32[512,128]{1,0:T(8,128)}), f32[4096,128]{1,0:T(8,128)}) %all-gather.5.cloned.1.call-update) | async-done | bytes 2097168 | tf_op jit(solution)/shard_map/all_gather | solution.py:81
  59.9 13.5 %convolution_bitcast_fusion.4 = f32[512,128]{0,1:T(8,128)} fusion(f32[4096,128]{1,0:T(8,128)} %all-gather.5.cloned.1.call-done, f32[512,4096]{1,0:T(8,128)} %param.14), kind=kOutput, calls=%fused_computation.14 | convolution fusion | flops 3221225472 | bytes 10747904 | tf_op jit(solution)/shard_map/dot_general | solution.py:87
  73.4 0.0 all-gather.7.cloned.1.call-update
  73.4 0.2 all-gather.9.cloned.1.call-start
  73.7 4.0 %reshape.73 = f32[128,4,4,2,128]{4,3,2,1,0:T(2,128)} reshape(f32[128,4096]{1,0:T(8,128)} %param.15) | data formatting | bytes 4194304 | tf_op jit(solution)/shard_map/reshape | solution.py:67
  77.7 9.9 %fusion.6 = (f32[128,4,4,128]{3,2,1,0:T(4,128)S(1)}, f32[128,4,4,128]{3,2,1,0:T(4,128)}) fusion(pred[]{:T(512)S(6)} %eq.20, f32[128,4,4,2,128]{4,3,2,1,0:T(2,128)} %reshape.73), kind=kLoop, calls=%fused_computation.16 | loop fusion | flops 524288 | bytes 4194305 | tf_op jit(solution)/shard_map/jit(_where)/select_n | solution.py:71
  87.6 1.4 select_n.58
  89.0 3.8 %collective-permute-start = (f32[128,2048]{1,0:T(8,128)}, f32[128,2048]{1,0:T(8,128)}, u32[]{:S(2)}, u32[]{:S(2)}) collective-permute-start(f32[128,2048]{1,0:T(8,128)} %select_n.58), channel_id=1, source_target_pairs={{0,1},{1,0},{2,3},{3,2},{4,5},{5,4},{6,7},{7,6},{8,9},{9,8},{10,11... | collective-permute-start | bytes 3145736 | tf_op jit(solution)/shard_map/ppermute | solution.py:72
  92.8 1.7 select_n.56
  94.5 45.2 %collective-permute-done = f32[128,2048]{1,0:T(8,128)} collective-permute-done((f32[128,2048]{1,0:T(8,128)}, f32[128,2048]{1,0:T(8,128)}, u32[]{:S(2)}, u32[]{:S(2)}) %collective-permute-start) | collective-permute-done | bytes 1048608 | tf_op jit(solution)/shard_map/ppermute | solution.py:72
  139.7 8.9 %fusion.44 = f32[512,128]{1,0:T(8,128)S(1)} fusion(f32[512,2048]{0,1:T(8,128)} %all-gather.7.cloned.1.call-done, f32[128,2048]{1,0:T(8,128)} %collective-permute-done), kind=kOutput, calls=%fused_computation.72 | convolution fusion | flops 1610612736 | bytes 5505024 | tf_op jit(solution)/shard_map/dot_general | solution.py:95
  148.6 0.0 copy-start.5
  148.6 3.1 collective-permute-start.1
  151.7 6.8 %fusion.43 = f32[512,128]{1,0:T(8,128)S(1)} fusion(f32[512,2048]{0,1:T(8,128)S(1)} %copy-done.2, f32[128,2048]{1,0:T(8,128)S(1)} %select_n.56), kind=kOutput, calls=%fused_computation.71 | convolution fusion | flops 1610612736 | bytes 5505024 | tf_op jit(solution)/shard_map/dot_general | solution.py:104
  158.5 1.2 collective-permute-done.1
  159.7 0.5 fusion.20
  160.2 1.2 fusion.2
  161.4 2.1 convolution_bitcast_fusion.1
  163.5 0.6 fusion.10
  164.1 0.8 copy.36
  164.9 0.0 all-gather.9.cloned.1.call-update
  164.9 0.0 copy-start.4
  164.9 0.4 all-gather.11.cloned.1.call-start
  165.3 36.8 %all-gather.9.cloned.1.call-done = f32[4096,128]{1,0:T(8,128)} async-done(((f32[512,128]{1,0:T(8,128)}), f32[4096,128]{1,0:T(8,128)}) %all-gather.9.cloned.1.call-update) | async-done | bytes 2097168 | tf_op jit(solution)/shard_map/all_gather | solution.py:85
  202.2 13.5 %convolution_bitcast_fusion.3 = f32[512,128]{0,1:T(8,128)} fusion(f32[4096,128]{1,0:T(8,128)} %all-gather.9.cloned.1.call-done, f32[512,4096]{1,0:T(8,128)} %param.14), kind=kOutput, calls=%fused_computation.13 | convolution fusion | flops 3221225472 | bytes 10747904 | tf_op jit(solution)/shard_map/dot_general | solution.py:87
  215.7 0.0 all-gather.11.cloned.1.call-update
  215.7 0.6 multiply_reduce_fusion.3
  216.3 1.4 maximum_bitcast_fusion
  217.7 16.2 %all_gather.20 = f32[64,128]{1,0:T(8,128)S(1)} all-gather(f32[8,128]{1,0:T(8,128)S(1)} %scatter.4), channel_id=1, replica_groups=mesh['sensor'=8,'tx'=4,'ty'=4,'tz'=2] {'sensor'}, dimensions={0}, use_global_device_ids=true | all-gather | bytes 36864 | tf_op jit(solution)/shard_map/all_gather | solution.py:85
  233.9 18.4 %all_gather.21 = f32[8,2048]{1,0:T(8,128)S(1)} all-gather(f32[8,128]{1,0:T(8,128)S(1)} %bitcast_reduce_fusion.1), channel_id=1, replica_groups=mesh['sensor'=8,'tx'=4,'ty'=4,'tz'=2] {'tx','ty'}, dimensions={1}, use_global_device_ids=true | all-gather | bytes 69632 | tf_op jit(solution)/shard_map/all_gather | solution.py:93
  252.4 4.2 %collective-permute-start.2 = (f32[8,128]{1,0:T(8,128)S(1)}, f32[8,128]{1,0:T(8,128)S(1)}, u32[]{:S(2)}, u32[]{:S(2)}) collective-permute-start(f32[8,128]{1,0:T(8,128)S(1)} %bitcast_reduce_fusion), channel_id=1, source_target_pairs={{0,1},{1,0},{2,3},{3,2},{4,5},{5,4},{6,7},{7,6},{8,9},{9,8},{10,11... | collective-permute-start | bytes 12296 | tf_op jit(solution)/shard_map/ppermute | solution.py:101
  256.6 2.4 collective-permute-done.2
  259.0 0.6 fusion.41
  260.9 12.4 %all-gather.11.cloned.1.call-done = f32[512,2048]{0,1:T(8,128)} async-done(((f32[512,128]{0,1:T(8,128)}), f32[512,2048]{0,1:T(8,128)}) %all-gather.11.cloned.1.call-update) | async-done | bytes 4194320 | tf_op jit(solution)/shard_map/all_gather | solution.py:93
  273.3 8.9 %fusion.46 = f32[512,128]{1,0:T(8,128)S(1)} fusion(f32[512,2048]{0,1:T(8,128)} %all-gather.11.cloned.1.call-done, f32[128,2048]{1,0:T(8,128)} %collective-permute-done), kind=kOutput, calls=%fused_computation.74 | convolution fusion | flops 1610612736 | bytes 5505024 | tf_op jit(solution)/shard_map/dot_general | solution.py:95
  282.2 5.5 %collective-permute-start.3 = (f32[512,128]{1,0:T(8,128)S(1)}, f32[512,128]{1,0:T(8,128)S(1)}, u32[]{:S(2)}, u32[]{:S(2)}) collective-permute-start(f32[512,128]{1,0:T(8,128)S(1)} %fusion.46), channel_id=1, source_target_pairs={{0,1},{1,0},{2,3},{3,2},{4,5},{5,4},{6,7},{7,6},{8,9},{9,8},{10,11... | collective-permute-start | bytes 786440 | tf_op jit(solution)/shard_map/ppermute | solution.py:101
  287.6 6.8 %fusion.45 = f32[512,128]{1,0:T(8,128)S(1)} fusion(f32[512,2048]{0,1:T(8,128)S(1)} %copy-done.1, f32[128,2048]{1,0:T(8,128)S(1)} %select_n.56), kind=kOutput, calls=%fused_computation.73 | convolution fusion | flops 1610612736 | bytes 5505024 | tf_op jit(solution)/shard_map/dot_general | solution.py:104
  294.4 0.6 collective-permute-done.3
  295.0 0.5 fusion.18
  295.5 1.2 fusion.3
  296.7 0.7 multiply_reduce_fusion.1
  297.4 2.0 pad_maximum_fusion
  299.3 0.1 broadcast_in_dim.2
  299.4 29.3 %all_to_all.6 = f32[256,1,3]{2,1,0:T(1,128)S(1)} all-to-all(f32[256,1,3]{2,1,0:T(1,128)S(1)} %broadcast_in_dim.2), channel_id=1, replica_groups=mesh['sensor'=8,'tx'=4,'ty'=4,'tz'=2] {'sensor','tx','ty','tz'}, dimensions={0} | all-to-all | bytes 6144 | tf_op jit(solution)/shard_map/all_to_all | solution.py:27
  328.6 0.3 reduce_sum.119
  328.9 0.7 fusion.42
  333.5 0.6 multiply_subtract_fusion
  (15 shorter events, 0.1 us)
Async XLA Ops:
  7.2 10.2 %copy-start.6 = (s32[16]{0:T(128)S(1)}, s32[16]{0:T(128)}, u32[]{:S(2)}) copy-start(s32[16]{0:T(128)} %param.13) | copy-start | bytes 196
  7.2 8.1 %copy-start.3 = (f32[16,64,128]{2,1,0:T(8,128)S(1)}, f32[16,64,128]{2,1,0:T(8,128)}, u32[]{:S(2)}) copy-start(f32[16,64,128]{2,1,0:T(8,128)} %param.11) | copy-start | bytes 1572868
  7.2 8.1 %copy-start = (f32[16,128,128]{2,1,0:T(8,128)S(1)}, f32[16,128,128]{2,1,0:T(8,128)}, u32[]{:S(2)}) copy-start(f32[16,128,128]{2,1,0:T(8,128)} %param.12) | copy-start | bytes 3145732
  7.2 52.7 %all-gather.5.cloned.1.call-start = ((), (), s32[]{:S(2)}) async-start(), calls=%async_computation.1 | async-start | bytes 2359296 | tf_op jit(solution)/shard_map/all_gather | solution.py:81
  18.8 120.9 %all-gather.7.cloned.1.call-start = ((), (), s32[]{:S(2)}) async-start(), calls=%async_computation.2 | async-start | bytes 4456448 | tf_op jit(solution)/shard_map/all_gather | solution.py:91
  73.4 128.7 %all-gather.9.cloned.1.call-start = ((), (), s32[]{:S(2)}) async-start(), calls=%async_computation.3 | async-start | bytes 2359296 | tf_op jit(solution)/shard_map/all_gather | solution.py:85
  89.0 50.7 %collective-permute-start = (f32[128,2048]{1,0:T(8,128)}, f32[128,2048]{1,0:T(8,128)}, u32[]{:S(2)}, u32[]{:S(2)}) collective-permute-start(f32[128,2048]{1,0:T(8,128)} %select_n.58), channel_id=1, source_target_pairs={{0,1},{1,0},{2,3},{3,2},{4,5},{5,4},{6,7},{7,6},{8,9},{9,8},{10,11... | collective-permute-start | bytes 3145736 | tf_op jit(solution)/shard_map/ppermute | solution.py:72
  139.7 12.0 %copy-start.2 = (f32[512,2048]{0,1:T(8,128)S(1)}, f32[512,2048]{0,1:T(8,128)}, u32[]{:S(2)}) copy-start(f32[512,2048]{0,1:T(8,128)} %all-gather.7.cloned.1.call-done) | copy-start | bytes 12582916
  148.6 12.8 %copy-start.5 = (f32[16,128]{1,0:T(8,128)S(1)}, f32[16,128]{1,0:T(8,128)}, u32[]{:S(2)}) copy-start(f32[16,128]{1,0:T(8,128)} %param.10) | copy-start | bytes 24580
  148.6 11.1 %collective-permute-start.1 = (f32[512,128]{1,0:T(8,128)S(1)}, f32[512,128]{1,0:T(8,128)S(1)}, u32[]{:S(2)}, u32[]{:S(2)}) collective-permute-start(f32[512,128]{1,0:T(8,128)S(1)} %fusion.44), channel_id=1, source_target_pairs={{0,1},{1,0},{2,3},{3,2},{4,5},{5,4},{6,7},{7,6},{8,9},{9,8},{10,11... | collective-permute-start | bytes 786440 | tf_op jit(solution)/shard_map/ppermute | solution.py:99
  164.9 50.8 %copy-start.4 = (f32[16,128]{1,0:T(8,128)S(1)}, f32[16,128]{1,0:T(8,128)}, u32[]{:S(2)}) copy-start(f32[16,128]{1,0:T(8,128)} %param.9) | copy-start | bytes 24580
  164.9 108.4 %all-gather.11.cloned.1.call-start = ((), (), s32[]{:S(2)}) async-start(), calls=%async_computation.4 | async-start | bytes 4456448 | tf_op jit(solution)/shard_map/all_gather | solution.py:93
  252.4 6.6 %collective-permute-start.2 = (f32[8,128]{1,0:T(8,128)S(1)}, f32[8,128]{1,0:T(8,128)S(1)}, u32[]{:S(2)}, u32[]{:S(2)}) collective-permute-start(f32[8,128]{1,0:T(8,128)S(1)} %bitcast_reduce_fusion), channel_id=1, source_target_pairs={{0,1},{1,0},{2,3},{3,2},{4,5},{5,4},{6,7},{7,6},{8,9},{9,8},{10,11... | collective-permute-start | bytes 12296 | tf_op jit(solution)/shard_map/ppermute | solution.py:101
  273.3 14.4 %copy-start.1 = (f32[512,2048]{0,1:T(8,128)S(1)}, f32[512,2048]{0,1:T(8,128)}, u32[]{:S(2)}) copy-start(f32[512,2048]{0,1:T(8,128)} %all-gather.11.cloned.1.call-done) | copy-start | bytes 12582916
  282.2 12.8 %collective-permute-start.3 = (f32[512,128]{1,0:T(8,128)S(1)}, f32[512,128]{1,0:T(8,128)S(1)}, u32[]{:S(2)}, u32[]{:S(2)}) collective-permute-start(f32[512,128]{1,0:T(8,128)S(1)} %fusion.46), channel_id=1, source_target_pairs={{0,1},{1,0},{2,3},{3,2},{4,5},{5,4},{6,7},{7,6},{8,9},{9,8},{10,11... | collective-permute-start | bytes 786440 | tf_op jit(solution)/shard_map/ppermute | solution.py:101
Sparse Core Ops, SparseCore 0:
  18.9 40.9 all-gather.4
  73.6 57.3 all-gather.6
  165.0 37.1 all-gather.8
  215.8 57.4 all-gather.10
